TPU v7x, 512 devices: a whole 4x8x8 slice. The times are simulated.
512 devices in a mesh: req: 64 (over z, x, core), tp: 8 (over y).
Axes of the slice: x: 4, y: 8, z: 8, core: 2. Of those that a mesh axis runs over, the one named last changes fastest.
Arguments:
- queries: bfloat16 [1024, 2048], P('req', 'tp'), may hold values from -27 to 27
- fresh_cache: bfloat16 [1024, 2, 2048], P('req', None, 'tp'), may hold values from -4 to 4
- tail_cache: bfloat16 [1024, 32, 2, 2048], P('req', None, None, 'tp'), may hold values from -4 to 4
- tail_len: int32 [1024], P('req'), may hold values from 1 to 32, as said below
- pool_cache: bfloat16 [2048, 64, 2, 2048], P('req', None, None, 'tp'), may hold values from -4 to 4
- page_group: int32 [2048], P('req'), may hold values from 0 to 63, as said below
- page_start: int32 [2048], P('req'), may hold values from 0 to 16320, as said below
- prompt_len: int32 [64], replicated, may hold values from 1 to 16384, as said below
- residual: bfloat16 [1024, 2048], P('req'), may hold values from -80 to 80
- out_weight: bfloat16 [2048, 2048], P('tp'), may hold values from -0.125 to 0.125
- out_bias: bfloat16 [2048], replicated, may hold values from -0.796875 to 0.796875
- norm_gain: bfloat16 [2048], P('tp'), may hold values from 0.5 to 1.5
- norm_shift: bfloat16 [2048], P('tp'), may hold values from -0.796875 to 0.796875
Outputs:
- attention_out: bfloat16 [1024, 2048], P('req', 'tp')
- normed: bfloat16 [1024, 2048], P('req', 'tp')
Inputs may be any that keep to these rules, and one draw needn't show every extreme that they name: page_group[p] is the group whose prompt page p holds; every page holds some group's prompt; every group holds at least one page and at most 256 pages, and some group holds exactly 256; the pages of a group of n pages lie on min(n, 64) different indices of req, none holding more than ceil(n / 64) of them. The pages of a group of n pages have page_start 0, 64, ..., (n - 1) * 64, each once. `prompt_len`: a group of n pages has a prompt of (n - 1) * 64 + 1 to n * 64 positions. `tail_len`: some request has exactly 32 tail positions.
All inputs are finite; a program needn't handle non-finite values.
Results may differ from a plain program's by a relative error of at most 0.02.
Values may be sent and summed in bfloat16 or wider, within the bound.
No kernel may reach another device: no remote copies, remote signals or barrier semaphores. Data moves between devices by JAX's collectives and lax.ppermute only.
A program may use at most 64 MiB of HBM per device.

v0:
```python
import math

import jax
import jax.numpy as jnp
from jax import lax
from jax.sharding import PartitionSpec as P

HEADS = 16
HEAD = 128
PAGE = 64


masked_score = -1e30
norm_epsilon = 1e-05


def split_halves(values):
    upper_part = lax.optimization_barrier(values.astype(jnp.bfloat16))
    lower_part = (values - upper_part.astype(jnp.float32)).astype(jnp.bfloat16)
    return (upper_part, lower_part)


def local(
    queries,
    fresh_cache,
    tail_cache,
    tail_len,
    pool_cache,
    page_group,
    page_start,
    prompt_len,
    residual,
    out_weight,
    out_bias,
    norm_gain,
    norm_shift,
):
    f32 = jnp.float32
    highest = lax.Precision.HIGHEST
    row_count, feat_width = queries.shape
    heads_here = feat_width // HEAD
    inv_root = 1.0 / math.sqrt(HEAD)
    head_ids = lax.axis_index("tp") * heads_here + jnp.arange(heads_here)
    slopes = jnp.exp2(-8.0 * (head_ids.astype(f32) + 1.0) / HEADS)
    group_count = prompt_len.shape[0]
    page_count = pool_cache.shape[0]
    tail_slots = tail_cache.shape[1]
    req_index = lax.axis_index("req")
    everyone = lax.all_gather(queries, "req", axis=0, tiled=True)
    by_group = everyone.reshape(group_count, row_count, heads_here, HEAD)
    safe_group = jnp.clip(page_group, 0, group_count - 1)
    page_queries = by_group[safe_group]
    page_keys = pool_cache[:, :, 0].reshape(page_count, PAGE, heads_here, HEAD)
    page_values = pool_cache[:, :, 1].reshape(page_count, PAGE, heads_here, HEAD)
    prompt_here = prompt_len[safe_group]
    positions = page_start[:, None] + jnp.arange(PAGE)[None, :]
    usable = (positions < prompt_here[:, None]) & (page_group[:, None] >= 0)
    offsets = (positions - prompt_here[:, None]).astype(f32)
    scores = (
        jnp.einsum("pqhd,pshd->pqhs", page_queries, page_keys, preferred_element_type=f32)
        * inv_root
    )
    scores = scores + slopes[None, None, :, None] * offsets[:, None, None, :]
    scores = jnp.where(usable[:, None, None, :], scores, masked_score)
    member = page_group[:, None] == jnp.arange(group_count)[None, :]
    page_top = scores.max(-1)
    group_top = jnp.where(member[:, :, None, None], page_top[:, None], masked_score).max(0)
    group_top = group_top.reshape(group_count * row_count, heads_here)
    home_queries = queries.reshape(row_count, heads_here, HEAD)
    tail_keys = tail_cache[:, :, 0].reshape(row_count, tail_slots, heads_here, HEAD)
    tail_values = tail_cache[:, :, 1].reshape(row_count, tail_slots, heads_here, HEAD)
    fresh_keys = fresh_cache[:, 0].reshape(row_count, heads_here, HEAD)
    fresh_values = fresh_cache[:, 1].reshape(row_count, heads_here, HEAD)
    slot_ids = jnp.arange(tail_slots)
    tail_scores = (
        jnp.einsum("qhd,qjhd->qhj", home_queries, tail_keys, preferred_element_type=f32) * inv_root
    )
    tail_scores = tail_scores + slopes[None, :, None] * slot_ids.astype(f32)[None, None, :]
    tail_scores = jnp.where(
        slot_ids[None, None, :] < tail_len[:, None, None], tail_scores, masked_score
    )
    own_scores = (
        jnp.einsum("qhd,qhd->qh", home_queries, fresh_keys, preferred_element_type=f32) * inv_root
    )
    own_scores = own_scores + slopes[None, :] * tail_len.astype(f32)[:, None]
    home_top = jnp.maximum(tail_scores.max(-1), own_scores)
    mine = lax.dynamic_slice_in_dim(group_top, req_index * row_count, row_count, 0)
    merged = lax.dynamic_update_slice_in_dim(
        group_top, jnp.maximum(mine, home_top), req_index * row_count, 0
    )
    all_top = lax.pmax(merged, "req")
    reference_top = all_top.reshape(group_count, row_count, heads_here)[safe_group]
    weights = jnp.where(usable[:, None, None, :], jnp.exp(scores - reference_top[..., None]), 0.0)
    page_totals = weights.sum(-1)
    upper_part, lower_part = split_halves(weights)
    page_accum = jnp.einsum("pqhs,pshd->pqhd", upper_part, page_values, preferred_element_type=f32)
    page_accum = page_accum + jnp.einsum(
        "pqhs,pshd->pqhd", lower_part, page_values, preferred_element_type=f32
    )
    accum_upper, accum_lower = split_halves(page_accum.reshape(page_count, -1))
    spread = member.T.astype(jnp.bfloat16)
    accum = jnp.dot(spread, accum_upper, preferred_element_type=f32)
    accum = accum + jnp.dot(spread, accum_lower, preferred_element_type=f32)
    totals = jnp.dot(member.T.astype(f32), page_totals.reshape(page_count, -1), precision=highest)
    totals, accum = (
        totals.reshape(group_count * row_count, heads_here),
        accum.reshape(group_count * row_count, feat_width),
    )
    pool_totals, pool_accum = (
        lax.psum_scatter(totals, "req", scatter_dimension=0, tiled=True),
        lax.psum_scatter(accum, "req", scatter_dimension=0, tiled=True),
    )
    pool_accum = pool_accum.reshape(row_count, heads_here, HEAD)
    row_top = lax.dynamic_slice_in_dim(all_top, req_index * row_count, row_count, 0)
    tail_weights = jnp.exp(tail_scores - row_top[:, :, None])
    own_weights = jnp.exp(own_scores - row_top)
    totals = tail_weights.sum(-1) + own_weights
    upper_part, lower_part = split_halves(tail_weights)
    accum = jnp.einsum("qhj,qjhd->qhd", upper_part, tail_values, preferred_element_type=f32)
    accum = accum + jnp.einsum("qhj,qjhd->qhd", lower_part, tail_values, preferred_element_type=f32)
    home_accum = accum + own_weights[:, :, None] * fresh_values.astype(f32)
    attention = ((pool_accum + home_accum) / (pool_totals + totals)[:, :, None]).astype(
        jnp.bfloat16
    )
    attention = attention.reshape(row_count, feat_width)
    partial_value = jnp.dot(attention, out_weight, preferred_element_type=f32)
    model_width = residual.shape[1]
    own_start = lax.axis_index("tp") * feat_width
    summed = lax.psum_scatter(
        partial_value.astype(jnp.bfloat16), "tp", scatter_dimension=1, tiled=True
    ).astype(jnp.float32)
    bias_mine = lax.dynamic_slice_in_dim(out_bias, own_start, feat_width, 0).astype(f32)
    attention_mine = (summed + bias_mine[None, :]).astype(jnp.bfloat16)
    residual_mine = lax.dynamic_slice_in_dim(residual, own_start, feat_width, 1).astype(f32)
    hidden_mine = residual_mine + attention_mine.astype(f32)
    first_sum, second_sum = lax.psum(
        (jnp.sum(hidden_mine, -1), jnp.sum(hidden_mine * hidden_mine, -1)), "tp"
    )
    row_mean = (first_sum / model_width)[:, None]
    mean_square = (second_sum / model_width)[:, None]
    row_var = mean_square - row_mean * row_mean
    normed = (
        (hidden_mine - row_mean)
        * lax.rsqrt(row_var + norm_epsilon)
        * norm_gain.astype(f32)[None, :]
    )
    normed = normed + norm_shift.astype(f32)[None, :]
    return (attention_mine, normed.astype(jnp.bfloat16))


def solution(mesh):
    in_specs = (
        P("req", "tp"),
        P("req", None, "tp"),
        P("req", None, None, "tp"),
        P("req"),
        P("req", None, None, "tp"),
        P("req"),
        P("req"),
        P(),
        P("req", None),
        P("tp", None),
        P(),
        P("tp"),
        P("tp"),
    )
    out_specs = (P("req", "tp"), P("req", "tp"))
    return jax.shard_map(local, mesh=mesh, in_specs=in_specs, out_specs=out_specs, check_vma=False)
```

profile of v0, /device:TPU:1, one launch (start us, length us, event | category | flops | bytes accessed | tf_op | source)
XLA Modules:
  0.0 528.3 jit_solution(4596948644088355456)
XLA Ops:
  7.2 0.7 compare_select_fusion
  8.0 0.7 broadcast_compare_fusion
  8.6 0.7 iota_compare_fusion
  9.4 57.6 %all_gather.3 = bf16[1024,256]{1,0:T(8,128)(2,1)S(1)} all-gather(bf16[16,256]{1,0:T(8,128)(2,1)} %param.13), channel_id=1, replica_groups=mesh['req'=64,'tp'=8] {'req'}, dimensions={0}, use_global_device_ids=true | all-gather | bytes 532480 | tf_op jit(solution)/shard_map/all_gather | solution.py:49
  67.0 0.7 reshape.271
  67.7 0.7 reshape.226
  68.4 0.7 iota_compare_fusion.3
  69.1 0.7 convert_element_type.100
  69.8 1.4 gather_fusion
  71.2 0.7 subtract_convert_fusion.5
  71.9 0.7 fusion.31
  72.6 0.1 reshape.224
  72.9 0.6 gather_fusion.1
  73.5 10.7 %slice_reduce_fusion = (bf16[32,64,256]{2,1,0:T(8,128)(2,1)S(1)}, bf16[32,64,256]{2,1,0:T(8,128)(2,1)S(1)}) fusion(bf16[32,64,2,256]{3,2,1,0:T(2,128)(2,1)} %param.17), kind=kLoop, calls=%fused_computation.5 | loop fusion | bytes 4194304 | tf_op jit(solution)/shard_map/slice | solution.py:54
  84.2 0.8 fusion.48
  85.0 0.2 select_reduce_fusion
  85.3 0.1 reshape.225
  85.5 2.9 slice_reduce_fusion.2
  88.4 0.1 fusion.25
  88.6 1.2 fusion.17
  89.8 0.1 fusion.46
  90.0 0.2 dynamic_update_slice.3
  90.2 125.7 %pmax.7 = f32[1024,2]{0,1:T(2,128)S(1)} all-reduce(f32[1024,2]{0,1:T(2,128)S(1)} %dynamic_update_slice.3), channel_id=1, replica_groups=mesh['req'=64,'tp'=8] {'req'}, use_global_device_ids=true, to_apply=%region_3.4 | all-reduce | flops 2048 | bytes 16384 | tf_op jit(solution)/shard_map/pmax | solution.py:91
  216.0 0.6 gather_fusion.2
  216.6 0.4 fusion.11
  217.1 0.4 fusion.5
  217.4 0.5 fusion
  217.9 0.3 copy.55
  218.2 0.4 reshape.228
  218.7 0.4 fusion.35
  219.1 0.4 convolution_add_fusion
  219.5 1.1 reshape.229
  221.0 0.3 fusion.38
  221.3 0.3 reshape.232
  221.6 1.3 dynamic-slice
  223.5 246.9 %all-reduce = f32[1024,2]{1,0:T(8,128)S(1)} all-reduce(f32[1024,2]{1,0:T(8,128)S(1)} %reshape.232), channel_id=3, replica_groups=mesh['req'=64,'tp'=8] {'req'}, use_global_device_ids=true, to_apply=%region_6.7.clone | all-reduce | flops 2048 | bytes 16384
  470.5 0.2 fusion.36
  470.8 0.1 copy.56
  470.9 0.2 fusion.13
  471.1 0.2 fusion.15
  471.3 0.7 reshape.230
  472.0 0.1 fusion.32
  472.2 0.9 convolution_convert_fusion
  473.1 0.8 dynamic-slice_convert_fusion
  473.9 33.1 %reduce-scatter.5.cloned.1.call-done = bf16[16,256]{1,0:T(8,128)(2,1)} async-done(((bf16[16,2048]{1,0:T(8,128)(2,1)}), bf16[16,256]{1,0:T(8,128)(2,1)}) %reduce-scatter.5.cloned.1.call-update) | async-done | bytes 8208 | tf_op jit(solution)/shard_map/reduce_scatter | solution.py:129
  507.0 0.8 fusion.33
  507.9 12.2 %all-reduce.1 = (f32[16]{0:T(128)S(1)}, f32[16]{0:T(128)S(1)}) all-reduce(f32[16]{0:T(128)S(1)} %get-tuple-element.7, f32[16]{0:T(128)S(1)} %get-tuple-element.6), channel_id=1, replica_groups=mesh['req'=64,'tp'=8] {'tp'}, use_global_device_ids=true, to_apply=%region_12.13 | all-reduce | flops 32 | bytes 256 | tf_op jit(solution)/shard_map/psum | solution.py:136
  520.1 1.4 add_convert_fusion
  (43 shorter events, 1.4 us)
Async XLA Ops:
  7.2 465.0 %copy-start = (bf16[256,2048]{1,0:T(8,128)(2,1)S(1)}, bf16[256,2048]{1,0:T(8,128)(2,1)}, u32[]{:S(2)}) copy-start(bf16[256,2048]{1,0:T(8,128)(2,1)} %param.22) | copy-start | bytes 3145732
  7.2 464.1 %reduce-scatter.3.cloned.1.call-start = ((), (), s32[]{:S(2)}) async-start(), calls=%async_computation.2 | async-start | bytes 1064960 | tf_op jit(solution)/shard_map/reduce_scatter | solution.py:111
  84.1 1.3 copy-start.1
  84.2 4.2 copy-start.2
  217.9 0.8 copy-start.4
  220.7 252.4 %copy-start.5 = (bf16[256]{0:T(256)(128)(2,1)S(1)}, bf16[256]{0:T(256)(128)(2,1)}, u32[]{:S(2)}) copy-start(bf16[256]{0:T(256)(128)(2,1)} %param.24) | copy-start | bytes 1540
  220.7 252.4 %copy-start.6 = (bf16[256]{0:T(256)(128)(2,1)S(1)}, bf16[256]{0:T(256)(128)(2,1)}, u32[]{:S(2)}) copy-start(bf16[256]{0:T(256)(128)(2,1)} %param.25) | copy-start | bytes 1540
  220.7 286.3 %reduce-scatter.5.cloned.1.call-start = ((), (), s32[]{:S(2)}) async-start(), calls=%async_computation.3 | async-start | bytes 73728 | tf_op jit(solution)/shard_map/reduce_scatter | solution.py:129
  507.8 13.6 %copy-start.3 = (bf16[16,256]{1,0:T(8,128)(2,1)}, bf16[16,256]{1,0:T(8,128)(2,1)S(1)}, u32[]{:S(2)}) copy-start(bf16[16,256]{1,0:T(8,128)(2,1)S(1)} %get-tuple-element.10) | copy-start | bytes 24580
Sparse Core Ops, SparseCore 0:
  220.8 142.0 reduce-scatter.2
  473.2 33.7 reduce-scatter.4
where the time goes:
time: 537 us; the launch traced here: 528 us
  blocking collectives  442 us (82%)
  waiting for transfers between devices  33.2 us (6%)
  local copies, waits for them, and re-layouts  22.9 us (4%)
  between operations  15 us (3%)
  other arithmetic  9.58 us (2%)
    unnamed x1, blocking collectives  247 us
    pmax x1, blocking collectives, local(): all_top = lax.pmax(merged, 'req')  126 us
    all_gather x1, blocking collectives, local(): everyone = lax.all_gather(queries, 'req', axis=0, tiled=True)  57.6 us
    reduce_scatter x1, waiting for transfers between devices, local(): lax.psum_scatter(partial_value.astype(jnp.bfloat16), 'tp', scatter_dimens...  33.1 us
    psum x1, blocking collectives, local(): lax.psum((jnp.sum(hidden_mine, -1), jnp.sum(hidden_mine * hidden_mine, -1...  12.2 us
  transfers between devices with their start and end apart: 2, of which 1 were waited for; matrix products, arithmetic and copies ran while one was open for 1% of the time, Pallas kernels for 0%

commit v1 on v0

--- a/solution.py
+++ b/solution.py
@@ -45,7 +45,9 @@
     group_count = prompt_len.shape[0]
     page_count = pool_cache.shape[0]
     tail_slots = tail_cache.shape[1]
-    req_index = lax.axis_index("req")
+    n_req = lax.axis_size("req")
+    assert group_count == n_req
+
     everyone = lax.all_gather(queries, "req", axis=0, tiled=True)
     by_group = everyone.reshape(group_count, row_count, heads_here, HEAD)
     safe_group = jnp.clip(page_group, 0, group_count - 1)
@@ -62,10 +64,46 @@
     )
     scores = scores + slopes[None, None, :, None] * offsets[:, None, None, :]
     scores = jnp.where(usable[:, None, None, :], scores, masked_score)
-    member = page_group[:, None] == jnp.arange(group_count)[None, :]
+
+    member = (page_group[:, None] == jnp.arange(group_count)[None, :]) & (page_group[:, None] >= 0)
     page_top = scores.max(-1)
-    group_top = jnp.where(member[:, :, None, None], page_top[:, None], masked_score).max(0)
-    group_top = group_top.reshape(group_count * row_count, heads_here)
+    local_top = jnp.where(member[:, :, None, None], page_top[:, None], masked_score).max(0)
+    page_ref = local_top[safe_group]
+    weights = jnp.where(usable[:, None, None, :], jnp.exp(scores - page_ref[..., None]), 0.0)
+    page_totals = weights.sum(-1)
+    upper_part, lower_part = split_halves(weights)
+    page_accum = jnp.einsum("pqhs,pshd->pqhd", upper_part, page_values, preferred_element_type=f32)
+    page_accum = page_accum + jnp.einsum(
+        "pqhs,pshd->pqhd", lower_part, page_values, preferred_element_type=f32
+    )
+    accum_upper, accum_lower = split_halves(page_accum.reshape(page_count, -1))
+    spread = member.T.astype(jnp.bfloat16)
+    group_accum = jnp.dot(spread, accum_upper, preferred_element_type=f32)
+    group_accum = group_accum + jnp.dot(spread, accum_lower, preferred_element_type=f32)
+    group_totals = jnp.dot(
+        member.T.astype(f32), page_totals.reshape(page_count, -1), precision=highest
+    )
+    stats_width = row_count * heads_here
+    pad_width = (-(group_accum.shape[1] + 2 * stats_width)) % 128
+    packed = jnp.concatenate(
+        [
+            group_accum,
+            local_top.reshape(group_count, stats_width),
+            group_totals,
+            jnp.zeros((group_count, pad_width), f32),
+        ],
+        axis=1,
+    )
+    arrived = lax.all_to_all(packed, "req", 0, 0, tiled=True)
+    accum_width = row_count * feat_width
+    part_accum = arrived[:, :accum_width].reshape(n_req, row_count, heads_here, HEAD)
+    part_top = arrived[:, accum_width : accum_width + stats_width].reshape(
+        n_req, row_count, heads_here
+    )
+    part_totals = arrived[:, accum_width + stats_width : accum_width + 2 * stats_width].reshape(
+        n_req, row_count, heads_here
+    )
+
     home_queries = queries.reshape(row_count, heads_here, HEAD)
     tail_keys = tail_cache[:, :, 0].reshape(row_count, tail_slots, heads_here, HEAD)
     tail_values = tail_cache[:, :, 1].reshape(row_count, tail_slots, heads_here, HEAD)
@@ -84,34 +122,10 @@
     )
     own_scores = own_scores + slopes[None, :] * tail_len.astype(f32)[:, None]
     home_top = jnp.maximum(tail_scores.max(-1), own_scores)
-    mine = lax.dynamic_slice_in_dim(group_top, req_index * row_count, row_count, 0)
-    merged = lax.dynamic_update_slice_in_dim(
-        group_top, jnp.maximum(mine, home_top), req_index * row_count, 0
-    )
-    all_top = lax.pmax(merged, "req")
-    reference_top = all_top.reshape(group_count, row_count, heads_here)[safe_group]
-    weights = jnp.where(usable[:, None, None, :], jnp.exp(scores - reference_top[..., None]), 0.0)
-    page_totals = weights.sum(-1)
-    upper_part, lower_part = split_halves(weights)
-    page_accum = jnp.einsum("pqhs,pshd->pqhd", upper_part, page_values, preferred_element_type=f32)
-    page_accum = page_accum + jnp.einsum(
-        "pqhs,pshd->pqhd", lower_part, page_values, preferred_element_type=f32
-    )
-    accum_upper, accum_lower = split_halves(page_accum.reshape(page_count, -1))
-    spread = member.T.astype(jnp.bfloat16)
-    accum = jnp.dot(spread, accum_upper, preferred_element_type=f32)
-    accum = accum + jnp.dot(spread, accum_lower, preferred_element_type=f32)
-    totals = jnp.dot(member.T.astype(f32), page_totals.reshape(page_count, -1), precision=highest)
-    totals, accum = (
-        totals.reshape(group_count * row_count, heads_here),
-        accum.reshape(group_count * row_count, feat_width),
-    )
-    pool_totals, pool_accum = (
-        lax.psum_scatter(totals, "req", scatter_dimension=0, tiled=True),
-        lax.psum_scatter(accum, "req", scatter_dimension=0, tiled=True),
-    )
-    pool_accum = pool_accum.reshape(row_count, heads_here, HEAD)
-    row_top = lax.dynamic_slice_in_dim(all_top, req_index * row_count, row_count, 0)
+    row_top = jnp.maximum(home_top, part_top.max(0))
+    part_scale = jnp.exp(part_top - row_top[None])
+    pool_totals = jnp.sum(part_scale * part_totals, 0)
+    pool_accum = jnp.sum(part_scale[..., None] * part_accum, 0)
     tail_weights = jnp.exp(tail_scores - row_top[:, :, None])
     own_weights = jnp.exp(own_scores - row_top)
     totals = tail_weights.sum(-1) + own_weights

time: 537 us -> 194 us (0.36)
  the two profiles are of different devices: /device:TPU:1 before, /device:TPU:2 now
where the time goes in v1:
time: 194 us; the launch traced here: 193 us
  blocking collectives  71.6 us (37%)
  waiting for transfers between devices  59.5 us (31%)
  local copies, waits for them, and re-layouts  25.5 us (13%)
  between operations  14.3 us (7%)
  other arithmetic  11.6 us (6%)
  starting transfers between devices  6.56 us (3%)
  matrix products  4.23 us (2%)
    all_gather x1, blocking collectives, local(): everyone = lax.all_gather(queries, 'req', axis=0, tiled=True)  56 us
    reduce_scatter x1, waiting for transfers between devices, local(): lax.psum_scatter(partial_value.astype(jnp.bfloat16), 'tp', scatter_dimens...  33.2 us
    all_to_all x1, waiting for transfers between devices, local(): arrived = lax.all_to_all(packed, 'req', 0, 0, tiled=True)  26.2 us
    psum x1, blocking collectives, local(): lax.psum((jnp.sum(hidden_mine, -1), jnp.sum(hidden_mine * hidden_mine, -1...  15.6 us
    slice x1, local copies, waits for them, and re-layouts, local(): pool_cache[:, :, 1].reshape(page_count, PAGE, heads_here, HEAD)  10.7 us
    all_to_all x1, starting transfers between devices, local(): arrived = lax.all_to_all(packed, 'req', 0, 0, tiled=True)  6.34 us
    all_to_all x2, local copies, waits for them, and re-layouts, local(): arrived = lax.all_to_all(packed, 'req', 0, 0, tiled=True)  5.25 us
  transfers between devices with their start and end apart: 2, of which 2 were waited for; matrix products, arithmetic and copies ran while one was open for 3% of the time, Pallas kernels for 0%

profile of v1, /device:TPU:2, one launch (start us, length us, event | category | flops | bytes accessed | tf_op | source)
XLA Modules:
  0.0 193.3 jit_solution(1942544731091071462)
XLA Ops:
  7.2 0.7 compare_select_fusion
  7.9 0.7 broadcast_compare_fusion
  8.6 1.4 gather_fusion
  10.0 0.7 subtract_convert_fusion.5
  10.7 0.8 fusion.33
  11.5 56.0 %all_gather.3 = bf16[1024,256]{1,0:T(8,128)(2,1)S(1)} all-gather(bf16[16,256]{1,0:T(8,128)(2,1)} %param.13), channel_id=1, replica_groups=mesh['req'=64,'tp'=8] {'req'}, dimensions={0}, use_global_device_ids=true | all-gather | bytes 532480 | tf_op jit(solution)/shard_map/all_gather | solution.py:51
  67.5 0.1 reshape.244
  67.7 0.6 gather_fusion.1
  68.3 10.7 %slice_reduce_fusion = (bf16[32,64,256]{2,1,0:T(8,128)(2,1)S(1)}, bf16[32,64,256]{2,1,0:T(8,128)(2,1)S(1)}) fusion(bf16[32,64,2,256]{3,2,1,0:T(2,128)(2,1)} %param.17), kind=kLoop, calls=%fused_computation.7 | loop fusion | bytes 4194304 | tf_op jit(solution)/shard_map/slice | solution.py:56
  79.1 0.8 fusion.50
  79.9 0.2 select_reduce_fusion
  80.2 0.6 gather_fusion.2
  80.8 0.4 fusion.12
  81.2 0.4 fusion.6
  81.6 0.5 fusion.1
  82.1 0.3 copy.52
  82.4 0.4 reshape.245
  82.9 0.4 fusion.48
  83.3 0.4 convolution_add_fusion
  83.8 0.3 fusion.42
  84.2 0.3 concatenate.3
  84.5 2.1 %copy.57 = f32[64,1,4224]{2,1,0:T(1,128)} copy(f32[64,1,4224]{2,0,1:T(8,128)S(1)} %bitcast.87) | data formatting | bytes 2162688 | tf_op jit(solution)/shard_map/all_to_all | solution.py:97
  86.6 6.3 %all-to-all-start = ((f32[64,1,4224]{2,1,0:T(1,128)}), f32[64,1,4224]{2,1,0:T(1,128)}, u32[]{:S(2)}, u32[]{:S(2)}) async-start(f32[64,1,4224]{2,1,0:T(1,128)} %copy.57), calls=%async_computation | async-start | bytes 2162688 | tf_op jit(solution)/shard_map/all_to_all | solution.py:97
  93.0 0.2 reduce-scatter.2.cloned.1.call-start
  93.7 2.2 %slice_reduce_fusion.2 = (bf16[16,32,256]{2,1,0:T(8,128)(2,1)S(1)}, bf16[16,32,256]{2,1,0:T(8,128)(2,1)S(1)}) fusion(bf16[16,32,2,256]{3,2,1,0:T(2,128)(2,1)S(1)} %copy-done.1), kind=kLoop, calls=%fused_computation.22 | loop fusion | bytes 1048576 | tf_op jit(solution)/shard_map/slice | solution.py:109
  95.8 0.2 fusion.18
  96.2 26.2 %all-to-all-done = f32[64,1,4224]{2,1,0:T(1,128)} async-done(((f32[64,1,4224]{2,1,0:T(1,128)}), f32[64,1,4224]{2,1,0:T(1,128)}, u32[]{:S(2)}, u32[]{:S(2)}) %all-to-all-start) | async-done | bytes 1081376 | tf_op jit(solution)/shard_map/all_to_all | solution.py:97
  122.4 3.1 %copy.58 = f32[64,1,4224]{0,2,1:T(8,128)S(1)} copy(f32[64,1,4224]{2,1,0:T(1,128)} %all-to-all-done) | data formatting | bytes 2162688 | tf_op jit(solution)/shard_map/all_to_all | solution.py:97
  125.5 0.1 slice_reduce_fusion.5
  126.0 0.2 fusion.37
  126.3 0.7 fusion.26
  127.0 0.7 reduce_sum.62
  127.7 0.6 copy.63
  128.4 1.3 add_add_fusion
  129.7 0.8 copy.61
  130.5 0.8 copy.64
  131.2 0.2 fusion.14
  131.4 0.2 fusion.16
  131.7 0.6 fusion
  132.3 0.1 fusion.35
  132.4 0.9 convolution_convert_fusion
  133.3 0.7 convert_element_type.119
  134.0 0.7 convert_element_type.120
  134.7 0.8 dynamic-slice_convert_fusion
  135.4 33.2 %reduce-scatter.2.cloned.1.call-done = bf16[16,256]{1,0:T(8,128)(2,1)} async-done(((bf16[16,2048]{1,0:T(8,128)(2,1)}), bf16[16,256]{1,0:T(8,128)(2,1)}) %reduce-scatter.2.cloned.1.call-update) | async-done | bytes 8208 | tf_op jit(solution)/shard_map/reduce_scatter | solution.py:143
  168.7 0.8 fusion.36
  169.5 15.6 %all-reduce = (f32[16]{0:T(128)S(1)}, f32[16]{0:T(128)S(1)}) all-reduce(f32[16]{0:T(128)S(1)} %get-tuple-element.7, f32[16]{0:T(128)S(1)} %get-tuple-element.6), channel_id=1, replica_groups=mesh['req'=64,'tp'=8] {'tp'}, use_global_device_ids=true, to_apply=%region_12.13 | all-reduce | flops 32 | bytes 256 | tf_op jit(solution)/shard_map/psum | solution.py:150
  185.1 1.4 add_convert_fusion
  (46 shorter events, 1.6 us)
Async XLA Ops:
  7.2 125.3 %copy-start = (bf16[256,2048]{1,0:T(8,128)(2,1)S(1)}, bf16[256,2048]{1,0:T(8,128)(2,1)}, u32[]{:S(2)}) copy-start(bf16[256,2048]{1,0:T(8,128)(2,1)} %param.22) | copy-start | bytes 3145732
  82.1 0.8 copy-start.5
  84.4 8.8 %copy-start.2 = (bf16[16,256]{1,0:T(8,128)(2,1)S(1)}, bf16[16,256]{1,0:T(8,128)(2,1)}, u32[]{:S(2)}) copy-start(bf16[16,256]{1,0:T(8,128)(2,1)} %param.13) | copy-start | bytes 24580
  84.4 8.8 %copy-start.3 = (bf16[16,2,256]{2,1,0:T(2,128)(2,1)S(1)}, bf16[16,2,256]{2,1,0:T(2,128)(2,1)}, u32[]{:S(2)}) copy-start(bf16[16,2,256]{2,1,0:T(2,128)(2,1)} %param.14) | copy-start | bytes 49156
  84.4 9.1 %copy-start.7 = (s32[16]{0:T(128)S(1)}, s32[16]{0:T(128)}, u32[]{:S(2)}) copy-start(s32[16]{0:T(128)} %param.16) | copy-start | bytes 196
  84.5 9.2 %copy-start.1 = (bf16[16,32,2,256]{3,2,1,0:T(2,128)(2,1)S(1)}, bf16[16,32,2,256]{3,2,1,0:T(2,128)(2,1)}, u32[]{:S(2)}) copy-start(bf16[16,32,2,256]{3,2,1,0:T(2,128)(2,1)} %param.15) | copy-start | bytes 1572868
  86.6 35.8 %all-to-all-start = ((f32[64,1,4224]{2,1,0:T(1,128)}), f32[64,1,4224]{2,1,0:T(1,128)}, u32[]{:S(2)}, u32[]{:S(2)}) async-start(f32[64,1,4224]{2,1,0:T(1,128)} %copy.57), calls=%async_computation | async-start | bytes 2162688 | tf_op jit(solution)/shard_map/all_to_all | solution.py:97
  93.0 75.7 %reduce-scatter.2.cloned.1.call-start = ((), (), s32[]{:S(2)}) async-start(), calls=%async_computation.2 | async-start | bytes 73728 | tf_op jit(solution)/shard_map/reduce_scatter | solution.py:143
  93.5 32.3 %copy-start.6 = (f32[16]{0:T(128)}, f32[16]{0:T(128)S(1)}, u32[]{:S(2)}) copy-start(f32[16]{0:T(128)S(1)} %convert_element_type.106) | copy-start | bytes 196
  169.5 17.0 %copy-start.4 = (bf16[16,256]{1,0:T(8,128)(2,1)}, bf16[16,256]{1,0:T(8,128)(2,1)S(1)}, u32[]{:S(2)}) copy-start(bf16[16,256]{1,0:T(8,128)(2,1)S(1)} %get-tuple-element.10) | copy-start | bytes 24580
Sparse Core Ops, SparseCore 0:
  133.5 35.1 reduce-scatter.1

commit v2 on v1

--- a/solution.py
+++ b/solution.py
@@ -48,7 +48,8 @@
     n_req = lax.axis_size("req")
     assert group_count == n_req
 
-    everyone = lax.all_gather(queries, "req", axis=0, tiled=True)
+    copies = jnp.broadcast_to(queries.reshape(1, row_count * feat_width), (n_req, row_count * feat_width))
+    everyone = lax.all_to_all(copies, "req", 0, 0, tiled=True)
     by_group = everyone.reshape(group_count, row_count, heads_here, HEAD)
     safe_group = jnp.clip(page_group, 0, group_count - 1)
     page_queries = by_group[safe_group]
@@ -140,19 +141,15 @@
     partial_value = jnp.dot(attention, out_weight, preferred_element_type=f32)
     model_width = residual.shape[1]
     own_start = lax.axis_index("tp") * feat_width
-    summed = lax.psum_scatter(
-        partial_value.astype(jnp.bfloat16), "tp", scatter_dimension=1, tiled=True
-    ).astype(jnp.float32)
-    bias_mine = lax.dynamic_slice_in_dim(out_bias, own_start, feat_width, 0).astype(f32)
-    attention_mine = (summed + bias_mine[None, :]).astype(jnp.bfloat16)
-    residual_mine = lax.dynamic_slice_in_dim(residual, own_start, feat_width, 1).astype(f32)
-    hidden_mine = residual_mine + attention_mine.astype(f32)
-    first_sum, second_sum = lax.psum(
-        (jnp.sum(hidden_mine, -1), jnp.sum(hidden_mine * hidden_mine, -1)), "tp"
-    )
-    row_mean = (first_sum / model_width)[:, None]
-    mean_square = (second_sum / model_width)[:, None]
+    gathered = lax.all_gather(partial_value.astype(jnp.bfloat16), "tp", axis=0, tiled=False)
+    projected = gathered.astype(f32).sum(0) + out_bias.astype(f32)[None, :]
+    attention_full = projected.astype(jnp.bfloat16)
+    hidden = residual.astype(f32) + attention_full.astype(f32)
+    row_mean = jnp.mean(hidden, -1, keepdims=True)
+    mean_square = jnp.mean(hidden * hidden, -1, keepdims=True)
     row_var = mean_square - row_mean * row_mean
+    attention_mine = lax.dynamic_slice_in_dim(attention_full, own_start, feat_width, 1)
+    hidden_mine = lax.dynamic_slice_in_dim(hidden, own_start, feat_width, 1)
     normed = (
         (hidden_mine - row_mean)
         * lax.rsqrt(row_var + norm_epsilon)

time: 194 us -> 134 us (0.69)
  the two profiles are of different devices: /device:TPU:2 before, /device:TPU:6 now
where the time goes in v2:
time: 134 us; the launch traced here: 133 us
  local copies, waits for them, and re-layouts  33.5 us (25%)
  waiting for transfers between devices  30.1 us (22%)
  blocking collectives  27.2 us (20%)
  starting transfers between devices  20.3 us (15%)
  other arithmetic  15.2 us (11%)
  matrix products  5.51 us (4%)
    all_gather x1, blocking collectives, local(): lax.all_gather(partial_value.astype(jnp.bfloat16), 'tp', axis=0, tiled=Fa...  27.2 us
    all_to_all x1, waiting for transfers between devices, local(): arrived = lax.all_to_all(packed, 'req', 0, 0, tiled=True)  25.3 us
    all_to_all x1, starting transfers between devices, local(): everyone = lax.all_to_all(copies, 'req', 0, 0, tiled=True)  14 us
    slice x1, local copies, waits for them, and re-layouts, local(): pool_cache[:, :, 1].reshape(page_count, PAGE, heads_here, HEAD)  11.7 us
    all_to_all x1, starting transfers between devices, local(): arrived = lax.all_to_all(packed, 'req', 0, 0, tiled=True)  6.25 us
    unnamed x33, local copies, waits for them, and re-layouts  5.69 us
    all_to_all x2, local copies, waits for them, and re-layouts, local(): arrived = lax.all_to_all(packed, 'req', 0, 0, tiled=True)  5.25 us
    all_to_all x1, waiting for transfers between devices, local(): everyone = lax.all_to_all(copies, 'req', 0, 0, tiled=True)  4.78 us
  transfers between devices with their start and end apart: 2, of which 2 were waited for; matrix products, arithmetic and copies ran while one was open for 13% of the time, Pallas kernels for 0%

profile of v2, /device:TPU:6, one launch (start us, length us, event | category | flops | bytes accessed | tf_op | source)
XLA Modules:
  0.0 132.9 jit_solution(18227831158995961358)
XLA Ops:
  0.6 0.8 copy.74
  1.4 1.0 broadcast_in_dim.64
  2.5 0.5 broadcast.250
  3.0 3.9 %reduce.16 = bf16[64,4096]{1,0:T(8,128)(2,1)S(1)} reduce(bf16[64,1,4096]{2,1,0:T(2,128)(2,1)S(1)} %broadcast_in_dim.64, bf16[]{:T(256)} %broadcast.250), dimensions={1}, to_apply=%broadcast_in_dim.64.reduce_sub_computation | reduce | bytes 1048578 | tf_op jit(solution)/shard_map/broadcast_in_dim | solution.py:51
  6.9 1.2 reshape.319
  8.1 14.0 %all-to-all-start = ((bf16[64,2,2048]{2,1,0:T(2,128)(2,1)}), bf16[64,2,2048]{2,1,0:T(2,128)(2,1)}, u32[]{:S(2)}, u32[]{:S(2)}) async-start(bf16[64,2,2048]{2,1,0:T(2,128)(2,1)} %reshape.319), calls=%async_computation | async-start | bytes 1048576 | tf_op jit(solution)/shard_map/all_to_all | solution.py:52
  22.2 0.7 gather_fusion
  23.2 11.7 %slice_reduce_fusion = (bf16[32,64,256]{2,1,0:T(8,128)(2,1)S(1)}, bf16[32,64,256]{2,1,0:T(8,128)(2,1)}) fusion(bf16[32,64,2,256]{3,2,1,0:T(2,128)(2,1)} %param.17), kind=kLoop, calls=%fused_computation.7 | loop fusion | bytes 4194304 | tf_op jit(solution)/shard_map/slice | solution.py:57
  34.8 4.8 %all-to-all-done = bf16[64,2,2048]{2,1,0:T(2,128)(2,1)} async-done(((bf16[64,2,2048]{2,1,0:T(2,128)(2,1)}), bf16[64,2,2048]{2,1,0:T(2,128)(2,1)}, u32[]{:S(2)}, u32[]{:S(2)}) %all-to-all-start) | async-done | bytes 524320 | tf_op jit(solution)/shard_map/all_to_all | solution.py:52
  39.6 3.6 %reshape.320 = bf16[64,1,4096]{2,1,0:T(2,128)(2,1)S(1)} reshape(bf16[64,2,2048]{2,1,0:T(2,128)(2,1)} %all-to-all-done) | data formatting | bytes 1048576
  43.3 4.0 %reduce.4 = bf16[64,4096]{1,0:T(8,128)(2,1)} reduce(bf16[64,1,4096]{2,1,0:T(2,128)(2,1)S(1)} %reshape.320, bf16[]{:T(256)} %constant.55), dimensions={1}, to_apply=%all_to_all.12.reduce_sub_computation | reduce | bytes 1048578 | tf_op jit(solution)/shard_map/all_to_all | solution.py:52
  47.2 1.4 %reshape.266 = bf16[64,16,2,128]{3,2,1,0:T(2,128)(2,1)S(1)} reshape(bf16[64,4096]{1,0:T(8,128)(2,1)} %reduce.4) | data formatting | bytes 1048576 | tf_op jit(solution)/shard_map/reshape | solution.py:53
  48.7 0.6 gather_fusion.1
  49.3 2.0 %fusion.50 = (f32[32,16,2]{1,2,0:T(2,128)S(1)}, f32[32,16,2,64]{3,1,2,0:T(8,128)S(1)}) fusion(f32[32,2,64]{2,1,0:T(2,128)S(1)} %broadcast_multiply_fusion, bf16[32,16,2,128]{3,1,2,0:T(8,128)(2,1)S(1)} %gather_fusion.1, pred[32,64]{1,0:T(8,128)(4,1)S(1)} %get-tuple-element.22, bf16[32,64,256]{2,1,0:T(8,128)(2,1)} %get-tuple-element.3), kind=kOutput, calls=%fused_computation.96 | convolution fusion | flops 17038336 | bytes 1595392 | tf_op jit(solution)/shard_map/pqhd,pshd->pqhs/dot_general | solution.py:63
  51.3 0.2 select_reduce_fusion
  51.6 0.6 gather_fusion.2
  52.2 0.4 fusion.12
  52.7 0.4 fusion.6
  53.1 0.5 fusion.1
  53.5 0.3 copy.43
  53.8 0.4 reshape.267
  54.3 0.4 fusion.48
  54.7 0.4 convolution_add_fusion
  55.2 0.3 fusion.41
  55.6 0.3 concatenate.3
  55.9 2.1 %copy.48 = f32[64,1,4224]{2,1,0:T(1,128)} copy(f32[64,1,4224]{2,0,1:T(8,128)S(1)} %bitcast.91) | data formatting | bytes 2162688 | tf_op jit(solution)/shard_map/all_to_all | solution.py:98
  58.1 6.2 %all-to-all-start.1 = ((f32[64,1,4224]{2,1,0:T(1,128)}), f32[64,1,4224]{2,1,0:T(1,128)}, u32[]{:S(2)}, u32[]{:S(2)}) async-start(f32[64,1,4224]{2,1,0:T(1,128)} %copy.48), calls=%async_computation.1 | async-start | bytes 2162688 | tf_op jit(solution)/shard_map/all_to_all | solution.py:98
  64.7 0.6 convert_element_type.119
  65.2 0.6 convert_element_type.120
  66.0 2.2 %slice_reduce_fusion.2 = (bf16[16,32,256]{2,1,0:T(8,128)(2,1)S(1)}, bf16[16,32,256]{2,1,0:T(8,128)(2,1)S(1)}) fusion(bf16[16,32,2,256]{3,2,1,0:T(2,128)(2,1)S(1)} %copy-done.2), kind=kLoop, calls=%fused_computation.23 | loop fusion | bytes 1048576 | tf_op jit(solution)/shard_map/slice | solution.py:110
  68.1 0.2 fusion.18
  68.5 25.3 %all-to-all-done.1 = f32[64,1,4224]{2,1,0:T(1,128)} async-done(((f32[64,1,4224]{2,1,0:T(1,128)}), f32[64,1,4224]{2,1,0:T(1,128)}, u32[]{:S(2)}, u32[]{:S(2)}) %all-to-all-start.1) | async-done | bytes 1081376 | tf_op jit(solution)/shard_map/all_to_all | solution.py:98
  93.8 3.1 %copy.49 = f32[64,1,4224]{0,2,1:T(8,128)S(1)} copy(f32[64,1,4224]{2,1,0:T(1,128)} %all-to-all-done.1) | data formatting | bytes 2162688 | tf_op jit(solution)/shard_map/all_to_all | solution.py:98
  96.9 0.1 slice_reduce_fusion.5
  97.4 1.2 fusion.36
  98.8 0.2 fusion.26
  99.0 0.7 copy.54
  99.7 1.3 %add_add_fusion = (f32[16,2]{0,1:T(2,128)S(1)}, f32[16,2]{0,1:T(2,128)}) fusion(f32[16,2]{0,1:T(2,128)} %copy.54, f32[16,2]{0,1:T(2,128)} %get-tuple-element.15, f32[16,2]{0,1:T(2,128)S(1)} %maximum_maximum_fusion, f32[16]{0:T(128)} %copy-done.8, f32[2]{0:T(128)S(1)} %multiply_exponential_fusion, f32[16,2]{0,1:T(2,128)S(1)} %copy.63), kind=kLoop, calls=%fused_computation.80 | loop fusion | flops 192 | bytes 840 | tf_op jit(solution)/shard_map/add | solution.py:137
  101.1 0.8 copy.52
  101.9 0.9 fusion.14
  102.8 0.2 fusion.16
  103.1 0.6 fusion
  103.7 0.1 fusion.35
  103.8 0.2 convolution_convert_fusion
  104.1 27.2 %all-gather = bf16[128,2048]{1,0:T(8,128)(2,1)S(1)} all-gather(bf16[16,2048]{1,0:T(8,128)(2,1)S(1)} %convolution_convert_fusion), channel_id=2, replica_groups=mesh['req'=64,'tp'=8] {'tp'}, dimensions={0}, use_global_device_ids=true | all-gather | bytes 589824 | tf_op jit(solution)/shard_map/all_gather | solution.py:144
  131.4 0.2 fusion.45
  131.6 0.6 constant_dynamic-slice_fusion
  132.2 0.7 add_convert_fusion.1
  (68 shorter events, 2.1 us)
Async XLA Ops:
  0.6 103.2 %copy-start = (bf16[256,2048]{1,0:T(8,128)(2,1)S(1)}, bf16[256,2048]{1,0:T(8,128)(2,1)}, u32[]{:S(2)}) copy-start(bf16[256,2048]{1,0:T(8,128)(2,1)} %param.22) | copy-start | bytes 3145732
  2.4 19.7 %copy-start.6 = (s32[32]{0:T(128)S(1)}, s32[32]{0:T(128)}, u32[]{:S(2)}) copy-start(s32[32]{0:T(128)} %param.18) | copy-start | bytes 388
  2.5 19.7 %copy-start.1 = (s32[64]{0:T(128)S(1)}, s32[64]{0:T(128)}, u32[]{:S(2)}) copy-start(s32[64]{0:T(128)} %param.20) | copy-start | bytes 772
  3.0 19.9 %copy-start.9 = (s32[32]{0:T(128)S(1)}, s32[32]{0:T(128)}, u32[]{:S(2)}) copy-start(s32[32]{0:T(128)} %param.19) | copy-start | bytes 388
  8.1 31.5 %all-to-all-start = ((bf16[64,2,2048]{2,1,0:T(2,128)(2,1)}), bf16[64,2,2048]{2,1,0:T(2,128)(2,1)}, u32[]{:S(2)}, u32[]{:S(2)}) async-start(bf16[64,2,2048]{2,1,0:T(2,128)(2,1)} %reshape.319), calls=%async_computation | async-start | bytes 1048576 | tf_op jit(solution)/shard_map/all_to_all | solution.py:52
  55.9 8.5 %copy-start.4 = (bf16[16,256]{1,0:T(8,128)(2,1)S(1)}, bf16[16,256]{1,0:T(8,128)(2,1)}, u32[]{:S(2)}) copy-start(bf16[16,256]{1,0:T(8,128)(2,1)} %param.13) | copy-start | bytes 24580
  55.9 8.5 %copy-start.5 = (bf16[16,2,256]{2,1,0:T(2,128)(2,1)S(1)}, bf16[16,2,256]{2,1,0:T(2,128)(2,1)}, u32[]{:S(2)}) copy-start(bf16[16,2,256]{2,1,0:T(2,128)(2,1)} %param.14) | copy-start | bytes 49156
  55.9 8.8 %copy-start.12 = (s32[16]{0:T(128)S(1)}, s32[16]{0:T(128)}, u32[]{:S(2)}) copy-start(s32[16]{0:T(128)} %param.16) | copy-start | bytes 196
  55.9 8.8 %copy-start.7 = (bf16[2048]{0:T(1024)(128)(2,1)S(1)}, bf16[2048]{0:T(1024)(128)(2,1)}, u32[]{:S(2)}) copy-start(bf16[2048]{0:T(1024)(128)(2,1)} %param.23) | copy-start | bytes 12292
  55.9 8.8 %copy-start.13 = (bf16[256]{0:T(256)(128)(2,1)S(1)}, bf16[256]{0:T(256)(128)(2,1)}, u32[]{:S(2)}) copy-start(bf16[256]{0:T(256)(128)(2,1)} %param.24) | copy-start | bytes 1540
  55.9 9.3 %copy-start.14 = (bf16[256]{0:T(256)(128)(2,1)S(1)}, bf16[256]{0:T(256)(128)(2,1)}, u32[]{:S(2)}) copy-start(bf16[256]{0:T(256)(128)(2,1)} %param.25) | copy-start | bytes 1540
  55.9 10.0 %copy-start.2 = (bf16[16,32,2,256]{3,2,1,0:T(2,128)(2,1)S(1)}, bf16[16,32,2,256]{3,2,1,0:T(2,128)(2,1)}, u32[]{:S(2)}) copy-start(bf16[16,32,2,256]{3,2,1,0:T(2,128)(2,1)} %param.15) | copy-start | bytes 1572868
  58.1 35.7 %all-to-all-start.1 = ((f32[64,1,4224]{2,1,0:T(1,128)}), f32[64,1,4224]{2,1,0:T(1,128)}, u32[]{:S(2)}, u32[]{:S(2)}) async-start(f32[64,1,4224]{2,1,0:T(1,128)} %copy.48), calls=%async_computation.1 | async-start | bytes 2162688 | tf_op jit(solution)/shard_map/all_to_all | solution.py:98
  64.6 32.5 %copy-start.8 = (f32[16]{0:T(128)}, f32[16]{0:T(128)S(1)}, u32[]{:S(2)}) copy-start(f32[16]{0:T(128)S(1)} %convert_element_type.106) | copy-start | bytes 196
  103.1 28.3 %copy-start.3 = (bf16[16,2048]{1,0:T(8,128)(2,1)S(1)}, bf16[16,2048]{1,0:T(8,128)(2,1)}, u32[]{:S(2)}) copy-start(bf16[16,2048]{1,0:T(8,128)(2,1)} %param.21) | copy-start | bytes 196612
  103.1 29.1 %copy-start.10 = (f32[256]{0:T(256)S(1)}, f32[256]{0:T(256)}, u32[]{:S(2)}) copy-start(f32[256]{0:T(256)} %convert_element_type.119) | copy-start | bytes 3076
  103.1 29.1 %copy-start.11 = (f32[256]{0:T(256)S(1)}, f32[256]{0:T(256)}, u32[]{:S(2)}) copy-start(f32[256]{0:T(256)} %convert_element_type.120) | copy-start | bytes 3076

commit v3 on v2

--- a/solution.py
+++ b/solution.py
@@ -48,7 +48,7 @@
     n_req = lax.axis_size("req")
     assert group_count == n_req
 
-    copies = jnp.broadcast_to(queries.reshape(1, row_count * feat_width), (n_req, row_count * feat_width))
+    copies = jnp.broadcast_to(queries[None], (n_req, row_count, feat_width))
     everyone = lax.all_to_all(copies, "req", 0, 0, tiled=True)
     by_group = everyone.reshape(group_count, row_count, heads_here, HEAD)
     safe_group = jnp.clip(page_group, 0, group_count - 1)
@@ -69,7 +69,8 @@
     member = (page_group[:, None] == jnp.arange(group_count)[None, :]) & (page_group[:, None] >= 0)
     page_top = scores.max(-1)
     local_top = jnp.where(member[:, :, None, None], page_top[:, None], masked_score).max(0)
-    page_ref = local_top[safe_group]
+    local_top = local_top.astype(jnp.bfloat16)
+    page_ref = local_top.astype(f32)[safe_group]
     weights = jnp.where(usable[:, None, None, :], jnp.exp(scores - page_ref[..., None]), 0.0)
     page_totals = weights.sum(-1)
     upper_part, lower_part = split_halves(weights)
@@ -85,25 +86,34 @@
         member.T.astype(f32), page_totals.reshape(page_count, -1), precision=highest
     )
     stats_width = row_count * heads_here
-    pad_width = (-(group_accum.shape[1] + 2 * stats_width)) % 128
+    totals_upper, totals_lower = split_halves(group_totals)
+    stats = jnp.concatenate(
+        [
+            local_top.reshape(group_count, stats_width),
+            totals_upper,
+            totals_lower,
+        ],
+        axis=1,
+    )
+    lanes = 128
+    accum_rows = group_accum.shape[1] // lanes
+    stats = jnp.pad(stats, ((0, 0), (0, lanes - stats.shape[1])))
     packed = jnp.concatenate(
         [
-            group_accum,
-            local_top.reshape(group_count, stats_width),
-            group_totals,
-            jnp.zeros((group_count, pad_width), f32),
+            group_accum.astype(jnp.bfloat16).reshape(group_count, accum_rows, lanes),
+            stats[:, None, :],
+            jnp.zeros((group_count, 7, lanes), jnp.bfloat16),
         ],
         axis=1,
     )
     arrived = lax.all_to_all(packed, "req", 0, 0, tiled=True)
-    accum_width = row_count * feat_width
-    part_accum = arrived[:, :accum_width].reshape(n_req, row_count, heads_here, HEAD)
-    part_top = arrived[:, accum_width : accum_width + stats_width].reshape(
-        n_req, row_count, heads_here
-    )
-    part_totals = arrived[:, accum_width + stats_width : accum_width + 2 * stats_width].reshape(
-        n_req, row_count, heads_here
-    )
+    part_accum = arrived[:, :accum_rows].astype(f32).reshape(n_req, row_count, heads_here, HEAD)
+    arrived_stats = arrived[:, accum_rows].astype(f32)
+    part_top = arrived_stats[:, :stats_width].reshape(n_req, row_count, heads_here)
+    part_totals = (
+        arrived_stats[:, stats_width : 2 * stats_width]
+        + arrived_stats[:, 2 * stats_width : 3 * stats_width]
+    ).reshape(n_req, row_count, heads_here)
 
     home_queries = queries.reshape(row_count, heads_here, HEAD)
     tail_keys = tail_cache[:, :, 0].reshape(row_count, tail_slots, heads_here, HEAD)

time: 134 us -> 99.6 us (0.74)
  local copies, waits for them, and re-layouts: 33.5 us -> 20.1 us
  other arithmetic: 15.2 us -> 4.34 us
  waiting for transfers between devices: 30.1 us -> 22.1 us
    all_to_all x1, waiting for transfers between devices: 25.3 us -> 17.5 us  [local(): arrived = lax.all_to_all(packed, 'req', 0, 0, tiled=True)]
    unnamed x33 -> x25, local copies, waits for them, and re-layouts: 5.69 us -> 0.16 us
    all_to_all x2 -> x0, local copies, waits for them, and re-layouts: 5.25 us -> none  [local(): arrived = lax.all_to_all(packed, 'req', 0, 0, tiled=True)]
    all_to_all x1 -> x0, other arithmetic: 3.97 us -> none  [local(): everyone = lax.all_to_all(copies, 'req', 0, 0, tiled=True)]
    broadcast_in_dim x1, other arithmetic: 3.94 us -> 0.01 us  [local(): stats[:, None, :]]
    reshape x2 -> x1, local copies, waits for them, and re-layouts: 1.48 us -> 0.09 us  [local(): by_group = everyone.reshape(group_count, row_count, heads_here, HEAD)]
  transfers between devices with their start and end apart: 2 -> 2, of which waited for: 2 -> 2; matrix products, arithmetic and copies ran while one was open for 13% -> 16% of each run, Pallas kernels for 0% -> 0%
where the time goes in v3:
time: 99.6 us; the launch traced here: 99.2 us
  blocking collectives  27.2 us (27%)
  waiting for transfers between devices  22.1 us (22%)
  local copies, waits for them, and re-layouts  20.1 us (20%)
  starting transfers between devices  19.7 us (20%)
  matrix products  4.76 us (5%)
  other arithmetic  4.34 us (4%)
  between operations  1.07 us (1%)
    all_gather x1, blocking collectives, local(): lax.all_gather(partial_value.astype(jnp.bfloat16), 'tp', axis=0, tiled=Fa...  27.2 us
    all_to_all x1, waiting for transfers between devices, local(): arrived = lax.all_to_all(packed, 'req', 0, 0, tiled=True)  17.5 us
    all_to_all x1, starting transfers between devices, local(): everyone = lax.all_to_all(copies, 'req', 0, 0, tiled=True)  13.8 us
    slice x1, local copies, waits for them, and re-layouts, local(): pool_cache[:, :, 1].reshape(page_count, PAGE, heads_here, HEAD)  11.7 us
    all_to_all x1, starting transfers between devices, local(): arrived = lax.all_to_all(packed, 'req', 0, 0, tiled=True)  5.87 us
    all_to_all x1, waiting for transfers between devices, local(): everyone = lax.all_to_all(copies, 'req', 0, 0, tiled=True)  4.66 us
    slice x1, local copies, waits for them, and re-layouts, local(): tail_cache[:, :, 1].reshape(row_count, tail_slots, heads_here, HEAD)  2.17 us
  transfers between devices with their start and end apart: 2, of which 2 were waited for; matrix products, arithmetic and copies ran while one was open for 16% of the time, Pallas kernels for 0%

profile of v3, /device:TPU:6, one launch (start us, length us, event | category | flops | bytes accessed | tf_op | source)
XLA Modules:
  0.0 99.2 jit_solution(16368545176154953651)
XLA Ops:
  0.7 1.6 %broadcast_in_dim.63 = bf16[64,16,256]{2,1,0:T(8,128)(2,1)} broadcast(bf16[16,256]{1,0:T(8,128)(2,1)} %param.13), dimensions={1,2} | broadcast | bytes 532480 | tf_op jit(solution)/shard_map/broadcast_in_dim | solution.py:51
  2.3 13.8 %all-to-all-start = ((bf16[64,16,256]{2,1,0:T(8,128)(2,1)}), bf16[64,16,256]{2,1,0:T(8,128)(2,1)S(1)}, u32[]{:S(2)}, u32[]{:S(2)}) async-start(bf16[64,16,256]{2,1,0:T(8,128)(2,1)} %broadcast_in_dim.63), calls=%async_computation | async-start | bytes 1048576 | tf_op jit(solution)/shard_map/all_to_all | solution.py:52
  16.2 0.7 gather_fusion
  17.0 0.1 fusion.41
  17.4 11.7 %slice_reduce_fusion = (bf16[32,64,256]{2,1,0:T(8,128)(2,1)S(1)}, bf16[32,64,256]{2,1,0:T(8,128)(2,1)}) fusion(bf16[32,64,2,256]{3,2,1,0:T(2,128)(2,1)} %param.17), kind=kLoop, calls=%fused_computation.6 | loop fusion | bytes 4194304 | tf_op jit(solution)/shard_map/slice | solution.py:57
  29.1 4.7 %all-to-all-done = bf16[64,16,256]{2,1,0:T(8,128)(2,1)S(1)} async-done(((bf16[64,16,256]{2,1,0:T(8,128)(2,1)}), bf16[64,16,256]{2,1,0:T(8,128)(2,1)S(1)}, u32[]{:S(2)}, u32[]{:S(2)}) %all-to-all-start) | async-done | bytes 524320 | tf_op jit(solution)/shard_map/all_to_all | solution.py:52
  33.7 0.1 copy_bitcast_fusion
  33.8 0.6 gather_fusion.1
  34.4 2.0 %fusion.57 = (bf16[32,16,2]{1,2,0:T(2,128)(2,1)S(1)}, f32[32,16,2,64]{3,1,2,0:T(8,128)S(1)}) fusion(f32[32,2,64]{2,1,0:T(2,128)S(1)} %broadcast_multiply_fusion, bf16[32,16,2,128]{3,1,2,0:T(8,128)(2,1)S(1)} %gather_fusion.1, pred[32,64]{1,0:T(8,128)(4,1)S(1)} %get-tuple-element.22, bf16[32,64,256]{2,1,0:T(8,128)(2,1)} %get-tuple-element.3), kind=kOutput, calls=%fused_computation.108 | convolution fusion | flops 17038336 | bytes 1593344 | tf_op jit(solution)/shard_map/pqhd,pshd->pqhs/dot_general | solution.py:63
  36.4 0.2 select_reduce_fusion
  36.6 0.1 copy.67
  36.7 0.6 gather_fusion.2
  37.4 0.4 fusion.14
  37.8 0.4 fusion.7
  38.2 0.5 fusion.1
  38.7 0.3 copy.70
  38.9 0.4 reshape.260
  39.4 0.4 fusion.55
  39.8 0.4 fusion.4
  40.2 0.1 copy.97
  40.4 0.2 fusion.58
  40.7 0.1 copy.73
  40.8 1.0 %maximum_maximum_fusion = bf16[64,40,128]{2,1,0:T(8,128)(2,1)} fusion(bf16[64,1,128]{2,1,0:T(2,128)(2,1)S(1)} %copy.73, bf16[64,32,128]{2,1,0:T(8,128)(2,1)S(1)} %bitcast.93, bf16[40]{0:T(256)(128)(2,1)S(1)} %pad.7.clone), kind=kLoop, calls=%fused_computation.24 | loop fusion | flops 1966080 | bytes 1196112 | tf_op jit(solution)/shard_map/concatenate | solution.py:101
  41.9 5.9 %all-to-all-start.1 = ((bf16[64,40,128]{2,1,0:T(8,128)(2,1)}), bf16[64,40,128]{2,1,0:T(8,128)(2,1)S(1)}, u32[]{:S(2)}, u32[]{:S(2)}) async-start(bf16[64,40,128]{2,1,0:T(8,128)(2,1)} %maximum_maximum_fusion), calls=%async_computation.1 | async-start | bytes 1310720 | tf_op jit(solution)/shard_map/all_to_all | solution.py:109
  47.8 0.1 fusion.35
  48.2 2.2 %slice_reduce_fusion.2 = (bf16[16,32,256]{2,1,0:T(8,128)(2,1)S(1)}, bf16[16,32,256]{2,1,0:T(8,128)(2,1)S(1)}) fusion(bf16[16,32,2,256]{3,2,1,0:T(2,128)(2,1)S(1)} %copy-done.2), kind=kLoop, calls=%fused_computation.26 | loop fusion | bytes 1048576 | tf_op jit(solution)/shard_map/slice | solution.py:120
  50.3 0.2 fusion.19
  50.6 0.1 fusion.49
  50.7 17.5 %all-to-all-done.1 = bf16[64,40,128]{2,1,0:T(8,128)(2,1)S(1)} async-done(((bf16[64,40,128]{2,1,0:T(8,128)(2,1)}), bf16[64,40,128]{2,1,0:T(8,128)(2,1)S(1)}, u32[]{:S(2)}, u32[]{:S(2)}) %all-to-all-start.1) | async-done | bytes 655392 | tf_op jit(solution)/shard_map/all_to_all | solution.py:109
  68.2 0.1 reduce_max.42
  68.3 0.1 copy.74
  68.4 0.1 fusion.45
  68.5 0.1 copy.75
  68.6 0.2 fusion.44
  68.8 0.1 sub.78
  68.9 0.1 fusion.34
  69.0 0.1 copy.77
  69.2 0.1 copy.76
  69.3 0.1 copy.78
  69.4 0.2 fusion.15
  69.6 0.2 fusion.17
  69.8 0.3 multiply_reduce_fusion
  70.1 0.1 fusion.43
  70.2 0.2 convolution_convert_fusion
  70.5 27.2 %all-gather = bf16[128,2048]{1,0:T(8,128)(2,1)S(1)} all-gather(bf16[16,2048]{1,0:T(8,128)(2,1)S(1)} %convolution_convert_fusion), channel_id=2, replica_groups=mesh['req'=64,'tp'=8] {'tp'}, dimensions={0}, use_global_device_ids=true | all-gather | bytes 589824 | tf_op jit(solution)/shard_map/all_gather | solution.py:154
  97.7 0.2 fusion.51
  97.9 0.6 constant_dynamic-slice_fusion
  98.5 0.7 add_convert_fusion.1
  (57 shorter events, 1.2 us)
Async XLA Ops:
  0.6 69.6 %copy-start = (bf16[256,2048]{1,0:T(8,128)(2,1)S(1)}, bf16[256,2048]{1,0:T(8,128)(2,1)}, u32[]{:S(2)}) copy-start(bf16[256,2048]{1,0:T(8,128)(2,1)} %param.22) | copy-start | bytes 3145732
  0.6 16.5 %copy-start.4 = (bf16[16,256]{1,0:T(8,128)(2,1)S(1)}, bf16[16,256]{1,0:T(8,128)(2,1)}, u32[]{:S(2)}) copy-start(bf16[16,256]{1,0:T(8,128)(2,1)} %param.13) | copy-start | bytes 24580
  0.7 15.5 %copy-start.6 = (s32[32]{0:T(128)S(1)}, s32[32]{0:T(128)}, u32[]{:S(2)}) copy-start(s32[32]{0:T(128)} %param.18) | copy-start | bytes 388
  0.7 15.5 %copy-start.1 = (s32[64]{0:T(128)S(1)}, s32[64]{0:T(128)}, u32[]{:S(2)}) copy-start(s32[64]{0:T(128)} %param.20) | copy-start | bytes 772
  0.7 16.2 %copy-start.8 = (s32[32]{0:T(128)S(1)}, s32[32]{0:T(128)}, u32[]{:S(2)}) copy-start(s32[32]{0:T(128)} %param.19) | copy-start | bytes 388
  0.7 16.4 %copy-start.5 = (bf16[16,2,256]{2,1,0:T(2,128)(2,1)S(1)}, bf16[16,2,256]{2,1,0:T(2,128)(2,1)}, u32[]{:S(2)}) copy-start(bf16[16,2,256]{2,1,0:T(2,128)(2,1)} %param.14) | copy-start | bytes 49156
  2.3 31.4 %all-to-all-start = ((bf16[64,16,256]{2,1,0:T(8,128)(2,1)}), bf16[64,16,256]{2,1,0:T(8,128)(2,1)S(1)}, u32[]{:S(2)}, u32[]{:S(2)}) async-start(bf16[64,16,256]{2,1,0:T(8,128)(2,1)} %broadcast_in_dim.63), calls=%async_computation | async-start | bytes 1048576 | tf_op jit(solution)/shard_map/all_to_all | solution.py:52
  40.7 7.3 %copy-start.9 = (s32[16]{0:T(128)S(1)}, s32[16]{0:T(128)}, u32[]{:S(2)}) copy-start(s32[16]{0:T(128)} %param.16) | copy-start | bytes 196
  40.7 7.3 %copy-start.7 = (bf16[2048]{0:T(1024)(128)(2,1)S(1)}, bf16[2048]{0:T(1024)(128)(2,1)}, u32[]{:S(2)}) copy-start(bf16[2048]{0:T(1024)(128)(2,1)} %param.23) | copy-start | bytes 12292
  40.7 7.3 %copy-start.10 = (bf16[256]{0:T(256)(128)(2,1)S(1)}, bf16[256]{0:T(256)(128)(2,1)}, u32[]{:S(2)}) copy-start(bf16[256]{0:T(256)(128)(2,1)} %param.24) | copy-start | bytes 1540
  40.7 7.3 %copy-start.11 = (bf16[256]{0:T(256)(128)(2,1)S(1)}, bf16[256]{0:T(256)(128)(2,1)}, u32[]{:S(2)}) copy-start(bf16[256]{0:T(256)(128)(2,1)} %param.25) | copy-start | bytes 1540
  40.8 7.3 %copy-start.2 = (bf16[16,32,2,256]{3,2,1,0:T(2,128)(2,1)S(1)}, bf16[16,32,2,256]{3,2,1,0:T(2,128)(2,1)}, u32[]{:S(2)}) copy-start(bf16[16,32,2,256]{3,2,1,0:T(2,128)(2,1)} %param.15) | copy-start | bytes 1572868
  41.9 26.3 %all-to-all-start.1 = ((bf16[64,40,128]{2,1,0:T(8,128)(2,1)}), bf16[64,40,128]{2,1,0:T(8,128)(2,1)S(1)}, u32[]{:S(2)}, u32[]{:S(2)}) async-start(bf16[64,40,128]{2,1,0:T(8,128)(2,1)} %maximum_maximum_fusion), calls=%async_computation.1 | async-start | bytes 1310720 | tf_op jit(solution)/shard_map/all_to_all | solution.py:109
  70.1 27.6 %copy-start.3 = (bf16[16,2048]{1,0:T(8,128)(2,1)S(1)}, bf16[16,2048]{1,0:T(8,128)(2,1)}, u32[]{:S(2)}) copy-start(bf16[16,2048]{1,0:T(8,128)(2,1)} %param.21) | copy-start | bytes 196612

commit v4 on v3

--- a/solution.py
+++ b/solution.py
@@ -151,7 +151,11 @@
     partial_value = jnp.dot(attention, out_weight, preferred_element_type=f32)
     model_width = residual.shape[1]
     own_start = lax.axis_index("tp") * feat_width
-    gathered = lax.all_gather(partial_value.astype(jnp.bfloat16), "tp", axis=0, tiled=False)
+    tp_size = lax.axis_size("tp")
+    partial_copies = jnp.broadcast_to(
+        partial_value.astype(jnp.bfloat16)[None], (tp_size,) + partial_value.shape
+    )
+    gathered = lax.all_to_all(partial_copies, "tp", 0, 0, tiled=True)
     projected = gathered.astype(f32).sum(0) + out_bias.astype(f32)[None, :]
     attention_full = projected.astype(jnp.bfloat16)
     hidden = residual.astype(f32) + attention_full.astype(f32)

time: 99.6 us -> 99.1 us (level)
  the two profiles are of different devices: /device:TPU:6 before, /device:TPU:1 now
where the time goes in v4:
time: 99.1 us; the launch traced here: 98.7 us
  waiting for transfers between devices  40.2 us (41%)
  starting transfers between devices  27.4 us (28%)
  local copies, waits for them, and re-layouts  20.9 us (21%)
  matrix products  4.75 us (5%)
  other arithmetic  4.34 us (4%)
  between operations  1.06 us (1%)
    all_to_all x1, waiting for transfers between devices, local(): gathered = lax.all_to_all(partial_copies, 'tp', 0, 0, tiled=True)  17.9 us
    all_to_all x1, waiting for transfers between devices, local(): arrived = lax.all_to_all(packed, 'req', 0, 0, tiled=True)  17.5 us
    all_to_all x1, starting transfers between devices, local(): everyone = lax.all_to_all(copies, 'req', 0, 0, tiled=True)  14.8 us
    slice x1, local copies, waits for them, and re-layouts, local(): pool_cache[:, :, 1].reshape(page_count, PAGE, heads_here, HEAD)  11.7 us
    all_to_all x1, starting transfers between devices, local(): gathered = lax.all_to_all(partial_copies, 'tp', 0, 0, tiled=True)  6.82 us
    all_to_all x1, starting transfers between devices, local(): arrived = lax.all_to_all(packed, 'req', 0, 0, tiled=True)  5.73 us
    all_to_all x1, waiting for transfers between devices, local(): everyone = lax.all_to_all(copies, 'req', 0, 0, tiled=True)  4.8 us
    slice x1, local copies, waits for them, and re-layouts, local(): tail_cache[:, :, 1].reshape(row_count, tail_slots, heads_here, HEAD)  2.17 us
  transfers between devices with their start and end apart: 3, of which 3 were waited for; matrix products, arithmetic and copies ran while one was open for 16% of the time, Pallas kernels for 0%

profile of v4, /device:TPU:1, one launch (start us, length us, event | category | flops | bytes accessed | tf_op | source)
XLA Modules:
  0.0 98.7 jit_solution(9838720075037861736)
XLA Ops:
  0.7 1.6 %broadcast_in_dim.65 = bf16[64,16,256]{2,1,0:T(8,128)(2,1)} broadcast(bf16[16,256]{1,0:T(8,128)(2,1)} %param.13), dimensions={1,2} | broadcast | bytes 532480 | tf_op jit(solution)/shard_map/broadcast_in_dim | solution.py:51
  2.3 14.8 %all-to-all-start = ((bf16[64,16,256]{2,1,0:T(8,128)(2,1)}), bf16[64,16,256]{2,1,0:T(8,128)(2,1)S(1)}, u32[]{:S(2)}, u32[]{:S(2)}) async-start(bf16[64,16,256]{2,1,0:T(8,128)(2,1)} %broadcast_in_dim.65), calls=%async_computation | async-start | bytes 1048576 | tf_op jit(solution)/shard_map/all_to_all | solution.py:52
  17.2 0.7 gather_fusion
  18.0 0.1 fusion.41
  18.4 11.7 %slice_reduce_fusion = (bf16[32,64,256]{2,1,0:T(8,128)(2,1)S(1)}, bf16[32,64,256]{2,1,0:T(8,128)(2,1)}) fusion(bf16[32,64,2,256]{3,2,1,0:T(2,128)(2,1)} %param.17), kind=kLoop, calls=%fused_computation.6 | loop fusion | bytes 4194304 | tf_op jit(solution)/shard_map/slice | solution.py:57
  30.1 4.8 %all-to-all-done = bf16[64,16,256]{2,1,0:T(8,128)(2,1)S(1)} async-done(((bf16[64,16,256]{2,1,0:T(8,128)(2,1)}), bf16[64,16,256]{2,1,0:T(8,128)(2,1)S(1)}, u32[]{:S(2)}, u32[]{:S(2)}) %all-to-all-start) | async-done | bytes 524320 | tf_op jit(solution)/shard_map/all_to_all | solution.py:52
  34.9 0.1 copy_bitcast_fusion
  35.0 0.6 gather_fusion.1
  35.6 2.0 %fusion.57 = (bf16[32,16,2]{1,2,0:T(2,128)(2,1)S(1)}, f32[32,16,2,64]{3,1,2,0:T(8,128)S(1)}) fusion(f32[32,2,64]{2,1,0:T(2,128)S(1)} %broadcast_multiply_fusion, bf16[32,16,2,128]{3,1,2,0:T(8,128)(2,1)S(1)} %gather_fusion.1, pred[32,64]{1,0:T(8,128)(4,1)S(1)} %get-tuple-element.22, bf16[32,64,256]{2,1,0:T(8,128)(2,1)} %get-tuple-element.3), kind=kOutput, calls=%fused_computation.108 | convolution fusion | flops 17038336 | bytes 1593344 | tf_op jit(solution)/shard_map/pqhd,pshd->pqhs/dot_general | solution.py:63
  37.6 0.2 select_reduce_fusion
  37.8 0.1 copy.67
  37.9 0.6 gather_fusion.2
  38.5 0.4 fusion.14
  39.0 0.4 fusion.7
  39.3 0.5 fusion.1
  39.8 0.3 copy.70
  40.1 0.4 reshape.261
  40.6 0.4 fusion.55
  41.0 0.4 fusion.4
  41.4 0.1 copy.97
  41.6 0.2 fusion.58
  41.9 0.1 copy.73
  42.0 1.0 %maximum_maximum_fusion = bf16[64,40,128]{2,1,0:T(8,128)(2,1)} fusion(bf16[64,1,128]{2,1,0:T(2,128)(2,1)S(1)} %copy.73, bf16[64,32,128]{2,1,0:T(8,128)(2,1)S(1)} %bitcast.90, bf16[40]{0:T(256)(128)(2,1)S(1)} %pad.7.clone), kind=kLoop, calls=%fused_computation.24 | loop fusion | flops 1966080 | bytes 1196112 | tf_op jit(solution)/shard_map/concatenate | solution.py:101
  43.0 5.7 %all-to-all-start.1 = ((bf16[64,40,128]{2,1,0:T(8,128)(2,1)}), bf16[64,40,128]{2,1,0:T(8,128)(2,1)S(1)}, u32[]{:S(2)}, u32[]{:S(2)}) async-start(bf16[64,40,128]{2,1,0:T(8,128)(2,1)} %maximum_maximum_fusion), calls=%async_computation.1 | async-start | bytes 1310720 | tf_op jit(solution)/shard_map/all_to_all | solution.py:109
  48.7 0.1 fusion.35
  49.1 2.2 %slice_reduce_fusion.2 = (bf16[16,32,256]{2,1,0:T(8,128)(2,1)S(1)}, bf16[16,32,256]{2,1,0:T(8,128)(2,1)S(1)}) fusion(bf16[16,32,2,256]{3,2,1,0:T(2,128)(2,1)S(1)} %copy-done.2), kind=kLoop, calls=%fused_computation.26 | loop fusion | bytes 1048576 | tf_op jit(solution)/shard_map/slice | solution.py:120
  51.3 0.2 fusion.19
  51.5 0.1 fusion.49
  51.6 17.5 %all-to-all-done.1 = bf16[64,40,128]{2,1,0:T(8,128)(2,1)S(1)} async-done(((bf16[64,40,128]{2,1,0:T(8,128)(2,1)}), bf16[64,40,128]{2,1,0:T(8,128)(2,1)S(1)}, u32[]{:S(2)}, u32[]{:S(2)}) %all-to-all-start.1) | async-done | bytes 655392 | tf_op jit(solution)/shard_map/all_to_all | solution.py:109
  69.2 0.1 copy.74
  69.4 0.1 fusion.45
  69.5 0.1 copy.75
  69.6 0.2 fusion.44
  69.7 0.1 sub.78
  69.8 0.1 fusion.34
  70.0 0.1 copy.77
  70.2 0.1 copy.76
  70.3 0.2 fusion.15
  70.5 0.2 fusion.17
  70.7 0.3 multiply_reduce_fusion
  71.1 0.1 fusion.43
  71.2 0.2 convolution_convert_fusion
  71.5 0.8 broadcast_in_dim.119
  72.3 6.8 %all-to-all-start.2 = ((bf16[8,16,2048]{2,1,0:T(8,128)(2,1)}), bf16[8,16,2048]{2,1,0:T(8,128)(2,1)S(1)}, u32[]{:S(2)}, u32[]{:S(2)}) async-start(bf16[8,16,2048]{2,1,0:T(8,128)(2,1)} %broadcast_in_dim.119), calls=%async_computation.2 | async-start | bytes 1048576 | tf_op jit(solution)/shard_map/all_to_all | solution.py:158
  79.2 17.9 %all-to-all-done.2 = bf16[8,16,2048]{2,1,0:T(8,128)(2,1)S(1)} async-done(((bf16[8,16,2048]{2,1,0:T(8,128)(2,1)}), bf16[8,16,2048]{2,1,0:T(8,128)(2,1)S(1)}, u32[]{:S(2)}, u32[]{:S(2)}) %all-to-all-start.2) | async-done | bytes 524320 | tf_op jit(solution)/shard_map/all_to_all | solution.py:158
  97.2 0.2 fusion.51
  97.4 0.6 constant_dynamic-slice_fusion
  98.0 0.7 add_convert_fusion.1
  (59 shorter events, 1.3 us)
Async XLA Ops:
  0.6 70.6 %copy-start = (bf16[256,2048]{1,0:T(8,128)(2,1)S(1)}, bf16[256,2048]{1,0:T(8,128)(2,1)}, u32[]{:S(2)}) copy-start(bf16[256,2048]{1,0:T(8,128)(2,1)} %param.22) | copy-start | bytes 3145732
  0.6 17.6 %copy-start.4 = (bf16[16,256]{1,0:T(8,128)(2,1)S(1)}, bf16[16,256]{1,0:T(8,128)(2,1)}, u32[]{:S(2)}) copy-start(bf16[16,256]{1,0:T(8,128)(2,1)} %param.13) | copy-start | bytes 24580
  0.7 16.5 %copy-start.6 = (s32[32]{0:T(128)S(1)}, s32[32]{0:T(128)}, u32[]{:S(2)}) copy-start(s32[32]{0:T(128)} %param.18) | copy-start | bytes 388
  0.7 16.6 %copy-start.1 = (s32[64]{0:T(128)S(1)}, s32[64]{0:T(128)}, u32[]{:S(2)}) copy-start(s32[64]{0:T(128)} %param.20) | copy-start | bytes 772
  0.7 17.3 %copy-start.8 = (s32[32]{0:T(128)S(1)}, s32[32]{0:T(128)}, u32[]{:S(2)}) copy-start(s32[32]{0:T(128)} %param.19) | copy-start | bytes 388
  0.7 17.4 %copy-start.5 = (bf16[16,2,256]{2,1,0:T(2,128)(2,1)S(1)}, bf16[16,2,256]{2,1,0:T(2,128)(2,1)}, u32[]{:S(2)}) copy-start(bf16[16,2,256]{2,1,0:T(2,128)(2,1)} %param.14) | copy-start | bytes 49156
  2.3 32.6 %all-to-all-start = ((bf16[64,16,256]{2,1,0:T(8,128)(2,1)}), bf16[64,16,256]{2,1,0:T(8,128)(2,1)S(1)}, u32[]{:S(2)}, u32[]{:S(2)}) async-start(bf16[64,16,256]{2,1,0:T(8,128)(2,1)} %broadcast_in_dim.65), calls=%async_computation | async-start | bytes 1048576 | tf_op jit(solution)/shard_map/all_to_all | solution.py:52
  41.8 7.1 %copy-start.9 = (s32[16]{0:T(128)S(1)}, s32[16]{0:T(128)}, u32[]{:S(2)}) copy-start(s32[16]{0:T(128)} %param.16) | copy-start | bytes 196
  41.8 7.2 %copy-start.2 = (bf16[16,32,2,256]{3,2,1,0:T(2,128)(2,1)S(1)}, bf16[16,32,2,256]{3,2,1,0:T(2,128)(2,1)}, u32[]{:S(2)}) copy-start(bf16[16,32,2,256]{3,2,1,0:T(2,128)(2,1)} %param.15) | copy-start | bytes 1572868
  43.0 26.1 %all-to-all-start.1 = ((bf16[64,40,128]{2,1,0:T(8,128)(2,1)}), bf16[64,40,128]{2,1,0:T(8,128)(2,1)S(1)}, u32[]{:S(2)}, u32[]{:S(2)}) async-start(bf16[64,40,128]{2,1,0:T(8,128)(2,1)} %maximum_maximum_fusion), calls=%async_computation.1 | async-start | bytes 1310720 | tf_op jit(solution)/shard_map/all_to_all | solution.py:109
  71.2 8.0 %copy-start.7 = (bf16[2048]{0:T(1024)(128)(2,1)S(1)}, bf16[2048]{0:T(1024)(128)(2,1)}, u32[]{:S(2)}) copy-start(bf16[2048]{0:T(1024)(128)(2,1)} %param.23) | copy-start | bytes 12292
  71.2 8.0 %copy-start.10 = (bf16[256]{0:T(256)(128)(2,1)S(1)}, bf16[256]{0:T(256)(128)(2,1)}, u32[]{:S(2)}) copy-start(bf16[256]{0:T(256)(128)(2,1)} %param.24) | copy-start | bytes 1540
  71.2 8.0 %copy-start.11 = (bf16[256]{0:T(256)(128)(2,1)S(1)}, bf16[256]{0:T(256)(128)(2,1)}, u32[]{:S(2)}) copy-start(bf16[256]{0:T(256)(128)(2,1)} %param.25) | copy-start | bytes 1540
  71.5 25.7 %copy-start.3 = (bf16[16,2048]{1,0:T(8,128)(2,1)S(1)}, bf16[16,2048]{1,0:T(8,128)(2,1)}, u32[]{:S(2)}) copy-start(bf16[16,2048]{1,0:T(8,128)(2,1)} %param.21) | copy-start | bytes 196612
  72.3 24.8 %all-to-all-start.2 = ((bf16[8,16,2048]{2,1,0:T(8,128)(2,1)}), bf16[8,16,2048]{2,1,0:T(8,128)(2,1)S(1)}, u32[]{:S(2)}, u32[]{:S(2)}) async-start(bf16[8,16,2048]{2,1,0:T(8,128)(2,1)} %broadcast_in_dim.119), calls=%async_computation.2 | async-start | bytes 1048576 | tf_op jit(solution)/shard_map/all_to_all | solution.py:158

commit v5 on v4

--- a/solution.py
+++ b/solution.py
@@ -102,7 +102,6 @@
         [
             group_accum.astype(jnp.bfloat16).reshape(group_count, accum_rows, lanes),
             stats[:, None, :],
-            jnp.zeros((group_count, 7, lanes), jnp.bfloat16),
         ],
         axis=1,
     )

time: 99.1 us -> 101 us (1.019)
  starting transfers between devices: 27.4 us -> 29.9 us
  waiting for transfers between devices: 40.2 us -> 37.7 us
  local copies, waits for them, and re-layouts: 20.9 us -> 22.2 us
  other arithmetic: 4.34 us -> 5.5 us
    all_to_all x1, waiting for transfers between devices: 4.8 us -> 2.08 us  [local(): everyone = lax.all_to_all(copies, 'req', 0, 0, tiled=True)]
    all_to_all x1, starting transfers between devices: 5.73 us -> 8.22 us  [local(): arrived = lax.all_to_all(packed, 'req', 0, 0, tiled=True)]
  transfers between devices with their start and end apart: 3 -> 3, of which waited for: 3 -> 3; matrix products, arithmetic and copies ran while one was open for 16% -> 18% of each run, Pallas kernels for 0% -> 0%
where the time goes in v5:
time: 101 us
  waiting for transfers between devices  37.7 us (37%)
  starting transfers between devices  29.9 us (30%)
  local copies, waits for them, and re-layouts  22.2 us (22%)
  other arithmetic  5.5 us (5%)
  matrix products  4.75 us (5%)
  between operations  1.01 us (1%)
    all_to_all x1, waiting for transfers between devices, local(): gathered = lax.all_to_all(partial_copies, 'tp', 0, 0, tiled=True)  17.9 us
    all_to_all x1, waiting for transfers between devices, local(): arrived = lax.all_to_all(packed, 'req', 0, 0, tiled=True)  17.7 us
    all_to_all x1, starting transfers between devices, local(): everyone = lax.all_to_all(copies, 'req', 0, 0, tiled=True)  14.8 us
    slice x1, local copies, waits for them, and re-layouts, local(): pool_cache[:, :, 1].reshape(page_count, PAGE, heads_here, HEAD)  11.7 us
    all_to_all x1, starting transfers between devices, local(): arrived = lax.all_to_all(packed, 'req', 0, 0, tiled=True)  8.22 us
    all_to_all x1, starting transfers between devices, local(): gathered = lax.all_to_all(partial_copies, 'tp', 0, 0, tiled=True)  6.82 us
    slice x1, local copies, waits for them, and re-layouts, local(): tail_cache[:, :, 1].reshape(row_count, tail_slots, heads_here, HEAD)  2.17 us
    all_to_all x1, waiting for transfers between devices, local(): everyone = lax.all_to_all(copies, 'req', 0, 0, tiled=True)  2.08 us
  transfers between devices with their start and end apart: 3, of which 3 were waited for; matrix products, arithmetic and copies ran while one was open for 18% of the time, Pallas kernels for 0%

profile of v5, /device:TPU:1, one launch (start us, length us, event | category | flops | bytes accessed | tf_op | source)
XLA Modules:
  0.0 101.0 jit_solution(8675872332990475137)
XLA Ops:
  0.7 1.6 %broadcast_in_dim.63 = bf16[64,16,256]{2,1,0:T(8,128)(2,1)} broadcast(bf16[16,256]{1,0:T(8,128)(2,1)} %param.13), dimensions={1,2} | broadcast | bytes 532480 | tf_op jit(solution)/shard_map/broadcast_in_dim | solution.py:51
  2.3 14.8 %all-to-all-start = ((bf16[64,16,256]{2,1,0:T(8,128)(2,1)}), bf16[64,16,256]{2,1,0:T(8,128)(2,1)S(1)}, u32[]{:S(2)}, u32[]{:S(2)}) async-start(bf16[64,16,256]{2,1,0:T(8,128)(2,1)} %broadcast_in_dim.63), calls=%async_computation | async-start | bytes 1048576 | tf_op jit(solution)/shard_map/all_to_all | solution.py:52
  17.2 0.7 compare_select_fusion
  17.8 0.7 broadcast_compare_fusion
  18.5 0.7 reshape.264
  19.2 1.4 %gather_fusion = s32[32]{0:T(128)S(1)} fusion(s32[64]{0:T(128)} %param.20, s32[1024]{0:T(1024)S(1)} %pad_clamp_fusion), kind=kCustom, calls=%fused_computation | custom fusion | bytes 384 | tf_op jit(solution)/shard_map/gather | solution.py:58
  20.6 0.1 fusion.41
  20.8 0.1 fusion.35
  21.1 11.7 %slice_reduce_fusion = (bf16[32,64,256]{2,1,0:T(8,128)(2,1)S(1)}, bf16[32,64,256]{2,1,0:T(8,128)(2,1)}) fusion(bf16[32,64,2,256]{3,2,1,0:T(2,128)(2,1)} %param.17), kind=kLoop, calls=%fused_computation.6 | loop fusion | bytes 4194304 | tf_op jit(solution)/shard_map/slice | solution.py:57
  32.8 2.1 %all-to-all-done = bf16[64,16,256]{2,1,0:T(8,128)(2,1)S(1)} async-done(((bf16[64,16,256]{2,1,0:T(8,128)(2,1)}), bf16[64,16,256]{2,1,0:T(8,128)(2,1)S(1)}, u32[]{:S(2)}, u32[]{:S(2)}) %all-to-all-start) | async-done | bytes 524320 | tf_op jit(solution)/shard_map/all_to_all | solution.py:52
  34.9 0.1 copy_bitcast_fusion
  35.0 0.6 gather_fusion.1
  35.6 2.0 %fusion.57 = (bf16[32,16,2]{1,2,0:T(2,128)(2,1)S(1)}, f32[32,16,2,64]{3,1,2,0:T(8,128)S(1)}) fusion(f32[32,2,64]{2,1,0:T(2,128)S(1)} %broadcast_multiply_fusion, bf16[32,16,2,128]{3,1,2,0:T(8,128)(2,1)S(1)} %gather_fusion.1, pred[32,64]{1,0:T(8,128)(4,1)S(1)} %get-tuple-element.22, bf16[32,64,256]{2,1,0:T(8,128)(2,1)} %get-tuple-element.3), kind=kOutput, calls=%fused_computation.108 | convolution fusion | flops 17038336 | bytes 1593344 | tf_op jit(solution)/shard_map/pqhd,pshd->pqhs/dot_general | solution.py:63
  37.6 0.2 select_reduce_fusion
  37.8 0.1 copy.67
  37.9 0.6 gather_fusion.2
  38.5 0.4 fusion.14
  39.0 0.4 fusion.7
  39.4 0.5 fusion.1
  39.8 0.3 copy.70
  40.1 0.4 reshape.261
  40.6 0.4 fusion.55
  41.0 0.4 fusion.4
  41.4 0.1 copy.97
  41.6 0.2 fusion.58
  41.9 0.1 copy.73
  42.0 0.9 pad_maximum_fusion
  42.9 8.2 %all-to-all-start.1 = ((bf16[64,33,128]{2,1,0:T(8,128)(2,1)}), bf16[64,33,128]{2,1,0:T(8,128)(2,1)S(1)}, u32[]{:S(2)}, u32[]{:S(2)}) async-start(bf16[64,33,128]{2,1,0:T(8,128)(2,1)} %pad_maximum_fusion), calls=%async_computation.1 | async-start | bytes 1310720 | tf_op jit(solution)/shard_map/all_to_all | solution.py:108
  51.2 2.2 %slice_reduce_fusion.2 = (bf16[16,32,256]{2,1,0:T(8,128)(2,1)S(1)}, bf16[16,32,256]{2,1,0:T(8,128)(2,1)S(1)}) fusion(bf16[16,32,2,256]{3,2,1,0:T(2,128)(2,1)S(1)} %copy-done.1), kind=kLoop, calls=%fused_computation.26 | loop fusion | bytes 1048576 | tf_op jit(solution)/shard_map/slice | solution.py:119
  53.4 0.2 fusion.19
  53.6 0.1 fusion.49
  53.7 17.7 %all-to-all-done.1 = bf16[64,33,128]{2,1,0:T(8,128)(2,1)S(1)} async-done(((bf16[64,33,128]{2,1,0:T(8,128)(2,1)}), bf16[64,33,128]{2,1,0:T(8,128)(2,1)S(1)}, u32[]{:S(2)}, u32[]{:S(2)}) %all-to-all-start.1) | async-done | bytes 540704 | tf_op jit(solution)/shard_map/all_to_all | solution.py:108
  71.7 0.1 fusion.45
  71.8 0.1 copy.75
  71.9 0.2 fusion.44
  72.1 0.1 sub.78
  72.2 0.1 fusion.34
  72.7 0.2 fusion.15
  72.9 0.2 fusion.17
  73.1 0.3 multiply_reduce_fusion
  73.4 0.1 fusion.43
  73.6 0.2 convolution_convert_fusion
  73.8 0.8 broadcast_in_dim.72
  74.7 6.8 %all-to-all-start.2 = ((bf16[8,16,2048]{2,1,0:T(8,128)(2,1)}), bf16[8,16,2048]{2,1,0:T(8,128)(2,1)S(1)}, u32[]{:S(2)}, u32[]{:S(2)}) async-start(bf16[8,16,2048]{2,1,0:T(8,128)(2,1)} %broadcast_in_dim.72), calls=%async_computation.2 | async-start | bytes 1048576 | tf_op jit(solution)/shard_map/all_to_all | solution.py:157
  81.5 17.9 %all-to-all-done.2 = bf16[8,16,2048]{2,1,0:T(8,128)(2,1)S(1)} async-done(((bf16[8,16,2048]{2,1,0:T(8,128)(2,1)}), bf16[8,16,2048]{2,1,0:T(8,128)(2,1)S(1)}, u32[]{:S(2)}, u32[]{:S(2)}) %all-to-all-start.2) | async-done | bytes 524320 | tf_op jit(solution)/shard_map/all_to_all | solution.py:157
  99.5 0.2 fusion.51
  99.7 0.6 constant_dynamic-slice_fusion
  100.3 0.7 add_convert_fusion.1
  (55 shorter events, 1.5 us)
Async XLA Ops:
  0.6 72.9 %copy-start = (bf16[256,2048]{1,0:T(8,128)(2,1)S(1)}, bf16[256,2048]{1,0:T(8,128)(2,1)}, u32[]{:S(2)}) copy-start(bf16[256,2048]{1,0:T(8,128)(2,1)} %param.22) | copy-start | bytes 3145732
  0.6 20.3 %copy-start.3 = (bf16[16,256]{1,0:T(8,128)(2,1)S(1)}, bf16[16,256]{1,0:T(8,128)(2,1)}, u32[]{:S(2)}) copy-start(bf16[16,256]{1,0:T(8,128)(2,1)} %param.13) | copy-start | bytes 24580
  0.7 20.0 %copy-start.5 = (s32[32]{0:T(128)S(1)}, s32[32]{0:T(128)}, u32[]{:S(2)}) copy-start(s32[32]{0:T(128)} %param.18) | copy-start | bytes 388
  0.7 19.9 %copy-start.7 = (s32[32]{0:T(128)S(1)}, s32[32]{0:T(128)}, u32[]{:S(2)}) copy-start(s32[32]{0:T(128)} %param.19) | copy-start | bytes 388
  0.7 20.1 %copy-start.4 = (bf16[16,2,256]{2,1,0:T(2,128)(2,1)S(1)}, bf16[16,2,256]{2,1,0:T(2,128)(2,1)}, u32[]{:S(2)}) copy-start(bf16[16,2,256]{2,1,0:T(2,128)(2,1)} %param.14) | copy-start | bytes 49156
  0.7 20.4 %copy-start.8 = (s32[16]{0:T(128)S(1)}, s32[16]{0:T(128)}, u32[]{:S(2)}) copy-start(s32[16]{0:T(128)} %param.16) | copy-start | bytes 196
  2.3 32.6 %all-to-all-start = ((bf16[64,16,256]{2,1,0:T(8,128)(2,1)}), bf16[64,16,256]{2,1,0:T(8,128)(2,1)S(1)}, u32[]{:S(2)}, u32[]{:S(2)}) async-start(bf16[64,16,256]{2,1,0:T(8,128)(2,1)} %broadcast_in_dim.63), calls=%async_computation | async-start | bytes 1048576 | tf_op jit(solution)/shard_map/all_to_all | solution.py:52
  41.4 9.8 %copy-start.1 = (bf16[16,32,2,256]{3,2,1,0:T(2,128)(2,1)S(1)}, bf16[16,32,2,256]{3,2,1,0:T(2,128)(2,1)}, u32[]{:S(2)}) copy-start(bf16[16,32,2,256]{3,2,1,0:T(2,128)(2,1)} %param.15) | copy-start | bytes 1572868
  42.9 28.6 %all-to-all-start.1 = ((bf16[64,33,128]{2,1,0:T(8,128)(2,1)}), bf16[64,33,128]{2,1,0:T(8,128)(2,1)S(1)}, u32[]{:S(2)}, u32[]{:S(2)}) async-start(bf16[64,33,128]{2,1,0:T(8,128)(2,1)} %pad_maximum_fusion), calls=%async_computation.1 | async-start | bytes 1310720 | tf_op jit(solution)/shard_map/all_to_all | solution.py:108
  72.3 9.2 %copy-start.6 = (bf16[2048]{0:T(1024)(128)(2,1)S(1)}, bf16[2048]{0:T(1024)(128)(2,1)}, u32[]{:S(2)}) copy-start(bf16[2048]{0:T(1024)(128)(2,1)} %param.23) | copy-start | bytes 12292
  72.3 9.2 %copy-start.9 = (bf16[256]{0:T(256)(128)(2,1)S(1)}, bf16[256]{0:T(256)(128)(2,1)}, u32[]{:S(2)}) copy-start(bf16[256]{0:T(256)(128)(2,1)} %param.24) | copy-start | bytes 1540
  72.3 9.2 %copy-start.10 = (bf16[256]{0:T(256)(128)(2,1)S(1)}, bf16[256]{0:T(256)(128)(2,1)}, u32[]{:S(2)}) copy-start(bf16[256]{0:T(256)(128)(2,1)} %param.25) | copy-start | bytes 1540
  73.1 26.4 %copy-start.2 = (bf16[16,2048]{1,0:T(8,128)(2,1)S(1)}, bf16[16,2048]{1,0:T(8,128)(2,1)}, u32[]{:S(2)}) copy-start(bf16[16,2048]{1,0:T(8,128)(2,1)} %param.21) | copy-start | bytes 196612
  74.7 24.8 %all-to-all-start.2 = ((bf16[8,16,2048]{2,1,0:T(8,128)(2,1)}), bf16[8,16,2048]{2,1,0:T(8,128)(2,1)S(1)}, u32[]{:S(2)}, u32[]{:S(2)}) async-start(bf16[8,16,2048]{2,1,0:T(8,128)(2,1)} %broadcast_in_dim.72), calls=%async_computation.2 | async-start | bytes 1048576 | tf_op jit(solution)/shard_map/all_to_all | solution.py:157

commit v6 on v4

--- a/solution.py
+++ b/solution.py
@@ -73,18 +73,12 @@
     page_ref = local_top.astype(f32)[safe_group]
     weights = jnp.where(usable[:, None, None, :], jnp.exp(scores - page_ref[..., None]), 0.0)
     page_totals = weights.sum(-1)
-    upper_part, lower_part = split_halves(weights)
-    page_accum = jnp.einsum("pqhs,pshd->pqhd", upper_part, page_values, preferred_element_type=f32)
-    page_accum = page_accum + jnp.einsum(
-        "pqhs,pshd->pqhd", lower_part, page_values, preferred_element_type=f32
+    page_accum = jnp.einsum(
+        "pqhs,pshd->pqhd", weights, page_values.astype(f32), precision=highest
     )
-    accum_upper, accum_lower = split_halves(page_accum.reshape(page_count, -1))
-    spread = member.T.astype(jnp.bfloat16)
-    group_accum = jnp.dot(spread, accum_upper, preferred_element_type=f32)
-    group_accum = group_accum + jnp.dot(spread, accum_lower, preferred_element_type=f32)
-    group_totals = jnp.dot(
-        member.T.astype(f32), page_totals.reshape(page_count, -1), precision=highest
-    )
+    member_f = member.T.astype(f32)
+    group_accum = jnp.einsum("gp,pqhd->gqhd", member_f, page_accum, precision=highest)
+    group_totals = jnp.dot(member_f, page_totals.reshape(page_count, -1), precision=highest)
     stats_width = row_count * heads_here
     totals_upper, totals_lower = split_halves(group_totals)
     stats = jnp.concatenate(
@@ -96,7 +90,7 @@
         axis=1,
     )
     lanes = 128
-    accum_rows = group_accum.shape[1] // lanes
+    accum_rows = row_count * feat_width // lanes
     stats = jnp.pad(stats, ((0, 0), (0, lanes - stats.shape[1])))
     packed = jnp.concatenate(
         [

time: 99.1 us -> 101 us (1.019)
  waiting for transfers between devices: 40.2 us -> 41.9 us
  local copies, waits for them, and re-layouts: 20.9 us -> 19.8 us
    slice x1, local copies, waits for them, and re-layouts: 11.7 us -> 9.88 us  [local(): pool_cache[:, :, 1].reshape(page_count, PAGE, heads_here, HEAD)]
    all_to_all x1, waiting for transfers between devices: 4.8 us -> 6.48 us  [local(): everyone = lax.all_to_all(copies, 'req', 0, 0, tiled=True)]
    reduce_sum x0 -> x1, other arithmetic: none -> 1.44 us  [local(): page_totals = weights.sum(-1)]
    reshape x1, local copies, waits for them, and re-layouts: 0.09 us -> 1.13 us  [local(): by_group = everyone.reshape(group_count, row_count, heads_here, HEAD)]
    dot_general x5 -> x3, matrix products: 1.89 us -> 2.13 us  [the longest x1 1 us: local(): jnp.einsum('pqhs,pshd->pqhd', weights, page_values.astype(f32), precision...]
  transfers between devices with their start and end apart: 3 -> 3, of which waited for: 3 -> 3; matrix products, arithmetic and copies ran while one was open for 16% -> 14% of each run, Pallas kernels for 0% -> 0%
where the time goes in v6:
time: 101 us; the launch traced here: 100 us
  waiting for transfers between devices  41.9 us (41%)
  starting transfers between devices  27.6 us (27%)
  local copies, waits for them, and re-layouts  19.8 us (20%)
  other arithmetic  5.31 us (5%)
  matrix products  4.51 us (4%)
  between operations  1.09 us (1%)
    all_to_all x1, waiting for transfers between devices, local(): gathered = lax.all_to_all(partial_copies, 'tp', 0, 0, tiled=True)  17.9 us
    all_to_all x1, waiting for transfers between devices, local(): arrived = lax.all_to_all(packed, 'req', 0, 0, tiled=True)  17.5 us
    all_to_all x1, starting transfers between devices, local(): everyone = lax.all_to_all(copies, 'req', 0, 0, tiled=True)  15 us
    slice x1, local copies, waits for them, and re-layouts, local(): pool_cache[:, :, 1].reshape(page_count, PAGE, heads_here, HEAD)  9.88 us
    all_to_all x1, starting transfers between devices, local(): gathered = lax.all_to_all(partial_copies, 'tp', 0, 0, tiled=True)  6.82 us
    all_to_all x1, waiting for transfers between devices, local(): everyone = lax.all_to_all(copies, 'req', 0, 0, tiled=True)  6.48 us
    all_to_all x1, starting transfers between devices, local(): arrived = lax.all_to_all(packed, 'req', 0, 0, tiled=True)  5.73 us
    slice x1, local copies, waits for them, and re-layouts, local(): tail_cache[:, :, 1].reshape(row_count, tail_slots, heads_here, HEAD)  2.17 us
  transfers between devices with their start and end apart: 3, of which 3 were waited for; matrix products, arithmetic and copies ran while one was open for 14% of the time, Pallas kernels for 0%

profile of v6, /device:TPU:1, one launch (start us, length us, event | category | flops | bytes accessed | tf_op | source)
XLA Modules:
  0.0 100.2 jit_solution(14138037197546931359)
XLA Ops:
  0.7 1.7 %broadcast_in_dim.65 = bf16[64,16,256]{2,1,0:T(8,128)(2,1)} broadcast(bf16[16,256]{1,0:T(8,128)(2,1)} %param.13), dimensions={1,2} | broadcast | bytes 532480 | tf_op jit(solution)/shard_map/broadcast_in_dim | solution.py:51
  2.4 15.0 %all-to-all-start = ((bf16[64,16,256]{2,1,0:T(8,128)(2,1)}), bf16[64,16,256]{2,1,0:T(8,128)(2,1)}, u32[]{:S(2)}, u32[]{:S(2)}) async-start(bf16[64,16,256]{2,1,0:T(8,128)(2,1)} %broadcast_in_dim.65), calls=%async_computation | async-start | bytes 1048576 | tf_op jit(solution)/shard_map/all_to_all | solution.py:52
  17.5 0.7 gather_fusion
  18.3 0.1 fusion.35
  18.7 9.9 %slice_reduce_fusion = (bf16[32,64,256]{2,1,0:T(8,128)(2,1)}, bf16[32,64,256]{2,1,0:T(8,128)(2,1)}) fusion(bf16[32,64,2,256]{3,2,1,0:T(2,128)(2,1)S(1)} %copy-done.2), kind=kLoop, calls=%fused_computation.4 | loop fusion | bytes 4194304 | tf_op jit(solution)/shard_map/slice | solution.py:57
  28.6 6.5 %all-to-all-done = bf16[64,16,256]{2,1,0:T(8,128)(2,1)} async-done(((bf16[64,16,256]{2,1,0:T(8,128)(2,1)}), bf16[64,16,256]{2,1,0:T(8,128)(2,1)}, u32[]{:S(2)}, u32[]{:S(2)}) %all-to-all-start) | async-done | bytes 524320 | tf_op jit(solution)/shard_map/all_to_all | solution.py:52
  35.1 1.1 %copy_bitcast_fusion = bf16[64,16,2,128]{3,1,2,0:T(8,128)(2,1)S(1)} fusion(bf16[64,16,256]{2,1,0:T(8,128)(2,1)} %all-to-all-done), kind=kLoop, calls=%fused_computation.19 | loop fusion | bytes 1048576 | tf_op jit(solution)/shard_map/reshape | solution.py:53
  36.2 0.6 gather_fusion.1
  36.8 1.5 %fusion.50 = (bf16[32,16,2]{1,2,0:T(2,128)(2,1)S(1)}, f32[32,16,2,64]{3,1,2,0:T(8,128)}) fusion(f32[32,2,64]{2,1,0:T(2,128)S(1)} %broadcast_multiply_fusion, bf16[32,16,2,128]{3,1,2,0:T(8,128)(2,1)S(1)} %gather_fusion.1, pred[32,64]{1,0:T(8,128)(4,1)S(1)} %get-tuple-element.20, bf16[32,64,256]{2,1,0:T(8,128)(2,1)S(1)} %copy-done.5), kind=kOutput, calls=%fused_computation.100 | convolution fusion | flops 17038336 | bytes 1593344 | tf_op jit(solution)/shard_map/pqhd,pshd->pqhs/dot_general | solution.py:63
  38.3 0.2 select_reduce_fusion
  38.6 0.1 copy.66
  38.7 0.6 gather_fusion.2
  39.3 1.4 %fusion.8 = f32[32,16,2]{1,2,0:T(2,128)S(1)} fusion(f32[32,16,2,64]{3,1,2,0:T(8,128)} %get-tuple-element.22, f32[32,16,2]{1,2,0:T(2,128)S(1)} %gather_fusion.2, pred[32,64]{1,0:T(8,128)(4,1)S(1)} %get-tuple-element.20), kind=kLoop, calls=%fused_computation.25 | loop fusion | flops 195584 | bytes 272384 | tf_op jit(solution)/shard_map/reduce_sum | solution.py:75
  40.7 0.1 copy.70
  40.8 0.2 fusion.51
  41.1 0.1 copy.72
  41.2 1.0 convolution_bitcast_fusion
  42.2 0.9 convolution_convert_fusion.1
  43.1 0.3 copy.71
  43.5 1.0 %maximum_maximum_fusion = bf16[64,40,128]{2,1,0:T(8,128)(2,1)} fusion(bf16[64,1,128]{2,1,0:T(2,128)(2,1)S(1)} %copy.72, bf16[64,32,128]{2,1,0:T(8,128)(2,1)S(1)} %copy.71, bf16[40]{0:T(256)(128)(2,1)S(1)} %pad.7.clone), kind=kLoop, calls=%fused_computation.18 | loop fusion | flops 1966080 | bytes 1196112 | tf_op jit(solution)/shard_map/concatenate | solution.py:95
  44.5 5.7 %all-to-all-start.1 = ((bf16[64,40,128]{2,1,0:T(8,128)(2,1)}), bf16[64,40,128]{2,1,0:T(8,128)(2,1)S(1)}, u32[]{:S(2)}, u32[]{:S(2)}) async-start(bf16[64,40,128]{2,1,0:T(8,128)(2,1)} %maximum_maximum_fusion), calls=%async_computation.1 | async-start | bytes 1310720 | tf_op jit(solution)/shard_map/all_to_all | solution.py:103
  50.3 0.1 fusion.29
  50.6 2.2 %slice_reduce_fusion.2 = (bf16[16,32,256]{2,1,0:T(8,128)(2,1)S(1)}, bf16[16,32,256]{2,1,0:T(8,128)(2,1)S(1)}) fusion(bf16[16,32,2,256]{3,2,1,0:T(2,128)(2,1)S(1)} %copy-done.3), kind=kLoop, calls=%fused_computation.21 | loop fusion | bytes 1048576 | tf_op jit(solution)/shard_map/slice | solution.py:114
  52.8 0.2 fusion.13
  53.0 0.1 fusion.44
  53.1 17.5 %all-to-all-done.1 = bf16[64,40,128]{2,1,0:T(8,128)(2,1)S(1)} async-done(((bf16[64,40,128]{2,1,0:T(8,128)(2,1)}), bf16[64,40,128]{2,1,0:T(8,128)(2,1)S(1)}, u32[]{:S(2)}, u32[]{:S(2)}) %all-to-all-start.1) | async-done | bytes 655392 | tf_op jit(solution)/shard_map/all_to_all | solution.py:103
  70.7 0.1 reduce_max.42
  70.8 0.1 copy.73
  70.9 0.1 fusion.40
  71.0 0.1 copy.74
  71.1 0.2 fusion.39
  71.3 0.1 sub.70
  71.4 0.1 fusion.28
  71.5 0.1 reduce_sum.71
  71.5 0.1 copy.76
  71.7 0.1 copy.75
  71.8 0.1 copy.77
  71.9 0.2 fusion.9
  72.1 0.2 fusion.11
  72.3 0.3 multiply_reduce_fusion
  72.6 0.1 fusion.38
  72.8 0.2 convolution_convert_fusion
  73.0 0.8 broadcast_in_dim.119
  73.9 6.8 %all-to-all-start.2 = ((bf16[8,16,2048]{2,1,0:T(8,128)(2,1)}), bf16[8,16,2048]{2,1,0:T(8,128)(2,1)S(1)}, u32[]{:S(2)}, u32[]{:S(2)}) async-start(bf16[8,16,2048]{2,1,0:T(8,128)(2,1)} %broadcast_in_dim.119), calls=%async_computation.2 | async-start | bytes 1048576 | tf_op jit(solution)/shard_map/all_to_all | solution.py:152
  80.7 17.9 %all-to-all-done.2 = bf16[8,16,2048]{2,1,0:T(8,128)(2,1)S(1)} async-done(((bf16[8,16,2048]{2,1,0:T(8,128)(2,1)}), bf16[8,16,2048]{2,1,0:T(8,128)(2,1)S(1)}, u32[]{:S(2)}, u32[]{:S(2)}) %all-to-all-start.2) | async-done | bytes 524320 | tf_op jit(solution)/shard_map/all_to_all | solution.py:152
  98.7 0.2 fusion.49
  98.9 0.6 constant_dynamic-slice_fusion
  99.5 0.7 add_convert_fusion.1
  (62 shorter events, 1.0 us)
Async XLA Ops:
  0.6 72.1 %copy-start = (bf16[256,2048]{1,0:T(8,128)(2,1)S(1)}, bf16[256,2048]{1,0:T(8,128)(2,1)}, u32[]{:S(2)}) copy-start(bf16[256,2048]{1,0:T(8,128)(2,1)} %param.22) | copy-start | bytes 3145732
  0.6 17.8 %copy-start.8 = (bf16[16,256]{1,0:T(8,128)(2,1)S(1)}, bf16[16,256]{1,0:T(8,128)(2,1)}, u32[]{:S(2)}) copy-start(bf16[16,256]{1,0:T(8,128)(2,1)} %param.13) | copy-start | bytes 24580
  0.7 16.8 %copy-start.11 = (s32[32]{0:T(128)S(1)}, s32[32]{0:T(128)}, u32[]{:S(2)}) copy-start(s32[32]{0:T(128)} %param.18) | copy-start | bytes 388
  0.7 16.8 %copy-start.1 = (s32[64]{0:T(128)S(1)}, s32[64]{0:T(128)}, u32[]{:S(2)}) copy-start(s32[64]{0:T(128)} %param.20) | copy-start | bytes 772
  0.7 17.5 %copy-start.12 = (s32[32]{0:T(128)S(1)}, s32[32]{0:T(128)}, u32[]{:S(2)}) copy-start(s32[32]{0:T(128)} %param.19) | copy-start | bytes 388
  0.7 17.7 %copy-start.9 = (bf16[16,2,256]{2,1,0:T(2,128)(2,1)S(1)}, bf16[16,2,256]{2,1,0:T(2,128)(2,1)}, u32[]{:S(2)}) copy-start(bf16[16,2,256]{2,1,0:T(2,128)(2,1)} %param.14) | copy-start | bytes 49156
  0.7 18.0 %copy-start.2 = (bf16[32,64,2,256]{3,2,1,0:T(2,128)(2,1)S(1)}, bf16[32,64,2,256]{3,2,1,0:T(2,128)(2,1)}, u32[]{:S(2)}) copy-start(bf16[32,64,2,256]{3,2,1,0:T(2,128)(2,1)} %param.17) | copy-start | bytes 6291460
  2.4 32.7 %all-to-all-start = ((bf16[64,16,256]{2,1,0:T(8,128)(2,1)}), bf16[64,16,256]{2,1,0:T(8,128)(2,1)}, u32[]{:S(2)}, u32[]{:S(2)}) async-start(bf16[64,16,256]{2,1,0:T(8,128)(2,1)} %broadcast_in_dim.65), calls=%async_computation | async-start | bytes 1048576 | tf_op jit(solution)/shard_map/all_to_all | solution.py:52
  28.6 8.2 %copy-start.5 = (bf16[32,64,256]{2,1,0:T(8,128)(2,1)S(1)}, bf16[32,64,256]{2,1,0:T(8,128)(2,1)}, u32[]{:S(2)}) copy-start(bf16[32,64,256]{2,1,0:T(8,128)(2,1)} %get-tuple-element.3) | copy-start | bytes 3145732
  36.8 4.3 %copy-start.4 = (bf16[32,64,256]{2,1,0:T(8,128)(2,1)S(1)}, bf16[32,64,256]{2,1,0:T(8,128)(2,1)}, u32[]{:S(2)}) copy-start(bf16[32,64,256]{2,1,0:T(8,128)(2,1)} %get-tuple-element.2) | copy-start | bytes 3145732
  38.3 2.8 %copy-start.6 = (f32[32,16,2,64]{3,1,2,0:T(8,128)S(1)}, f32[32,16,2,64]{3,1,2,0:T(8,128)}, u32[]{:S(2)}) copy-start(f32[32,16,2,64]{3,1,2,0:T(8,128)} %get-tuple-element.22) | copy-start | bytes 786436
  43.5 7.0 %copy-start.13 = (s32[16]{0:T(128)S(1)}, s32[16]{0:T(128)}, u32[]{:S(2)}) copy-start(s32[16]{0:T(128)} %param.16) | copy-start | bytes 196
  43.5 7.1 %copy-start.3 = (bf16[16,32,2,256]{3,2,1,0:T(2,128)(2,1)S(1)}, bf16[16,32,2,256]{3,2,1,0:T(2,128)(2,1)}, u32[]{:S(2)}) copy-start(bf16[16,32,2,256]{3,2,1,0:T(2,128)(2,1)} %param.15) | copy-start | bytes 1572868
  44.5 26.1 %all-to-all-start.1 = ((bf16[64,40,128]{2,1,0:T(8,128)(2,1)}), bf16[64,40,128]{2,1,0:T(8,128)(2,1)S(1)}, u32[]{:S(2)}, u32[]{:S(2)}) async-start(bf16[64,40,128]{2,1,0:T(8,128)(2,1)} %maximum_maximum_fusion), calls=%async_computation.1 | async-start | bytes 1310720 | tf_op jit(solution)/shard_map/all_to_all | solution.py:103
  72.7 8.0 %copy-start.10 = (bf16[2048]{0:T(1024)(128)(2,1)S(1)}, bf16[2048]{0:T(1024)(128)(2,1)}, u32[]{:S(2)}) copy-start(bf16[2048]{0:T(1024)(128)(2,1)} %param.23) | copy-start | bytes 12292
  72.7 8.0 %copy-start.14 = (bf16[256]{0:T(256)(128)(2,1)S(1)}, bf16[256]{0:T(256)(128)(2,1)}, u32[]{:S(2)}) copy-start(bf16[256]{0:T(256)(128)(2,1)} %param.24) | copy-start | bytes 1540
  72.8 8.0 %copy-start.15 = (bf16[256]{0:T(256)(128)(2,1)S(1)}, bf16[256]{0:T(256)(128)(2,1)}, u32[]{:S(2)}) copy-start(bf16[256]{0:T(256)(128)(2,1)} %param.25) | copy-start | bytes 1540
  73.0 25.7 %copy-start.7 = (bf16[16,2048]{1,0:T(8,128)(2,1)S(1)}, bf16[16,2048]{1,0:T(8,128)(2,1)}, u32[]{:S(2)}) copy-start(bf16[16,2048]{1,0:T(8,128)(2,1)} %param.21) | copy-start | bytes 196612
  73.9 24.8 %all-to-all-start.2 = ((bf16[8,16,2048]{2,1,0:T(8,128)(2,1)}), bf16[8,16,2048]{2,1,0:T(8,128)(2,1)S(1)}, u32[]{:S(2)}, u32[]{:S(2)}) async-start(bf16[8,16,2048]{2,1,0:T(8,128)(2,1)} %broadcast_in_dim.119), calls=%async_computation.2 | async-start | bytes 1048576 | tf_op jit(solution)/shard_map/all_to_all | solution.py:152

commit v7 on v4

--- a/solution.py
+++ b/solution.py
@@ -73,15 +73,13 @@
     page_ref = local_top.astype(f32)[safe_group]
     weights = jnp.where(usable[:, None, None, :], jnp.exp(scores - page_ref[..., None]), 0.0)
     page_totals = weights.sum(-1)
-    upper_part, lower_part = split_halves(weights)
-    page_accum = jnp.einsum("pqhs,pshd->pqhd", upper_part, page_values, preferred_element_type=f32)
-    page_accum = page_accum + jnp.einsum(
-        "pqhs,pshd->pqhd", lower_part, page_values, preferred_element_type=f32
+    page_accum = jnp.einsum(
+        "pqhs,pshd->pqhd", weights.astype(jnp.bfloat16), page_values, preferred_element_type=f32
     )
-    accum_upper, accum_lower = split_halves(page_accum.reshape(page_count, -1))
     spread = member.T.astype(jnp.bfloat16)
-    group_accum = jnp.dot(spread, accum_upper, preferred_element_type=f32)
-    group_accum = group_accum + jnp.dot(spread, accum_lower, preferred_element_type=f32)
+    group_accum = jnp.dot(
+        spread, page_accum.reshape(page_count, -1).astype(jnp.bfloat16), preferred_element_type=f32
+    )
     group_totals = jnp.dot(
         member.T.astype(f32), page_totals.reshape(page_count, -1), precision=highest
     )

time: 99.1 us -> 99.7 us (level)
  waiting for transfers between devices: 40.2 us -> 41.9 us
  matrix products: 4.75 us -> 3.44 us
    slice x1, local copies, waits for them, and re-layouts: 11.7 us -> 9.88 us  [local(): pool_cache[:, :, 1].reshape(page_count, PAGE, heads_here, HEAD)]
    all_to_all x1, waiting for transfers between devices: 4.8 us -> 6.48 us  [local(): everyone = lax.all_to_all(copies, 'req', 0, 0, tiled=True)]
    reduce_sum x0 -> x1, other arithmetic: none -> 1.44 us  [local(): page_totals = weights.sum(-1)]
    reshape x1, local copies, waits for them, and re-layouts: 0.09 us -> 1.13 us  [local(): by_group = everyone.reshape(group_count, row_count, heads_here, HEAD)]
  transfers between devices with their start and end apart: 3 -> 3, of which waited for: 3 -> 3; matrix products, arithmetic and copies ran while one was open for 16% -> 14% of each run, Pallas kernels for 0% -> 0%
where the time goes in v7:
time: 99.7 us; the launch traced here: 99.3 us
  waiting for transfers between devices  41.9 us (42%)
  starting transfers between devices  27.6 us (28%)
  local copies, waits for them, and re-layouts  20 us (20%)
  other arithmetic  5.31 us (5%)
  matrix products  3.44 us (3%)
  between operations  1.11 us (1%)
    all_to_all x1, waiting for transfers between devices, local(): gathered = lax.all_to_all(partial_copies, 'tp', 0, 0, tiled=True)  17.9 us
    all_to_all x1, waiting for transfers between devices, local(): arrived = lax.all_to_all(packed, 'req', 0, 0, tiled=True)  17.5 us
    all_to_all x1, starting transfers between devices, local(): everyone = lax.all_to_all(copies, 'req', 0, 0, tiled=True)  15 us
    slice x1, local copies, waits for them, and re-layouts, local(): pool_cache[:, :, 1].reshape(page_count, PAGE, heads_here, HEAD)  9.88 us
    all_to_all x1, starting transfers between devices, local(): gathered = lax.all_to_all(partial_copies, 'tp', 0, 0, tiled=True)  6.82 us
    all_to_all x1, waiting for transfers between devices, local(): everyone = lax.all_to_all(copies, 'req', 0, 0, tiled=True)  6.48 us
    all_to_all x1, starting transfers between devices, local(): arrived = lax.all_to_all(packed, 'req', 0, 0, tiled=True)  5.72 us
    slice x1, local copies, waits for them, and re-layouts, local(): tail_cache[:, :, 1].reshape(row_count, tail_slots, heads_here, HEAD)  2.17 us
  transfers between devices with their start and end apart: 3, of which 3 were waited for; matrix products, arithmetic and copies ran while one was open for 14% of the time, Pallas kernels for 0%

profile of v7, /device:TPU:1, one launch (start us, length us, event | category | flops | bytes accessed | tf_op | source)
XLA Modules:
  0.0 99.3 jit_solution(16922873576727042935)
XLA Ops:
  0.7 1.7 %broadcast_in_dim.65 = bf16[64,16,256]{2,1,0:T(8,128)(2,1)} broadcast(bf16[16,256]{1,0:T(8,128)(2,1)} %param.13), dimensions={1,2} | broadcast | bytes 532480 | tf_op jit(solution)/shard_map/broadcast_in_dim | solution.py:51
  2.4 15.0 %all-to-all-start = ((bf16[64,16,256]{2,1,0:T(8,128)(2,1)}), bf16[64,16,256]{2,1,0:T(8,128)(2,1)}, u32[]{:S(2)}, u32[]{:S(2)}) async-start(bf16[64,16,256]{2,1,0:T(8,128)(2,1)} %broadcast_in_dim.65), calls=%async_computation | async-start | bytes 1048576 | tf_op jit(solution)/shard_map/all_to_all | solution.py:52
  17.5 0.7 gather_fusion
  18.3 0.1 fusion.38
  18.7 9.9 %slice_reduce_fusion = (bf16[32,64,256]{2,1,0:T(8,128)(2,1)}, bf16[32,64,256]{2,1,0:T(8,128)(2,1)}) fusion(bf16[32,64,2,256]{3,2,1,0:T(2,128)(2,1)S(1)} %copy-done.2), kind=kLoop, calls=%fused_computation.5 | loop fusion | bytes 4194304 | tf_op jit(solution)/shard_map/slice | solution.py:57
  28.6 6.5 %all-to-all-done = bf16[64,16,256]{2,1,0:T(8,128)(2,1)} async-done(((bf16[64,16,256]{2,1,0:T(8,128)(2,1)}), bf16[64,16,256]{2,1,0:T(8,128)(2,1)}, u32[]{:S(2)}, u32[]{:S(2)}) %all-to-all-start) | async-done | bytes 524320 | tf_op jit(solution)/shard_map/all_to_all | solution.py:52
  35.1 1.1 %copy_bitcast_fusion = bf16[64,16,2,128]{3,1,2,0:T(8,128)(2,1)S(1)} fusion(bf16[64,16,256]{2,1,0:T(8,128)(2,1)} %all-to-all-done), kind=kLoop, calls=%fused_computation.21 | loop fusion | bytes 1048576 | tf_op jit(solution)/shard_map/reshape | solution.py:53
  36.2 0.6 gather_fusion.1
  36.8 1.5 %fusion.52 = (bf16[32,16,2]{1,2,0:T(2,128)(2,1)S(1)}, f32[32,16,2,64]{3,1,2,0:T(8,128)}) fusion(f32[32,2,64]{2,1,0:T(2,128)S(1)} %broadcast_multiply_fusion, bf16[32,16,2,128]{3,1,2,0:T(8,128)(2,1)S(1)} %gather_fusion.1, pred[32,64]{1,0:T(8,128)(4,1)S(1)} %get-tuple-element.20, bf16[32,64,256]{2,1,0:T(8,128)(2,1)S(1)} %copy-done.5), kind=kOutput, calls=%fused_computation.101 | convolution fusion | flops 17038336 | bytes 1593344 | tf_op jit(solution)/shard_map/pqhd,pshd->pqhs/dot_general | solution.py:63
  38.3 0.2 select_reduce_fusion
  38.6 0.1 copy.62
  38.7 0.6 gather_fusion.2
  39.3 1.4 %fusion.9 = f32[32,16,2]{1,2,0:T(2,128)S(1)} fusion(f32[32,16,2,64]{3,1,2,0:T(8,128)} %get-tuple-element.22, f32[32,16,2]{1,2,0:T(2,128)S(1)} %gather_fusion.2, pred[32,64]{1,0:T(8,128)(4,1)S(1)} %get-tuple-element.20), kind=kLoop, calls=%fused_computation.26 | loop fusion | flops 195584 | bytes 272384 | tf_op jit(solution)/shard_map/reduce_sum | solution.py:75
  40.8 0.2 fusion.53
  41.1 0.1 copy.67
  41.2 0.5 fusion.4
  41.6 0.2 copy.64
  41.9 0.2 convert_element_type.131
  42.0 0.4 fusion.2
  42.5 0.1 copy.91
  42.6 1.0 %maximum_maximum_fusion = bf16[64,40,128]{2,1,0:T(8,128)(2,1)} fusion(bf16[64,1,128]{2,1,0:T(2,128)(2,1)S(1)} %copy.67, bf16[64,32,128]{2,1,0:T(8,128)(2,1)S(1)} %bitcast.84, bf16[40]{0:T(256)(128)(2,1)S(1)} %pad.7.clone), kind=kLoop, calls=%fused_computation.20 | loop fusion | flops 1966080 | bytes 1196112 | tf_op jit(solution)/shard_map/concatenate | solution.py:99
  43.6 5.7 %all-to-all-start.1 = ((bf16[64,40,128]{2,1,0:T(8,128)(2,1)}), bf16[64,40,128]{2,1,0:T(8,128)(2,1)S(1)}, u32[]{:S(2)}, u32[]{:S(2)}) async-start(bf16[64,40,128]{2,1,0:T(8,128)(2,1)} %maximum_maximum_fusion), calls=%async_computation.1 | async-start | bytes 1310720 | tf_op jit(solution)/shard_map/all_to_all | solution.py:107
  49.4 0.1 fusion.32
  49.7 2.2 %slice_reduce_fusion.2 = (bf16[16,32,256]{2,1,0:T(8,128)(2,1)S(1)}, bf16[16,32,256]{2,1,0:T(8,128)(2,1)S(1)}) fusion(bf16[16,32,2,256]{3,2,1,0:T(2,128)(2,1)S(1)} %copy-done.3), kind=kLoop, calls=%fused_computation.22 | loop fusion | bytes 1048576 | tf_op jit(solution)/shard_map/slice | solution.py:118
  51.9 0.2 fusion.16
  52.1 0.1 fusion.46
  52.2 17.5 %all-to-all-done.1 = bf16[64,40,128]{2,1,0:T(8,128)(2,1)S(1)} async-done(((bf16[64,40,128]{2,1,0:T(8,128)(2,1)}), bf16[64,40,128]{2,1,0:T(8,128)(2,1)S(1)}, u32[]{:S(2)}, u32[]{:S(2)}) %all-to-all-start.1) | async-done | bytes 655392 | tf_op jit(solution)/shard_map/all_to_all | solution.py:107
  69.8 0.1 reduce_max.42
  69.8 0.1 copy.68
  70.0 0.1 fusion.42
  70.1 0.1 copy.69
  70.2 0.2 fusion.41
  70.3 0.1 sub.70
  70.4 0.1 fusion.31
  70.6 0.1 copy.71
  70.8 0.1 copy.70
  70.9 0.1 copy.72
  71.0 0.2 fusion.12
  71.2 0.2 fusion.14
  71.3 0.3 multiply_reduce_fusion
  71.7 0.1 fusion.40
  71.8 0.2 convolution_convert_fusion.1
  72.1 0.8 broadcast_in_dim.119
  72.9 6.8 %all-to-all-start.2 = ((bf16[8,16,2048]{2,1,0:T(8,128)(2,1)}), bf16[8,16,2048]{2,1,0:T(8,128)(2,1)S(1)}, u32[]{:S(2)}, u32[]{:S(2)}) async-start(bf16[8,16,2048]{2,1,0:T(8,128)(2,1)} %broadcast_in_dim.119), calls=%async_computation.2 | async-start | bytes 1048576 | tf_op jit(solution)/shard_map/all_to_all | solution.py:156
  79.8 17.9 %all-to-all-done.2 = bf16[8,16,2048]{2,1,0:T(8,128)(2,1)S(1)} async-done(((bf16[8,16,2048]{2,1,0:T(8,128)(2,1)}), bf16[8,16,2048]{2,1,0:T(8,128)(2,1)S(1)}, u32[]{:S(2)}, u32[]{:S(2)}) %all-to-all-start.2) | async-done | bytes 524320 | tf_op jit(solution)/shard_map/all_to_all | solution.py:156
  97.8 0.2 fusion.51
  98.0 0.6 constant_dynamic-slice_fusion
  98.6 0.7 add_convert_fusion.1
  (64 shorter events, 1.2 us)
Async XLA Ops:
  0.6 71.2 %copy-start = (bf16[256,2048]{1,0:T(8,128)(2,1)S(1)}, bf16[256,2048]{1,0:T(8,128)(2,1)}, u32[]{:S(2)}) copy-start(bf16[256,2048]{1,0:T(8,128)(2,1)} %param.22) | copy-start | bytes 3145732
  0.6 17.8 %copy-start.8 = (bf16[16,256]{1,0:T(8,128)(2,1)S(1)}, bf16[16,256]{1,0:T(8,128)(2,1)}, u32[]{:S(2)}) copy-start(bf16[16,256]{1,0:T(8,128)(2,1)} %param.13) | copy-start | bytes 24580
  0.7 16.8 %copy-start.11 = (s32[32]{0:T(128)S(1)}, s32[32]{0:T(128)}, u32[]{:S(2)}) copy-start(s32[32]{0:T(128)} %param.18) | copy-start | bytes 388
  0.7 16.8 %copy-start.1 = (s32[64]{0:T(128)S(1)}, s32[64]{0:T(128)}, u32[]{:S(2)}) copy-start(s32[64]{0:T(128)} %param.20) | copy-start | bytes 772
  0.7 17.5 %copy-start.12 = (s32[32]{0:T(128)S(1)}, s32[32]{0:T(128)}, u32[]{:S(2)}) copy-start(s32[32]{0:T(128)} %param.19) | copy-start | bytes 388
  0.7 17.7 %copy-start.9 = (bf16[16,2,256]{2,1,0:T(2,128)(2,1)S(1)}, bf16[16,2,256]{2,1,0:T(2,128)(2,1)}, u32[]{:S(2)}) copy-start(bf16[16,2,256]{2,1,0:T(2,128)(2,1)} %param.14) | copy-start | bytes 49156
  0.7 18.0 %copy-start.2 = (bf16[32,64,2,256]{3,2,1,0:T(2,128)(2,1)S(1)}, bf16[32,64,2,256]{3,2,1,0:T(2,128)(2,1)}, u32[]{:S(2)}) copy-start(bf16[32,64,2,256]{3,2,1,0:T(2,128)(2,1)} %param.17) | copy-start | bytes 6291460
  2.4 32.7 %all-to-all-start = ((bf16[64,16,256]{2,1,0:T(8,128)(2,1)}), bf16[64,16,256]{2,1,0:T(8,128)(2,1)}, u32[]{:S(2)}, u32[]{:S(2)}) async-start(bf16[64,16,256]{2,1,0:T(8,128)(2,1)} %broadcast_in_dim.65), calls=%async_computation | async-start | bytes 1048576 | tf_op jit(solution)/shard_map/all_to_all | solution.py:52
  28.6 8.2 %copy-start.5 = (bf16[32,64,256]{2,1,0:T(8,128)(2,1)S(1)}, bf16[32,64,256]{2,1,0:T(8,128)(2,1)}, u32[]{:S(2)}) copy-start(bf16[32,64,256]{2,1,0:T(8,128)(2,1)} %get-tuple-element.3) | copy-start | bytes 3145732
  36.8 4.3 %copy-start.4 = (bf16[32,64,256]{2,1,0:T(8,128)(2,1)S(1)}, bf16[32,64,256]{2,1,0:T(8,128)(2,1)}, u32[]{:S(2)}) copy-start(bf16[32,64,256]{2,1,0:T(8,128)(2,1)} %get-tuple-element.2) | copy-start | bytes 3145732
  38.3 2.8 %copy-start.6 = (f32[32,16,2,64]{3,1,2,0:T(8,128)S(1)}, f32[32,16,2,64]{3,1,2,0:T(8,128)}, u32[]{:S(2)}) copy-start(f32[32,16,2,64]{3,1,2,0:T(8,128)} %get-tuple-element.22) | copy-start | bytes 786436
  42.6 7.0 %copy-start.13 = (s32[16]{0:T(128)S(1)}, s32[16]{0:T(128)}, u32[]{:S(2)}) copy-start(s32[16]{0:T(128)} %param.16) | copy-start | bytes 196
  42.6 7.1 %copy-start.3 = (bf16[16,32,2,256]{3,2,1,0:T(2,128)(2,1)S(1)}, bf16[16,32,2,256]{3,2,1,0:T(2,128)(2,1)}, u32[]{:S(2)}) copy-start(bf16[16,32,2,256]{3,2,1,0:T(2,128)(2,1)} %param.15) | copy-start | bytes 1572868
  43.6 26.1 %all-to-all-start.1 = ((bf16[64,40,128]{2,1,0:T(8,128)(2,1)}), bf16[64,40,128]{2,1,0:T(8,128)(2,1)S(1)}, u32[]{:S(2)}, u32[]{:S(2)}) async-start(bf16[64,40,128]{2,1,0:T(8,128)(2,1)} %maximum_maximum_fusion), calls=%async_computation.1 | async-start | bytes 1310720 | tf_op jit(solution)/shard_map/all_to_all | solution.py:107
  71.8 8.0 %copy-start.10 = (bf16[2048]{0:T(1024)(128)(2,1)S(1)}, bf16[2048]{0:T(1024)(128)(2,1)}, u32[]{:S(2)}) copy-start(bf16[2048]{0:T(1024)(128)(2,1)} %param.23) | copy-start | bytes 12292
  71.8 8.0 %copy-start.14 = (bf16[256]{0:T(256)(128)(2,1)S(1)}, bf16[256]{0:T(256)(128)(2,1)}, u32[]{:S(2)}) copy-start(bf16[256]{0:T(256)(128)(2,1)} %param.24) | copy-start | bytes 1540
  71.8 8.0 %copy-start.15 = (bf16[256]{0:T(256)(128)(2,1)S(1)}, bf16[256]{0:T(256)(128)(2,1)}, u32[]{:S(2)}) copy-start(bf16[256]{0:T(256)(128)(2,1)} %param.25) | copy-start | bytes 1540
  72.1 25.7 %copy-start.7 = (bf16[16,2048]{1,0:T(8,128)(2,1)S(1)}, bf16[16,2048]{1,0:T(8,128)(2,1)}, u32[]{:S(2)}) copy-start(bf16[16,2048]{1,0:T(8,128)(2,1)} %param.21) | copy-start | bytes 196612
  72.9 24.8 %all-to-all-start.2 = ((bf16[8,16,2048]{2,1,0:T(8,128)(2,1)}), bf16[8,16,2048]{2,1,0:T(8,128)(2,1)S(1)}, u32[]{:S(2)}, u32[]{:S(2)}) async-start(bf16[8,16,2048]{2,1,0:T(8,128)(2,1)} %broadcast_in_dim.119), calls=%async_computation.2 | async-start | bytes 1048576 | tf_op jit(solution)/shard_map/all_to_all | solution.py:156

commit v8 on v4

--- a/solution.py
+++ b/solution.py
@@ -133,17 +133,20 @@
     )
     own_scores = own_scores + slopes[None, :] * tail_len.astype(f32)[:, None]
     home_top = jnp.maximum(tail_scores.max(-1), own_scores)
-    row_top = jnp.maximum(home_top, part_top.max(0))
-    part_scale = jnp.exp(part_top - row_top[None])
-    pool_totals = jnp.sum(part_scale * part_totals, 0)
-    pool_accum = jnp.sum(part_scale[..., None] * part_accum, 0)
-    tail_weights = jnp.exp(tail_scores - row_top[:, :, None])
-    own_weights = jnp.exp(own_scores - row_top)
+    tail_weights = jnp.exp(tail_scores - home_top[:, :, None])
+    own_weights = jnp.exp(own_scores - home_top)
     totals = tail_weights.sum(-1) + own_weights
     upper_part, lower_part = split_halves(tail_weights)
     accum = jnp.einsum("qhj,qjhd->qhd", upper_part, tail_values, preferred_element_type=f32)
     accum = accum + jnp.einsum("qhj,qjhd->qhd", lower_part, tail_values, preferred_element_type=f32)
     home_accum = accum + own_weights[:, :, None] * fresh_values.astype(f32)
+    row_top = jnp.maximum(home_top, part_top.max(0))
+    part_scale = jnp.exp(part_top - row_top[None])
+    pool_totals = jnp.sum(part_scale * part_totals, 0)
+    pool_accum = jnp.sum(part_scale[..., None] * part_accum, 0)
+    home_scale = jnp.exp(home_top - row_top)
+    totals = totals * home_scale
+    home_accum = home_accum * home_scale[:, :, None]
     attention = ((pool_accum + home_accum) / (pool_totals + totals)[:, :, None]).astype(
         jnp.bfloat16
     )

time: 99.1 us -> 99.2 us (level)
  no operation moved by 1% of the time
where the time goes in v8:
time: 99.2 us; the launch traced here: 98.8 us
  waiting for transfers between devices  40.2 us (41%)
  starting transfers between devices  27.4 us (28%)
  local copies, waits for them, and re-layouts  21 us (21%)
  matrix products  4.74 us (5%)
  other arithmetic  4.37 us (4%)
  between operations  1.07 us (1%)
    all_to_all x1, waiting for transfers between devices, local(): gathered = lax.all_to_all(partial_copies, 'tp', 0, 0, tiled=True)  17.9 us
    all_to_all x1, waiting for transfers between devices, local(): arrived = lax.all_to_all(packed, 'req', 0, 0, tiled=True)  17.5 us
    all_to_all x1, starting transfers between devices, local(): everyone = lax.all_to_all(copies, 'req', 0, 0, tiled=True)  14.8 us
    slice x1, local copies, waits for them, and re-layouts, local(): pool_cache[:, :, 1].reshape(page_count, PAGE, heads_here, HEAD)  11.7 us
    all_to_all x1, starting transfers between devices, local(): gathered = lax.all_to_all(partial_copies, 'tp', 0, 0, tiled=True)  6.82 us
    all_to_all x1, starting transfers between devices, local(): arrived = lax.all_to_all(packed, 'req', 0, 0, tiled=True)  5.73 us
    all_to_all x1, waiting for transfers between devices, local(): everyone = lax.all_to_all(copies, 'req', 0, 0, tiled=True)  4.8 us
    slice x1, local copies, waits for them, and re-layouts, local(): tail_cache[:, :, 1].reshape(row_count, tail_slots, heads_here, HEAD)  2.17 us
  transfers between devices with their start and end apart: 3, of which 3 were waited for; matrix products, arithmetic and copies ran while one was open for 16% of the time, Pallas kernels for 0%

profile of v8, /device:TPU:1, one launch (start us, length us, event | category | flops | bytes accessed | tf_op | source)
XLA Modules:
  0.0 98.8 jit_solution(14361707744501764597)
XLA Ops:
  0.7 1.6 %broadcast_in_dim.65 = bf16[64,16,256]{2,1,0:T(8,128)(2,1)} broadcast(bf16[16,256]{1,0:T(8,128)(2,1)} %param.13), dimensions={1,2} | broadcast | bytes 532480 | tf_op jit(solution)/shard_map/broadcast_in_dim | solution.py:51
  2.3 14.8 %all-to-all-start = ((bf16[64,16,256]{2,1,0:T(8,128)(2,1)}), bf16[64,16,256]{2,1,0:T(8,128)(2,1)S(1)}, u32[]{:S(2)}, u32[]{:S(2)}) async-start(bf16[64,16,256]{2,1,0:T(8,128)(2,1)} %broadcast_in_dim.65), calls=%async_computation | async-start | bytes 1048576 | tf_op jit(solution)/shard_map/all_to_all | solution.py:52
  17.2 0.7 gather_fusion
  18.0 0.1 fusion.41
  18.4 11.7 %slice_reduce_fusion = (bf16[32,64,256]{2,1,0:T(8,128)(2,1)S(1)}, bf16[32,64,256]{2,1,0:T(8,128)(2,1)}) fusion(bf16[32,64,2,256]{3,2,1,0:T(2,128)(2,1)} %param.17), kind=kLoop, calls=%fused_computation.6 | loop fusion | bytes 4194304 | tf_op jit(solution)/shard_map/slice | solution.py:57
  30.1 4.8 %all-to-all-done = bf16[64,16,256]{2,1,0:T(8,128)(2,1)S(1)} async-done(((bf16[64,16,256]{2,1,0:T(8,128)(2,1)}), bf16[64,16,256]{2,1,0:T(8,128)(2,1)S(1)}, u32[]{:S(2)}, u32[]{:S(2)}) %all-to-all-start) | async-done | bytes 524320 | tf_op jit(solution)/shard_map/all_to_all | solution.py:52
  34.9 0.1 copy_bitcast_fusion
  35.0 0.6 gather_fusion.1
  35.6 2.0 %fusion.60 = (bf16[32,16,2]{1,2,0:T(2,128)(2,1)S(1)}, f32[32,16,2,64]{3,1,2,0:T(8,128)S(1)}) fusion(f32[32,2,64]{2,1,0:T(2,128)S(1)} %broadcast_multiply_fusion, bf16[32,16,2,128]{3,1,2,0:T(8,128)(2,1)S(1)} %gather_fusion.1, pred[32,64]{1,0:T(8,128)(4,1)S(1)} %get-tuple-element.25, bf16[32,64,256]{2,1,0:T(8,128)(2,1)} %get-tuple-element.3), kind=kOutput, calls=%fused_computation.110 | convolution fusion | flops 17038336 | bytes 1593344 | tf_op jit(solution)/shard_map/pqhd,pshd->pqhs/dot_general | solution.py:63
  37.6 0.2 select_reduce_fusion
  37.8 0.1 copy.69
  37.9 0.6 gather_fusion.2
  38.5 0.4 fusion.14
  39.0 0.4 fusion.7
  39.3 0.5 fusion.1
  39.8 0.3 copy.72
  40.1 0.4 reshape.262
  40.6 0.4 fusion.56
  41.0 0.4 fusion.4
  41.4 0.1 copy.100
  41.6 0.2 fusion.61
  41.9 0.1 copy.75
  42.0 1.0 %maximum_maximum_fusion = bf16[64,40,128]{2,1,0:T(8,128)(2,1)} fusion(bf16[64,1,128]{2,1,0:T(2,128)(2,1)S(1)} %copy.75, bf16[64,32,128]{2,1,0:T(8,128)(2,1)S(1)} %bitcast.90, bf16[40]{0:T(256)(128)(2,1)S(1)} %pad.7.clone), kind=kLoop, calls=%fused_computation.24 | loop fusion | flops 1966080 | bytes 1196112 | tf_op jit(solution)/shard_map/concatenate | solution.py:101
  43.0 5.7 %all-to-all-start.1 = ((bf16[64,40,128]{2,1,0:T(8,128)(2,1)}), bf16[64,40,128]{2,1,0:T(8,128)(2,1)S(1)}, u32[]{:S(2)}, u32[]{:S(2)}) async-start(bf16[64,40,128]{2,1,0:T(8,128)(2,1)} %maximum_maximum_fusion), calls=%async_computation.1 | async-start | bytes 1310720 | tf_op jit(solution)/shard_map/all_to_all | solution.py:109
  48.7 0.1 fusion.35
  49.1 2.2 %slice_reduce_fusion.2 = (bf16[16,32,256]{2,1,0:T(8,128)(2,1)S(1)}, bf16[16,32,256]{2,1,0:T(8,128)(2,1)S(1)}) fusion(bf16[16,32,2,256]{3,2,1,0:T(2,128)(2,1)S(1)} %copy-done.2), kind=kLoop, calls=%fused_computation.26 | loop fusion | bytes 1048576 | tf_op jit(solution)/shard_map/slice | solution.py:120
  51.3 0.2 fusion.19
  51.5 0.1 fusion.49
  51.6 17.5 %all-to-all-done.1 = bf16[64,40,128]{2,1,0:T(8,128)(2,1)S(1)} async-done(((bf16[64,40,128]{2,1,0:T(8,128)(2,1)}), bf16[64,40,128]{2,1,0:T(8,128)(2,1)S(1)}, u32[]{:S(2)}, u32[]{:S(2)}) %all-to-all-start.1) | async-done | bytes 655392 | tf_op jit(solution)/shard_map/all_to_all | solution.py:109
  69.2 0.1 copy.76
  69.4 0.2 fusion.44
  69.6 0.1 copy.77
  69.6 0.1 sub.81
  69.7 0.1 fusion.34
  69.9 0.1 copy.80
  70.1 0.1 copy.78
  70.3 0.1 fusion.46
  70.4 0.2 fusion.15
  70.6 0.2 fusion.17
  70.8 0.3 multiply_reduce_fusion
  71.2 0.1 fusion.43
  71.3 0.2 convolution_convert_fusion
  71.6 0.8 broadcast_in_dim.120
  72.4 6.8 %all-to-all-start.2 = ((bf16[8,16,2048]{2,1,0:T(8,128)(2,1)}), bf16[8,16,2048]{2,1,0:T(8,128)(2,1)S(1)}, u32[]{:S(2)}, u32[]{:S(2)}) async-start(bf16[8,16,2048]{2,1,0:T(8,128)(2,1)} %broadcast_in_dim.120), calls=%async_computation.2 | async-start | bytes 1048576 | tf_op jit(solution)/shard_map/all_to_all | solution.py:161
  79.3 17.9 %all-to-all-done.2 = bf16[8,16,2048]{2,1,0:T(8,128)(2,1)S(1)} async-done(((bf16[8,16,2048]{2,1,0:T(8,128)(2,1)}), bf16[8,16,2048]{2,1,0:T(8,128)(2,1)S(1)}, u32[]{:S(2)}, u32[]{:S(2)}) %all-to-all-start.2) | async-done | bytes 524320 | tf_op jit(solution)/shard_map/all_to_all | solution.py:161
  97.3 0.2 fusion.52
  97.5 0.6 constant_dynamic-slice_fusion
  98.1 0.7 add_convert_fusion.1
  (60 shorter events, 1.4 us)
Async XLA Ops:
  0.6 70.7 %copy-start = (bf16[256,2048]{1,0:T(8,128)(2,1)S(1)}, bf16[256,2048]{1,0:T(8,128)(2,1)}, u32[]{:S(2)}) copy-start(bf16[256,2048]{1,0:T(8,128)(2,1)} %param.22) | copy-start | bytes 3145732
  0.6 17.6 %copy-start.4 = (bf16[16,256]{1,0:T(8,128)(2,1)S(1)}, bf16[16,256]{1,0:T(8,128)(2,1)}, u32[]{:S(2)}) copy-start(bf16[16,256]{1,0:T(8,128)(2,1)} %param.13) | copy-start | bytes 24580
  0.7 16.5 %copy-start.6 = (s32[32]{0:T(128)S(1)}, s32[32]{0:T(128)}, u32[]{:S(2)}) copy-start(s32[32]{0:T(128)} %param.18) | copy-start | bytes 388
  0.7 16.6 %copy-start.1 = (s32[64]{0:T(128)S(1)}, s32[64]{0:T(128)}, u32[]{:S(2)}) copy-start(s32[64]{0:T(128)} %param.20) | copy-start | bytes 772
  0.7 17.3 %copy-start.8 = (s32[32]{0:T(128)S(1)}, s32[32]{0:T(128)}, u32[]{:S(2)}) copy-start(s32[32]{0:T(128)} %param.19) | copy-start | bytes 388
  0.7 17.4 %copy-start.5 = (bf16[16,2,256]{2,1,0:T(2,128)(2,1)S(1)}, bf16[16,2,256]{2,1,0:T(2,128)(2,1)}, u32[]{:S(2)}) copy-start(bf16[16,2,256]{2,1,0:T(2,128)(2,1)} %param.14) | copy-start | bytes 49156
  2.3 32.6 %all-to-all-start = ((bf16[64,16,256]{2,1,0:T(8,128)(2,1)}), bf16[64,16,256]{2,1,0:T(8,128)(2,1)S(1)}, u32[]{:S(2)}, u32[]{:S(2)}) async-start(bf16[64,16,256]{2,1,0:T(8,128)(2,1)} %broadcast_in_dim.65), calls=%async_computation | async-start | bytes 1048576 | tf_op jit(solution)/shard_map/all_to_all | solution.py:52
  41.8 7.1 %copy-start.9 = (s32[16]{0:T(128)S(1)}, s32[16]{0:T(128)}, u32[]{:S(2)}) copy-start(s32[16]{0:T(128)} %param.16) | copy-start | bytes 196
  41.8 7.2 %copy-start.2 = (bf16[16,32,2,256]{3,2,1,0:T(2,128)(2,1)S(1)}, bf16[16,32,2,256]{3,2,1,0:T(2,128)(2,1)}, u32[]{:S(2)}) copy-start(bf16[16,32,2,256]{3,2,1,0:T(2,128)(2,1)} %param.15) | copy-start | bytes 1572868
  43.0 26.1 %all-to-all-start.1 = ((bf16[64,40,128]{2,1,0:T(8,128)(2,1)}), bf16[64,40,128]{2,1,0:T(8,128)(2,1)S(1)}, u32[]{:S(2)}, u32[]{:S(2)}) async-start(bf16[64,40,128]{2,1,0:T(8,128)(2,1)} %maximum_maximum_fusion), calls=%async_computation.1 | async-start | bytes 1310720 | tf_op jit(solution)/shard_map/all_to_all | solution.py:109
  71.3 8.0 %copy-start.7 = (bf16[2048]{0:T(1024)(128)(2,1)S(1)}, bf16[2048]{0:T(1024)(128)(2,1)}, u32[]{:S(2)}) copy-start(bf16[2048]{0:T(1024)(128)(2,1)} %param.23) | copy-start | bytes 12292
  71.3 8.0 %copy-start.10 = (bf16[256]{0:T(256)(128)(2,1)S(1)}, bf16[256]{0:T(256)(128)(2,1)}, u32[]{:S(2)}) copy-start(bf16[256]{0:T(256)(128)(2,1)} %param.24) | copy-start | bytes 1540
  71.3 8.0 %copy-start.11 = (bf16[256]{0:T(256)(128)(2,1)S(1)}, bf16[256]{0:T(256)(128)(2,1)}, u32[]{:S(2)}) copy-start(bf16[256]{0:T(256)(128)(2,1)} %param.25) | copy-start | bytes 1540
  71.6 25.7 %copy-start.3 = (bf16[16,2048]{1,0:T(8,128)(2,1)S(1)}, bf16[16,2048]{1,0:T(8,128)(2,1)}, u32[]{:S(2)}) copy-start(bf16[16,2048]{1,0:T(8,128)(2,1)} %param.21) | copy-start | bytes 196612
  72.4 24.8 %all-to-all-start.2 = ((bf16[8,16,2048]{2,1,0:T(8,128)(2,1)}), bf16[8,16,2048]{2,1,0:T(8,128)(2,1)S(1)}, u32[]{:S(2)}, u32[]{:S(2)}) async-start(bf16[8,16,2048]{2,1,0:T(8,128)(2,1)} %broadcast_in_dim.120), calls=%async_computation.2 | async-start | bytes 1048576 | tf_op jit(solution)/shard_map/all_to_all | solution.py:161

commit v9 on v4

--- a/solution.py
+++ b/solution.py
@@ -53,16 +53,13 @@
     by_group = everyone.reshape(group_count, row_count, heads_here, HEAD)
     safe_group = jnp.clip(page_group, 0, group_count - 1)
     page_queries = by_group[safe_group]
-    page_keys = pool_cache[:, :, 0].reshape(page_count, PAGE, heads_here, HEAD)
-    page_values = pool_cache[:, :, 1].reshape(page_count, PAGE, heads_here, HEAD)
+    page_kv = pool_cache.reshape(page_count, PAGE * 2, heads_here, HEAD)
     prompt_here = prompt_len[safe_group]
     positions = page_start[:, None] + jnp.arange(PAGE)[None, :]
     usable = (positions < prompt_here[:, None]) & (page_group[:, None] >= 0)
     offsets = (positions - prompt_here[:, None]).astype(f32)
-    scores = (
-        jnp.einsum("pqhd,pshd->pqhs", page_queries, page_keys, preferred_element_type=f32)
-        * inv_root
-    )
+    both = jnp.einsum("pqhd,pshd->pqhs", page_queries, page_kv, preferred_element_type=f32)
+    scores = both.reshape(both.shape[:3] + (PAGE, 2))[..., 0] * inv_root
     scores = scores + slopes[None, None, :, None] * offsets[:, None, None, :]
     scores = jnp.where(usable[:, None, None, :], scores, masked_score)
 
@@ -74,9 +71,14 @@
     weights = jnp.where(usable[:, None, None, :], jnp.exp(scores - page_ref[..., None]), 0.0)
     page_totals = weights.sum(-1)
     upper_part, lower_part = split_halves(weights)
-    page_accum = jnp.einsum("pqhs,pshd->pqhd", upper_part, page_values, preferred_element_type=f32)
+    on_values = lambda part: jnp.stack([jnp.zeros_like(part), part], -1).reshape(
+        part.shape[:3] + (PAGE * 2,)
+    )
+    page_accum = jnp.einsum(
+        "pqhs,pshd->pqhd", on_values(upper_part), page_kv, preferred_element_type=f32
+    )
     page_accum = page_accum + jnp.einsum(
-        "pqhs,pshd->pqhd", lower_part, page_values, preferred_element_type=f32
+        "pqhs,pshd->pqhd", on_values(lower_part), page_kv, preferred_element_type=f32
     )
     accum_upper, accum_lower = split_halves(page_accum.reshape(page_count, -1))
     spread = member.T.astype(jnp.bfloat16)

time: 99.1 us -> 133 us (1.34)
  local copies, waits for them, and re-layouts: 20.9 us -> 42.3 us
  other arithmetic: 4.34 us -> 10.5 us
  matrix products: 4.75 us -> 8.68 us
    reshape x0 -> x3, local copies, waits for them, and re-layouts: none -> 11.2 us  [the longest x1 6.03 us: local(): page_kv = pool_cache.reshape(page_count, PAGE * 2, heads_here, HEAD)]
    slice x1, local copies, waits for them, and re-layouts: 11.7 us -> 2.29 us  [local(): scores = both.reshape(both.shape[:3] + (PAGE, 2))[..., 0] * inv_root]
    unnamed x25 -> x38, local copies, waits for them, and re-layouts: 0.16 us -> 6.55 us
    another operation x0 -> x2, local copies, waits for them, and re-layouts: none -> 4.45 us  [local(): jnp.stack([jnp.zeros_like(part), part], -1)]
    transpose x0 -> x1, local copies, waits for them, and re-layouts: none -> 3.3 us  [local(): jnp.einsum('pqhd,pshd->pqhs', page_queries, page_kv, preferred_element_ty...]
    dot_general x3, matrix products: 2.85 us -> 6.13 us  [the longest x1 2.43 us: local(): jnp.einsum('pqhs,pshd->pqhd', on_values(lower_part), page_kv, preferred_e...]
    another operation x0 -> x1, other arithmetic: none -> 2.05 us  [local(): jnp.stack([jnp.zeros_like(part), part], -1)]
    reshape x2, local copies, waits for them, and re-layouts: 0.02 us -> 2.01 us  [local(): home_queries = queries.reshape(row_count, heads_here, HEAD)]
  transfers between devices with their start and end apart: 3 -> 3, of which waited for: 3 -> 3; matrix products, arithmetic and copies ran while one was open for 16% -> 11% of each run, Pallas kernels for 0% -> 0%
where the time goes in v9:
time: 133 us; the launch traced here: 131 us
  local copies, waits for them, and re-layouts  42.3 us (32%)
  waiting for transfers between devices  41.3 us (31%)
  starting transfers between devices  27.6 us (21%)
  other arithmetic  10.5 us (8%)
  matrix products  8.68 us (7%)
    all_to_all x1, waiting for transfers between devices, local(): gathered = lax.all_to_all(partial_copies, 'tp', 0, 0, tiled=True)  17.9 us
    all_to_all x1, waiting for transfers between devices, local(): arrived = lax.all_to_all(packed, 'req', 0, 0, tiled=True)  17.5 us
    all_to_all x1, starting transfers between devices, local(): everyone = lax.all_to_all(copies, 'req', 0, 0, tiled=True)  15 us
    all_to_all x1, starting transfers between devices, local(): gathered = lax.all_to_all(partial_copies, 'tp', 0, 0, tiled=True)  6.82 us
    unnamed x38, local copies, waits for them, and re-layouts  6.55 us
    reshape x1, local copies, waits for them, and re-layouts, local(): page_kv = pool_cache.reshape(page_count, PAGE * 2, heads_here, HEAD)  6.03 us
    all_to_all x1, waiting for transfers between devices, local(): everyone = lax.all_to_all(copies, 'req', 0, 0, tiled=True)  5.88 us
    all_to_all x1, starting transfers between devices, local(): arrived = lax.all_to_all(packed, 'req', 0, 0, tiled=True)  5.72 us
  transfers between devices with their start and end apart: 3, of which 3 were waited for; matrix products, arithmetic and copies ran while one was open for 11% of the time, Pallas kernels for 0%

profile of v9, /device:TPU:1, one launch (start us, length us, event | category | flops | bytes accessed | tf_op | source)
XLA Modules:
  0.0 131.4 jit_solution(15079574691781377172)
XLA Ops:
  0.6 1.6 %broadcast_in_dim.62 = bf16[64,16,256]{2,1,0:T(8,128)(2,1)} broadcast(bf16[16,256]{1,0:T(8,128)(2,1)} %param.13), dimensions={1,2} | broadcast | bytes 532480 | tf_op jit(solution)/shard_map/broadcast_in_dim | solution.py:51
  2.3 15.0 %all-to-all-start = ((bf16[64,16,256]{2,1,0:T(8,128)(2,1)}), bf16[64,16,256]{2,1,0:T(8,128)(2,1)}, u32[]{:S(2)}, u32[]{:S(2)}) async-start(bf16[64,16,256]{2,1,0:T(8,128)(2,1)} %broadcast_in_dim.62), calls=%async_computation | async-start | bytes 1048576 | tf_op jit(solution)/shard_map/all_to_all | solution.py:52
  17.3 0.7 compare_select_fusion
  18.0 0.9 slice_convert_fusion.1
  18.8 1.3 reshape.322
  20.1 0.7 reshape.282
  20.9 6.0 %reshape.275 = bf16[32,128,2,128]{3,2,1,0:T(2,128)(2,1)S(1)} reshape(bf16[32,64,2,256]{3,2,1,0:T(2,128)(2,1)} %param.17) | data formatting | bytes 4194304 | tf_op jit(solution)/shard_map/reshape | solution.py:56
  26.9 0.5 convert_element_type.148
  27.5 0.7 gather_fusion
  28.2 0.6 pad.9.clone
  29.1 5.9 %all-to-all-done = bf16[64,16,256]{2,1,0:T(8,128)(2,1)} async-done(((bf16[64,16,256]{2,1,0:T(8,128)(2,1)}), bf16[64,16,256]{2,1,0:T(8,128)(2,1)}, u32[]{:S(2)}, u32[]{:S(2)}) %all-to-all-start) | async-done | bytes 524320 | tf_op jit(solution)/shard_map/all_to_all | solution.py:52
  34.9 1.9 %copy_bitcast_fusion = bf16[64,16,2,128]{3,1,2,0:T(8,128)(2,1)} fusion(bf16[64,16,256]{2,1,0:T(8,128)(2,1)} %all-to-all-done), kind=kLoop, calls=%fused_computation.19 | loop fusion | bytes 1048576 | tf_op jit(solution)/shard_map/reshape | solution.py:53
  36.9 1.6 %gather_fusion.1 = bf16[32,16,2,128]{3,1,2,0:T(8,128)(2,1)S(1)} fusion(bf16[64,16,2,128]{3,1,2,0:T(8,128)(2,1)} %copy_bitcast_fusion, s32[1024]{0:T(1024)S(1)} %pad_clamp_fusion), kind=kCustom, calls=%fused_computation.1 | custom fusion | bytes 524416 | tf_op jit(solution)/shard_map/gather | solution.py:55
  38.5 2.0 %fusion.7 = f32[32,16,2,128]{3,1,2,0:T(8,128)} fusion(bf16[32,16,2,128]{3,1,2,0:T(8,128)(2,1)S(1)} %gather_fusion.1, bf16[32,128,2,128]{3,2,1,0:T(2,128)(2,1)S(1)} %reshape.275), kind=kOutput, calls=%fused_computation.12 | convolution fusion | flops 33554432 | bytes 2883584 | tf_op jit(solution)/shard_map/pqhd,pshd->pqhs/dot_general | solution.py:61
  40.5 3.3 %copy.103 = f32[32,16,2,128]{0,1,3,2:T(8,128)} copy(f32[32,16,2,128]{3,1,2,0:T(8,128)} %fusion.7) | data formatting | bytes 1048576 | tf_op jit(solution)/shard_map/pqhd,pshd->pqhs/transpose | solution.py:61
  43.8 2.3 %slice.46 = f32[32,16,2,64,1]{0,1,4,3,2:T(8,128)} slice(f32[32,16,2,64,2]{0,1,4,3,2:T(8,128)} %bitcast.90), slice={[0:32], [0:16], [0:2], [0:64], [0:1]} | slice | bytes 524288 | tf_op jit(solution)/shard_map/slice | solution.py:62
  46.1 2.6 %copy.134 = f32[32,16,2,64,1]{3,1,4,2,0:T(8,128)} copy(f32[32,16,2,64,1]{0,1,4,3,2:T(8,128)} %slice.46) | data formatting | bytes 524288
  48.7 1.3 fusion.18
  50.0 0.2 select_reduce_fusion
  50.3 0.6 gather_fusion.2
  50.9 1.3 fusion.30
  52.2 2.1 %fusion.19 = (bf16[32,16,2,64,1]{3,1,2,0,4:T(8,128)(2,1)}, f32[32,16,2]{1,2,0:T(2,128)S(1)}) fusion(bf16[32,16,2,64]{3,1,2,0:T(8,128)(2,1)S(1)} %fusion.30, f32[32,16,2]{1,2,0:T(2,128)S(1)} %gather_fusion.2, f32[32,2,64]{2,1,0:T(2,128)S(1)} %broadcast_multiply_fusion, f32[32,16,2,64,1]{3,1,4,2,0:T(8,128)} %copy.134, pred[32,64]{1,0:T(8,128)(4,1)S(1)} %get-tuple-element.20), kind=kLoop, calls=%fused_computation.29 | loop fusion | flops 588800 | bytes 550912 | tf_op jit(solution)/shard_map/stack | solution.py:74
  54.4 0.9 fusion.60
  55.4 2.4 %copy.136 = bf16[32,16,2,64,1]{0,1,4,3,2:T(8,128)(2,1)} copy(bf16[32,16,2,64,1]{3,1,2,0,4:T(8,128)(2,1)} %get-tuple-element.11) | data formatting | bytes 262144
  57.8 2.2 %stack.15.clone = bf16[32,16,2,64,2]{0,1,4,3,2:T(8,128)(2,1)} pad(bf16[32,16,2,64,1]{0,1,4,3,2:T(8,128)(2,1)} %copy.136, bf16[]{:T(256)} %constant.12.clone.1), padding=0_0x0_0x0_0x0_0x1_0 | pad | bytes 393218 | tf_op jit(solution)/shard_map/stack | solution.py:74
  60.0 2.9 %copy.110 = bf16[32,16,2,128]{3,1,2,0:T(8,128)(2,1)} copy(bf16[32,16,2,128]{0,1,3,2:T(8,128)(2,1)} %bitcast.92) | data formatting | bytes 524288 | tf_op jit(solution)/shard_map/reshape | solution.py:74
  62.9 2.4 %fusion.1 = f32[32,2,16,128]{3,2,1,0:T(8,128)} fusion(bf16[32,16,2,128]{3,1,2,0:T(8,128)(2,1)} %copy.110, bf16[32,128,2,128]{3,2,1,0:T(2,128)(2,1)S(1)} %reshape.275), kind=kOutput, calls=%fused_computation.6 | convolution fusion | flops 33554432 | bytes 2883584 | tf_op jit(solution)/shard_map/pqhs,pshd->pqhd/dot_general | solution.py:80
  65.4 1.4 %copy.135 = bf16[32,16,2,64,1]{0,1,4,3,2:T(8,128)(2,1)} copy(bf16[32,16,2,64,1]{3,1,2,0,4:T(8,128)(2,1)S(1)} %bitcast.93) | data formatting | bytes 262144
  66.7 2.2 %stack.13.clone = bf16[32,16,2,64,2]{0,1,4,3,2:T(8,128)(2,1)} pad(bf16[32,16,2,64,1]{0,1,4,3,2:T(8,128)(2,1)} %copy.135, bf16[]{:T(256)} %constant.12.clone.1), padding=0_0x0_0x0_0x0_0x1_0 | pad | bytes 393218 | tf_op jit(solution)/shard_map/stack | solution.py:74
  69.0 2.3 %copy.107 = bf16[32,16,2,128]{3,1,2,0:T(8,128)(2,1)S(1)} copy(bf16[32,16,2,128]{0,1,3,2:T(8,128)(2,1)} %bitcast.91) | data formatting | bytes 524288 | tf_op jit(solution)/shard_map/reshape | solution.py:74
  71.2 1.7 %fusion.14 = f32[32,16,2,128]{3,1,2,0:T(8,128)S(1)} fusion(f32[32,2,16,128]{3,2,1,0:T(8,128)} %fusion.1, bf16[32,16,2,128]{3,1,2,0:T(8,128)(2,1)S(1)} %copy.107, bf16[32,128,2,128]{3,2,1,0:T(2,128)(2,1)S(1)} %reshape.275), kind=kOutput, calls=%fused_computation.15 | convolution fusion | flops 33685504 | bytes 3407872 | tf_op jit(solution)/shard_map/pqhs,pshd->pqhd/dot_general | solution.py:77
  72.9 0.3 copy.112
  73.2 0.4 reshape.279
  73.7 0.4 fusion.58
  74.1 0.4 fusion.10
  74.7 1.0 maximum_maximum_fusion
  75.8 5.7 %all-to-all-start.1 = ((bf16[64,40,128]{2,1,0:T(8,128)(2,1)}), bf16[64,40,128]{2,1,0:T(8,128)(2,1)S(1)}, u32[]{:S(2)}, u32[]{:S(2)}) async-start(bf16[64,40,128]{2,1,0:T(8,128)(2,1)} %maximum_maximum_fusion), calls=%async_computation.1 | async-start | bytes 1310720 | tf_op jit(solution)/shard_map/all_to_all | solution.py:111
  81.8 2.2 %slice_reduce_fusion = (bf16[16,32,256]{2,1,0:T(8,128)(2,1)S(1)}, bf16[16,32,256]{2,1,0:T(8,128)(2,1)S(1)}) fusion(bf16[16,32,2,256]{3,2,1,0:T(2,128)(2,1)S(1)} %copy-done.2), kind=kLoop, calls=%fused_computation.22 | loop fusion | bytes 1048576 | tf_op jit(solution)/shard_map/slice | solution.py:122
  84.0 0.2 fusion.24
  84.3 17.5 %all-to-all-done.1 = bf16[64,40,128]{2,1,0:T(8,128)(2,1)S(1)} async-done(((bf16[64,40,128]{2,1,0:T(8,128)(2,1)}), bf16[64,40,128]{2,1,0:T(8,128)(2,1)S(1)}, u32[]{:S(2)}, u32[]{:S(2)}) %all-to-all-start.1) | async-done | bytes 655392 | tf_op jit(solution)/shard_map/all_to_all | solution.py:111
  102.9 0.2 fusion.20
  103.5 0.4 multiply_reduce_fusion
  104.0 0.2 convolution_convert_fusion
  104.2 0.8 broadcast_in_dim.72
  105.1 6.8 %all-to-all-start.2 = ((bf16[8,16,2048]{2,1,0:T(8,128)(2,1)}), bf16[8,16,2048]{2,1,0:T(8,128)(2,1)S(1)}, u32[]{:S(2)}, u32[]{:S(2)}) async-start(bf16[8,16,2048]{2,1,0:T(8,128)(2,1)} %broadcast_in_dim.72), calls=%async_computation.2 | async-start | bytes 1048576 | tf_op jit(solution)/shard_map/all_to_all | solution.py:160
  111.9 17.9 %all-to-all-done.2 = bf16[8,16,2048]{2,1,0:T(8,128)(2,1)S(1)} async-done(((bf16[8,16,2048]{2,1,0:T(8,128)(2,1)}), bf16[8,16,2048]{2,1,0:T(8,128)(2,1)S(1)}, u32[]{:S(2)}, u32[]{:S(2)}) %all-to-all-start.2) | async-done | bytes 524320 | tf_op jit(solution)/shard_map/all_to_all | solution.py:160
  130.1 0.6 constant_dynamic-slice_fusion
  130.7 0.7 add_convert_fusion.1
  (80 shorter events, 3.0 us)
Async XLA Ops:
  0.6 103.3 %copy-start = (bf16[256,2048]{1,0:T(8,128)(2,1)S(1)}, bf16[256,2048]{1,0:T(8,128)(2,1)}, u32[]{:S(2)}) copy-start(bf16[256,2048]{1,0:T(8,128)(2,1)} %param.22) | copy-start | bytes 3145732
  2.3 32.7 %all-to-all-start = ((bf16[64,16,256]{2,1,0:T(8,128)(2,1)}), bf16[64,16,256]{2,1,0:T(8,128)(2,1)}, u32[]{:S(2)}, u32[]{:S(2)}) async-start(bf16[64,16,256]{2,1,0:T(8,128)(2,1)} %broadcast_in_dim.62), calls=%async_computation | async-start | bytes 1048576 | tf_op jit(solution)/shard_map/all_to_all | solution.py:52
  20.9 6.1 %copy-start.13 = (s32[16]{0:T(128)S(1)}, s32[16]{0:T(128)}, u32[]{:S(2)}) copy-start(s32[16]{0:T(128)} %param.16) | copy-start | bytes 196
  20.9 6.6 %copy-start.1 = (s32[64]{0:T(128)S(1)}, s32[64]{0:T(128)}, u32[]{:S(2)}) copy-start(s32[64]{0:T(128)} %param.20) | copy-start | bytes 772
  20.9 7.9 %copy-start.5 = (s32[32]{0:T(128)S(1)}, s32[32]{0:T(128)}, u32[]{:S(2)}) copy-start(s32[32]{0:T(128)} %param.18) | copy-start | bytes 388
  20.9 7.9 %copy-start.11 = (s32[32]{0:T(128)S(1)}, s32[32]{0:T(128)}, u32[]{:S(2)}) copy-start(s32[32]{0:T(128)} %param.19) | copy-start | bytes 388
  28.8 11.7 %copy-start.7 = (pred[32]{0:T(512)(128)(4,1)}, pred[32]{0:T(512)(128)(4,1)S(1)}, u32[]{:S(2)}) copy-start(pred[32]{0:T(512)(128)(4,1)S(1)} %broadcast_compare_fusion) | copy-start | bytes 100
  72.9 0.8 copy-start.6
  72.9 0.8 copy-start.8
  73.7 1.0 copy-start.12
  74.6 7.2 %copy-start.14 = (s32[16]{0:T(128)S(1)}, s32[16]{0:T(128)}, u32[]{:S(2)}) copy-start(s32[16]{0:T(128)} %param.16) | copy-start | bytes 196
  74.6 7.2 %copy-start.2 = (bf16[16,32,2,256]{3,2,1,0:T(2,128)(2,1)S(1)}, bf16[16,32,2,256]{3,2,1,0:T(2,128)(2,1)}, u32[]{:S(2)}) copy-start(bf16[16,32,2,256]{3,2,1,0:T(2,128)(2,1)} %param.15) | copy-start | bytes 1572868
  74.7 9.3 %copy-start.4 = (bf16[16,2,128,1]{2,3,1,0:T(2,128)(2,1)S(1)}, bf16[16,2,128,1]{2,3,1,0:T(2,128)(2,1)}, u32[]{:S(2)}) copy-start(bf16[16,2,128,1]{2,3,1,0:T(2,128)(2,1)} %reshape.322) | copy-start | bytes 24580
  74.7 27.4 %copy-start.10 = (f32[16]{0:T(128)S(1)}, f32[16]{0:T(128)}, u32[]{:S(2)}) copy-start(f32[16]{0:T(128)} %convert_element_type.148) | copy-start | bytes 196
  75.8 26.1 %all-to-all-start.1 = ((bf16[64,40,128]{2,1,0:T(8,128)(2,1)}), bf16[64,40,128]{2,1,0:T(8,128)(2,1)S(1)}, u32[]{:S(2)}, u32[]{:S(2)}) async-start(bf16[64,40,128]{2,1,0:T(8,128)(2,1)} %maximum_maximum_fusion), calls=%async_computation.1 | async-start | bytes 1310720 | tf_op jit(solution)/shard_map/all_to_all | solution.py:111
  102.7 9.2 %copy-start.9 = (bf16[2048]{0:T(1024)(128)(2,1)S(1)}, bf16[2048]{0:T(1024)(128)(2,1)}, u32[]{:S(2)}) copy-start(bf16[2048]{0:T(1024)(128)(2,1)} %param.23) | copy-start | bytes 12292
  102.7 9.2 %copy-start.15 = (bf16[256]{0:T(256)(128)(2,1)S(1)}, bf16[256]{0:T(256)(128)(2,1)}, u32[]{:S(2)}) copy-start(bf16[256]{0:T(256)(128)(2,1)} %param.25) | copy-start | bytes 1540
  102.7 9.2 %copy-start.16 = (bf16[256]{0:T(256)(128)(2,1)S(1)}, bf16[256]{0:T(256)(128)(2,1)}, u32[]{:S(2)}) copy-start(bf16[256]{0:T(256)(128)(2,1)} %param.24) | copy-start | bytes 1540
  103.1 26.8 %copy-start.3 = (bf16[16,2048]{1,0:T(8,128)(2,1)S(1)}, bf16[16,2048]{1,0:T(8,128)(2,1)}, u32[]{:S(2)}) copy-start(bf16[16,2048]{1,0:T(8,128)(2,1)} %param.21) | copy-start | bytes 196612
  105.1 24.8 %all-to-all-start.2 = ((bf16[8,16,2048]{2,1,0:T(8,128)(2,1)}), bf16[8,16,2048]{2,1,0:T(8,128)(2,1)S(1)}, u32[]{:S(2)}, u32[]{:S(2)}) async-start(bf16[8,16,2048]{2,1,0:T(8,128)(2,1)} %broadcast_in_dim.72), calls=%async_computation.2 | async-start | bytes 1048576 | tf_op jit(solution)/shard_map/all_to_all | solution.py:160

commit v10 on v4

--- a/solution.py
+++ b/solution.py
@@ -52,7 +52,11 @@
     everyone = lax.all_to_all(copies, "req", 0, 0, tiled=True)
     by_group = everyone.reshape(group_count, row_count, heads_here, HEAD)
     safe_group = jnp.clip(page_group, 0, group_count - 1)
-    page_queries = by_group[safe_group]
+    member = (page_group[:, None] == jnp.arange(group_count)[None, :]) & (page_group[:, None] >= 0)
+    pick = member.astype(jnp.bfloat16)
+    page_queries = jnp.dot(
+        pick, everyone.reshape(group_count, -1), preferred_element_type=f32
+    ).astype(jnp.bfloat16).reshape(page_count, row_count, heads_here, HEAD)
     page_keys = pool_cache[:, :, 0].reshape(page_count, PAGE, heads_here, HEAD)
     page_values = pool_cache[:, :, 1].reshape(page_count, PAGE, heads_here, HEAD)
     prompt_here = prompt_len[safe_group]
@@ -66,11 +70,12 @@
     scores = scores + slopes[None, None, :, None] * offsets[:, None, None, :]
     scores = jnp.where(usable[:, None, None, :], scores, masked_score)
 
-    member = (page_group[:, None] == jnp.arange(group_count)[None, :]) & (page_group[:, None] >= 0)
     page_top = scores.max(-1)
     local_top = jnp.where(member[:, :, None, None], page_top[:, None], masked_score).max(0)
     local_top = local_top.astype(jnp.bfloat16)
-    page_ref = local_top.astype(f32)[safe_group]
+    page_ref = jnp.dot(
+        pick, local_top.reshape(group_count, -1), preferred_element_type=f32
+    ).reshape(page_count, row_count, heads_here)
     weights = jnp.where(usable[:, None, None, :], jnp.exp(scores - page_ref[..., None]), 0.0)
     page_totals = weights.sum(-1)
     upper_part, lower_part = split_halves(weights)

time: 99.1 us -> 98.6 us (level)
  local copies, waits for them, and re-layouts: 20.9 us -> 19.9 us
    gather x2 -> x0, local copies, waits for them, and re-layouts: 1.21 us -> none  [the longest x1 0.61 us: local(): page_ref = local_top.astype(f32)[safe_group]]
where the time goes in v10:
time: 98.6 us; the launch traced here: 98.2 us
  waiting for transfers between devices  40.2 us (41%)
  starting transfers between devices  27.4 us (28%)
  local copies, waits for them, and re-layouts  19.9 us (20%)
  matrix products  5.23 us (5%)
  other arithmetic  4.35 us (4%)
  between operations  1.07 us (1%)
    all_to_all x1, waiting for transfers between devices, local(): gathered = lax.all_to_all(partial_copies, 'tp', 0, 0, tiled=True)  17.9 us
    all_to_all x1, waiting for transfers between devices, local(): arrived = lax.all_to_all(packed, 'req', 0, 0, tiled=True)  17.5 us
    all_to_all x1, starting transfers between devices, local(): everyone = lax.all_to_all(copies, 'req', 0, 0, tiled=True)  14.8 us
    slice x1, local copies, waits for them, and re-layouts, local(): pool_cache[:, :, 1].reshape(page_count, PAGE, heads_here, HEAD)  11.7 us
    all_to_all x1, starting transfers between devices, local(): gathered = lax.all_to_all(partial_copies, 'tp', 0, 0, tiled=True)  6.82 us
    all_to_all x1, starting transfers between devices, local(): arrived = lax.all_to_all(packed, 'req', 0, 0, tiled=True)  5.73 us
    all_to_all x1, waiting for transfers between devices, local(): everyone = lax.all_to_all(copies, 'req', 0, 0, tiled=True)  4.8 us
    slice x1, local copies, waits for them, and re-layouts, local(): tail_cache[:, :, 1].reshape(row_count, tail_slots, heads_here, HEAD)  2.17 us
  transfers between devices with their start and end apart: 3, of which 3 were waited for; matrix products, arithmetic and copies ran while one was open for 16% of the time, Pallas kernels for 0%

profile of v10, /device:TPU:1, one launch (start us, length us, event | category | flops | bytes accessed | tf_op | source)
XLA Modules:
  0.0 98.2 jit_solution(10765641238959267347)
XLA Ops:
  0.7 1.6 %broadcast_in_dim.65 = bf16[64,16,256]{2,1,0:T(8,128)(2,1)} broadcast(bf16[16,256]{1,0:T(8,128)(2,1)} %param.13), dimensions={1,2} | broadcast | bytes 532480 | tf_op jit(solution)/shard_map/broadcast_in_dim | solution.py:51
  2.3 14.8 %all-to-all-start = ((bf16[64,16,256]{2,1,0:T(8,128)(2,1)}), bf16[64,16,256]{2,1,0:T(8,128)(2,1)S(1)}, u32[]{:S(2)}, u32[]{:S(2)}) async-start(bf16[64,16,256]{2,1,0:T(8,128)(2,1)} %broadcast_in_dim.65), calls=%async_computation | async-start | bytes 1048576 | tf_op jit(solution)/shard_map/all_to_all | solution.py:52
  17.2 0.7 gather_fusion
  18.0 0.1 fusion.42
  18.4 11.7 %slice_reduce_fusion = (bf16[32,64,256]{2,1,0:T(8,128)(2,1)S(1)}, bf16[32,64,256]{2,1,0:T(8,128)(2,1)}) fusion(bf16[32,64,2,256]{3,2,1,0:T(2,128)(2,1)} %param.17), kind=kLoop, calls=%fused_computation.5 | loop fusion | bytes 4194304 | tf_op jit(solution)/shard_map/slice | solution.py:61
  30.1 4.8 %all-to-all-done = bf16[64,16,256]{2,1,0:T(8,128)(2,1)S(1)} async-done(((bf16[64,16,256]{2,1,0:T(8,128)(2,1)}), bf16[64,16,256]{2,1,0:T(8,128)(2,1)S(1)}, u32[]{:S(2)}, u32[]{:S(2)}) %all-to-all-start) | async-done | bytes 524320 | tf_op jit(solution)/shard_map/all_to_all | solution.py:52
  34.9 0.2 copy.69
  35.1 0.3 convolution_convert_fusion
  35.3 0.2 reshape.271
  35.5 2.0 %fusion.64 = (bf16[32,16,2]{1,2,0:T(2,128)(2,1)S(1)}, f32[32,16,2,64]{3,1,2,0:T(8,128)S(1)}) fusion(f32[32,2,64]{2,1,0:T(2,128)S(1)} %broadcast_multiply_fusion, bf16[32,16,2,128]{3,2,1,0:T(2,128)(2,1)S(1)} %reshape.271, pred[32,64]{1,0:T(8,128)(4,1)S(1)} %get-tuple-element.24, bf16[32,64,256]{2,1,0:T(8,128)(2,1)} %get-tuple-element.3), kind=kOutput, calls=%fused_computation.112 | convolution fusion | flops 17038336 | bytes 1593344 | tf_op jit(solution)/shard_map/pqhd,pshd->pqhs/dot_general | solution.py:67
  37.5 0.2 select_reduce_fusion
  37.7 0.2 fusion.44
  37.9 0.1 copy.41
  38.0 0.4 fusion.14
  38.5 0.4 fusion.7
  38.9 0.5 fusion.1
  39.3 0.3 copy.44
  39.6 0.4 reshape.273
  40.1 0.4 fusion.59
  40.5 0.4 fusion.4
  40.9 0.1 copy.70
  41.1 0.2 fusion.65
  41.4 0.1 copy.46
  41.5 1.0 %maximum_maximum_fusion = bf16[64,40,128]{2,1,0:T(8,128)(2,1)} fusion(bf16[64,1,128]{2,1,0:T(2,128)(2,1)S(1)} %copy.46, bf16[64,32,128]{2,1,0:T(8,128)(2,1)S(1)} %bitcast.96, bf16[40]{0:T(256)(128)(2,1)S(1)} %pad.7.clone), kind=kLoop, calls=%fused_computation.23 | loop fusion | flops 1966080 | bytes 1196112 | tf_op jit(solution)/shard_map/concatenate | solution.py:106
  42.5 5.7 %all-to-all-start.1 = ((bf16[64,40,128]{2,1,0:T(8,128)(2,1)}), bf16[64,40,128]{2,1,0:T(8,128)(2,1)S(1)}, u32[]{:S(2)}, u32[]{:S(2)}) async-start(bf16[64,40,128]{2,1,0:T(8,128)(2,1)} %maximum_maximum_fusion), calls=%async_computation.1 | async-start | bytes 1310720 | tf_op jit(solution)/shard_map/all_to_all | solution.py:114
  48.3 0.1 fusion.36
  48.6 2.2 %slice_reduce_fusion.2 = (bf16[16,32,256]{2,1,0:T(8,128)(2,1)S(1)}, bf16[16,32,256]{2,1,0:T(8,128)(2,1)S(1)}) fusion(bf16[16,32,2,256]{3,2,1,0:T(2,128)(2,1)S(1)} %copy-done.2), kind=kLoop, calls=%fused_computation.24 | loop fusion | bytes 1048576 | tf_op jit(solution)/shard_map/slice | solution.py:125
  50.8 0.2 fusion.19
  51.0 0.1 fusion.53
  51.1 17.5 %all-to-all-done.1 = bf16[64,40,128]{2,1,0:T(8,128)(2,1)S(1)} async-done(((bf16[64,40,128]{2,1,0:T(8,128)(2,1)}), bf16[64,40,128]{2,1,0:T(8,128)(2,1)S(1)}, u32[]{:S(2)}, u32[]{:S(2)}) %all-to-all-start.1) | async-done | bytes 655392 | tf_op jit(solution)/shard_map/all_to_all | solution.py:114
  68.9 0.1 fusion.48
  69.0 0.1 copy.48
  69.1 0.2 fusion.47
  69.2 0.1 sub.78
  69.3 0.1 fusion.35
  69.5 0.1 copy.50
  69.7 0.1 copy.49
  69.9 0.2 fusion.15
  70.1 0.2 fusion.17
  70.2 0.3 multiply_reduce_fusion
  70.6 0.1 fusion.46
  70.7 0.2 convolution_convert_fusion.1
  71.0 0.8 broadcast_in_dim.116
  71.8 6.8 %all-to-all-start.2 = ((bf16[8,16,2048]{2,1,0:T(8,128)(2,1)}), bf16[8,16,2048]{2,1,0:T(8,128)(2,1)S(1)}, u32[]{:S(2)}, u32[]{:S(2)}) async-start(bf16[8,16,2048]{2,1,0:T(8,128)(2,1)} %broadcast_in_dim.116), calls=%async_computation.2 | async-start | bytes 1048576 | tf_op jit(solution)/shard_map/all_to_all | solution.py:163
  78.7 17.9 %all-to-all-done.2 = bf16[8,16,2048]{2,1,0:T(8,128)(2,1)S(1)} async-done(((bf16[8,16,2048]{2,1,0:T(8,128)(2,1)}), bf16[8,16,2048]{2,1,0:T(8,128)(2,1)S(1)}, u32[]{:S(2)}, u32[]{:S(2)}) %all-to-all-start.2) | async-done | bytes 524320 | tf_op jit(solution)/shard_map/all_to_all | solution.py:163
  96.7 0.2 fusion.55
  96.9 0.6 constant_dynamic-slice_fusion
  97.5 0.7 add_convert_fusion.1
  (60 shorter events, 1.4 us)
Async XLA Ops:
  0.6 70.1 %copy-start = (bf16[256,2048]{1,0:T(8,128)(2,1)S(1)}, bf16[256,2048]{1,0:T(8,128)(2,1)}, u32[]{:S(2)}) copy-start(bf16[256,2048]{1,0:T(8,128)(2,1)} %param.22) | copy-start | bytes 3145732
  0.6 17.6 %copy-start.4 = (bf16[16,256]{1,0:T(8,128)(2,1)S(1)}, bf16[16,256]{1,0:T(8,128)(2,1)}, u32[]{:S(2)}) copy-start(bf16[16,256]{1,0:T(8,128)(2,1)} %param.13) | copy-start | bytes 24580
  0.7 16.5 %copy-start.6 = (s32[32]{0:T(128)S(1)}, s32[32]{0:T(128)}, u32[]{:S(2)}) copy-start(s32[32]{0:T(128)} %param.18) | copy-start | bytes 388
  0.7 16.6 %copy-start.1 = (s32[64]{0:T(128)S(1)}, s32[64]{0:T(128)}, u32[]{:S(2)}) copy-start(s32[64]{0:T(128)} %param.20) | copy-start | bytes 772
  0.7 17.3 %copy-start.8 = (s32[32]{0:T(128)S(1)}, s32[32]{0:T(128)}, u32[]{:S(2)}) copy-start(s32[32]{0:T(128)} %param.19) | copy-start | bytes 388
  0.7 17.4 %copy-start.5 = (bf16[16,2,256]{2,1,0:T(2,128)(2,1)S(1)}, bf16[16,2,256]{2,1,0:T(2,128)(2,1)}, u32[]{:S(2)}) copy-start(bf16[16,2,256]{2,1,0:T(2,128)(2,1)} %param.14) | copy-start | bytes 49156
  2.3 32.6 %all-to-all-start = ((bf16[64,16,256]{2,1,0:T(8,128)(2,1)}), bf16[64,16,256]{2,1,0:T(8,128)(2,1)S(1)}, u32[]{:S(2)}, u32[]{:S(2)}) async-start(bf16[64,16,256]{2,1,0:T(8,128)(2,1)} %broadcast_in_dim.65), calls=%async_computation | async-start | bytes 1048576 | tf_op jit(solution)/shard_map/all_to_all | solution.py:52
  41.4 7.1 %copy-start.9 = (s32[16]{0:T(128)S(1)}, s32[16]{0:T(128)}, u32[]{:S(2)}) copy-start(s32[16]{0:T(128)} %param.16) | copy-start | bytes 196
  41.4 7.2 %copy-start.2 = (bf16[16,32,2,256]{3,2,1,0:T(2,128)(2,1)S(1)}, bf16[16,32,2,256]{3,2,1,0:T(2,128)(2,1)}, u32[]{:S(2)}) copy-start(bf16[16,32,2,256]{3,2,1,0:T(2,128)(2,1)} %param.15) | copy-start | bytes 1572868
  42.5 26.1 %all-to-all-start.1 = ((bf16[64,40,128]{2,1,0:T(8,128)(2,1)}), bf16[64,40,128]{2,1,0:T(8,128)(2,1)S(1)}, u32[]{:S(2)}, u32[]{:S(2)}) async-start(bf16[64,40,128]{2,1,0:T(8,128)(2,1)} %maximum_maximum_fusion), calls=%async_computation.1 | async-start | bytes 1310720 | tf_op jit(solution)/shard_map/all_to_all | solution.py:114
  70.7 8.0 %copy-start.7 = (bf16[2048]{0:T(1024)(128)(2,1)S(1)}, bf16[2048]{0:T(1024)(128)(2,1)}, u32[]{:S(2)}) copy-start(bf16[2048]{0:T(1024)(128)(2,1)} %param.23) | copy-start | bytes 12292
  70.7 8.0 %copy-start.10 = (bf16[256]{0:T(256)(128)(2,1)S(1)}, bf16[256]{0:T(256)(128)(2,1)}, u32[]{:S(2)}) copy-start(bf16[256]{0:T(256)(128)(2,1)} %param.24) | copy-start | bytes 1540
  70.7 8.0 %copy-start.11 = (bf16[256]{0:T(256)(128)(2,1)S(1)}, bf16[256]{0:T(256)(128)(2,1)}, u32[]{:S(2)}) copy-start(bf16[256]{0:T(256)(128)(2,1)} %param.25) | copy-start | bytes 1540
  71.0 25.7 %copy-start.3 = (bf16[16,2048]{1,0:T(8,128)(2,1)S(1)}, bf16[16,2048]{1,0:T(8,128)(2,1)}, u32[]{:S(2)}) copy-start(bf16[16,2048]{1,0:T(8,128)(2,1)} %param.21) | copy-start | bytes 196612
  71.8 24.8 %all-to-all-start.2 = ((bf16[8,16,2048]{2,1,0:T(8,128)(2,1)}), bf16[8,16,2048]{2,1,0:T(8,128)(2,1)S(1)}, u32[]{:S(2)}, u32[]{:S(2)}) async-start(bf16[8,16,2048]{2,1,0:T(8,128)(2,1)} %broadcast_in_dim.116), calls=%async_computation.2 | async-start | bytes 1048576 | tf_op jit(solution)/shard_map/all_to_all | solution.py:163

commit v11 on v10

--- a/solution.py
+++ b/solution.py
@@ -83,10 +83,12 @@
     page_accum = page_accum + jnp.einsum(
         "pqhs,pshd->pqhd", lower_part, page_values, preferred_element_type=f32
     )
-    accum_upper, accum_lower = split_halves(page_accum.reshape(page_count, -1))
+    accum_upper, accum_lower = split_halves(page_accum)
     spread = member.T.astype(jnp.bfloat16)
-    group_accum = jnp.dot(spread, accum_upper, preferred_element_type=f32)
-    group_accum = group_accum + jnp.dot(spread, accum_lower, preferred_element_type=f32)
+    group_accum = jnp.einsum("gp,pqhd->gqhd", spread, accum_upper, preferred_element_type=f32)
+    group_accum = group_accum + jnp.einsum(
+        "gp,pqhd->gqhd", spread, accum_lower, preferred_element_type=f32
+    )
     group_totals = jnp.dot(
         member.T.astype(f32), page_totals.reshape(page_count, -1), precision=highest
     )
@@ -101,7 +103,7 @@
         axis=1,
     )
     lanes = 128
-    accum_rows = group_accum.shape[1] // lanes
+    accum_rows = row_count * feat_width // lanes
     stats = jnp.pad(stats, ((0, 0), (0, lanes - stats.shape[1])))
     packed = jnp.concatenate(
         [

time: 98.6 us -> 98.2 us (level)
  no operation moved by 1% of the time
where the time goes in v11:
time: 98.2 us; the launch traced here: 97.8 us
  waiting for transfers between devices  40.2 us (41%)
  starting transfers between devices  27.4 us (28%)
  local copies, waits for them, and re-layouts  19.5 us (20%)
  matrix products  5.24 us (5%)
  other arithmetic  4.39 us (4%)
  between operations  1.05 us (1%)
    all_to_all x1, waiting for transfers between devices, local(): gathered = lax.all_to_all(partial_copies, 'tp', 0, 0, tiled=True)  17.9 us
    all_to_all x1, waiting for transfers between devices, local(): arrived = lax.all_to_all(packed, 'req', 0, 0, tiled=True)  17.5 us
    all_to_all x1, starting transfers between devices, local(): everyone = lax.all_to_all(copies, 'req', 0, 0, tiled=True)  14.8 us
    slice x1, local copies, waits for them, and re-layouts, local(): pool_cache[:, :, 1].reshape(page_count, PAGE, heads_here, HEAD)  11.7 us
    all_to_all x1, starting transfers between devices, local(): gathered = lax.all_to_all(partial_copies, 'tp', 0, 0, tiled=True)  6.82 us
    all_to_all x1, starting transfers between devices, local(): arrived = lax.all_to_all(packed, 'req', 0, 0, tiled=True)  5.73 us
    all_to_all x1, waiting for transfers between devices, local(): everyone = lax.all_to_all(copies, 'req', 0, 0, tiled=True)  4.8 us
    slice x1, local copies, waits for them, and re-layouts, local(): tail_cache[:, :, 1].reshape(row_count, tail_slots, heads_here, HEAD)  2.17 us
  transfers between devices with their start and end apart: 3, of which 3 were waited for; matrix products, arithmetic and copies ran while one was open for 16% of the time, Pallas kernels for 0%

profile of v11, /device:TPU:1, one launch (start us, length us, event | category | flops | bytes accessed | tf_op | source)
XLA Modules:
  0.0 97.8 jit_solution(5915392027952639775)
XLA Ops:
  0.7 1.6 %broadcast_in_dim.65 = bf16[64,16,256]{2,1,0:T(8,128)(2,1)} broadcast(bf16[16,256]{1,0:T(8,128)(2,1)} %param.13), dimensions={1,2} | broadcast | bytes 532480 | tf_op jit(solution)/shard_map/broadcast_in_dim | solution.py:51
  2.3 14.8 %all-to-all-start = ((bf16[64,16,256]{2,1,0:T(8,128)(2,1)}), bf16[64,16,256]{2,1,0:T(8,128)(2,1)S(1)}, u32[]{:S(2)}, u32[]{:S(2)}) async-start(bf16[64,16,256]{2,1,0:T(8,128)(2,1)} %broadcast_in_dim.65), calls=%async_computation | async-start | bytes 1048576 | tf_op jit(solution)/shard_map/all_to_all | solution.py:52
  17.2 0.7 gather_fusion
  18.0 0.1 fusion.44
  18.4 11.7 %slice_reduce_fusion = (bf16[32,64,256]{2,1,0:T(8,128)(2,1)S(1)}, bf16[32,64,256]{2,1,0:T(8,128)(2,1)}) fusion(bf16[32,64,2,256]{3,2,1,0:T(2,128)(2,1)} %param.17), kind=kLoop, calls=%fused_computation.3 | loop fusion | bytes 4194304 | tf_op jit(solution)/shard_map/slice | solution.py:61
  30.1 4.8 %all-to-all-done = bf16[64,16,256]{2,1,0:T(8,128)(2,1)S(1)} async-done(((bf16[64,16,256]{2,1,0:T(8,128)(2,1)}), bf16[64,16,256]{2,1,0:T(8,128)(2,1)S(1)}, u32[]{:S(2)}, u32[]{:S(2)}) %all-to-all-start) | async-done | bytes 524320 | tf_op jit(solution)/shard_map/all_to_all | solution.py:52
  34.9 0.2 copy.79
  35.1 0.3 convolution_convert_fusion
  35.3 0.2 reshape.268
  35.5 2.0 %fusion.67 = (bf16[32,16,2]{1,2,0:T(2,128)(2,1)S(1)}, f32[32,16,2,64]{3,1,2,0:T(8,128)S(1)}) fusion(f32[32,2,64]{2,1,0:T(2,128)S(1)} %broadcast_multiply_fusion, bf16[32,16,2,128]{3,2,1,0:T(2,128)(2,1)S(1)} %reshape.268, pred[32,64]{1,0:T(8,128)(4,1)S(1)} %get-tuple-element.24, bf16[32,64,256]{2,1,0:T(8,128)(2,1)} %get-tuple-element.3), kind=kOutput, calls=%fused_computation.115 | convolution fusion | flops 17038336 | bytes 1593344 | tf_op jit(solution)/shard_map/pqhd,pshd->pqhs/dot_general | solution.py:67
  37.5 0.2 select_reduce_fusion
  37.7 0.2 fusion.48
  37.9 0.1 copy.48
  38.0 0.4 fusion.13
  38.5 0.4 fusion.6
  38.9 0.5 fusion.69
  39.3 0.4 fusion.22
  39.9 0.4 fusion
  40.3 0.3 copy.54
  40.7 0.2 fusion.68
  41.0 0.1 copy.55
  41.1 1.0 %maximum_maximum_fusion = bf16[64,40,128]{2,1,0:T(8,128)(2,1)} fusion(bf16[64,1,128]{2,1,0:T(2,128)(2,1)S(1)} %copy.55, bf16[64,32,128]{2,1,0:T(8,128)(2,1)S(1)} %copy.54, bf16[40]{0:T(256)(128)(2,1)S(1)} %pad.7.clone), kind=kLoop, calls=%fused_computation.22 | loop fusion | flops 1966080 | bytes 1196112 | tf_op jit(solution)/shard_map/concatenate | solution.py:108
  42.1 5.7 %all-to-all-start.1 = ((bf16[64,40,128]{2,1,0:T(8,128)(2,1)}), bf16[64,40,128]{2,1,0:T(8,128)(2,1)S(1)}, u32[]{:S(2)}, u32[]{:S(2)}) async-start(bf16[64,40,128]{2,1,0:T(8,128)(2,1)} %maximum_maximum_fusion), calls=%async_computation.1 | async-start | bytes 1310720 | tf_op jit(solution)/shard_map/all_to_all | solution.py:116
  47.9 0.1 fusion.38
  48.2 2.2 %slice_reduce_fusion.2 = (bf16[16,32,256]{2,1,0:T(8,128)(2,1)S(1)}, bf16[16,32,256]{2,1,0:T(8,128)(2,1)S(1)}) fusion(bf16[16,32,2,256]{3,2,1,0:T(2,128)(2,1)S(1)} %copy-done.2), kind=kLoop, calls=%fused_computation.23 | loop fusion | bytes 1048576 | tf_op jit(solution)/shard_map/slice | solution.py:127
  50.4 0.2 fusion.18
  50.6 0.1 fusion.57
  50.7 17.5 %all-to-all-done.1 = bf16[64,40,128]{2,1,0:T(8,128)(2,1)S(1)} async-done(((bf16[64,40,128]{2,1,0:T(8,128)(2,1)}), bf16[64,40,128]{2,1,0:T(8,128)(2,1)S(1)}, u32[]{:S(2)}, u32[]{:S(2)}) %all-to-all-start.1) | async-done | bytes 655392 | tf_op jit(solution)/shard_map/all_to_all | solution.py:116
  68.3 0.1 copy.56
  68.5 0.1 fusion.52
  68.6 0.1 copy.57
  68.7 0.2 fusion.51
  68.8 0.1 sub.78
  68.9 0.1 fusion.37
  69.1 0.1 copy.59
  69.3 0.1 copy.58
  69.4 0.1 copy.60
  69.5 0.2 fusion.14
  69.7 0.2 fusion.16
  69.8 0.3 multiply_reduce_fusion
  70.2 0.1 fusion.50
  70.3 0.2 convolution_convert_fusion.1
  70.6 0.8 broadcast_in_dim.116
  71.4 6.8 %all-to-all-start.2 = ((bf16[8,16,2048]{2,1,0:T(8,128)(2,1)}), bf16[8,16,2048]{2,1,0:T(8,128)(2,1)S(1)}, u32[]{:S(2)}, u32[]{:S(2)}) async-start(bf16[8,16,2048]{2,1,0:T(8,128)(2,1)} %broadcast_in_dim.116), calls=%async_computation.2 | async-start | bytes 1048576 | tf_op jit(solution)/shard_map/all_to_all | solution.py:165
  78.3 17.9 %all-to-all-done.2 = bf16[8,16,2048]{2,1,0:T(8,128)(2,1)S(1)} async-done(((bf16[8,16,2048]{2,1,0:T(8,128)(2,1)}), bf16[8,16,2048]{2,1,0:T(8,128)(2,1)S(1)}, u32[]{:S(2)}, u32[]{:S(2)}) %all-to-all-start.2) | async-done | bytes 524320 | tf_op jit(solution)/shard_map/all_to_all | solution.py:165
  96.3 0.2 fusion.59
  96.5 0.6 constant_dynamic-slice_fusion
  97.1 0.7 add_convert_fusion.1
  (58 shorter events, 1.3 us)
Async XLA Ops:
  0.6 69.7 %copy-start = (bf16[256,2048]{1,0:T(8,128)(2,1)S(1)}, bf16[256,2048]{1,0:T(8,128)(2,1)}, u32[]{:S(2)}) copy-start(bf16[256,2048]{1,0:T(8,128)(2,1)} %param.22) | copy-start | bytes 3145732
  0.6 17.6 %copy-start.4 = (bf16[16,256]{1,0:T(8,128)(2,1)S(1)}, bf16[16,256]{1,0:T(8,128)(2,1)}, u32[]{:S(2)}) copy-start(bf16[16,256]{1,0:T(8,128)(2,1)} %param.13) | copy-start | bytes 24580
  0.7 16.5 %copy-start.6 = (s32[32]{0:T(128)S(1)}, s32[32]{0:T(128)}, u32[]{:S(2)}) copy-start(s32[32]{0:T(128)} %param.18) | copy-start | bytes 388
  0.7 16.6 %copy-start.1 = (s32[64]{0:T(128)S(1)}, s32[64]{0:T(128)}, u32[]{:S(2)}) copy-start(s32[64]{0:T(128)} %param.20) | copy-start | bytes 772
  0.7 17.3 %copy-start.8 = (s32[32]{0:T(128)S(1)}, s32[32]{0:T(128)}, u32[]{:S(2)}) copy-start(s32[32]{0:T(128)} %param.19) | copy-start | bytes 388
  0.7 17.4 %copy-start.5 = (bf16[16,2,256]{2,1,0:T(2,128)(2,1)S(1)}, bf16[16,2,256]{2,1,0:T(2,128)(2,1)}, u32[]{:S(2)}) copy-start(bf16[16,2,256]{2,1,0:T(2,128)(2,1)} %param.14) | copy-start | bytes 49156
  2.3 32.6 %all-to-all-start = ((bf16[64,16,256]{2,1,0:T(8,128)(2,1)}), bf16[64,16,256]{2,1,0:T(8,128)(2,1)S(1)}, u32[]{:S(2)}, u32[]{:S(2)}) async-start(bf16[64,16,256]{2,1,0:T(8,128)(2,1)} %broadcast_in_dim.65), calls=%async_computation | async-start | bytes 1048576 | tf_op jit(solution)/shard_map/all_to_all | solution.py:52
  41.0 7.1 %copy-start.9 = (s32[16]{0:T(128)S(1)}, s32[16]{0:T(128)}, u32[]{:S(2)}) copy-start(s32[16]{0:T(128)} %param.16) | copy-start | bytes 196
  41.0 7.2 %copy-start.2 = (bf16[16,32,2,256]{3,2,1,0:T(2,128)(2,1)S(1)}, bf16[16,32,2,256]{3,2,1,0:T(2,128)(2,1)}, u32[]{:S(2)}) copy-start(bf16[16,32,2,256]{3,2,1,0:T(2,128)(2,1)} %param.15) | copy-start | bytes 1572868
  42.1 26.1 %all-to-all-start.1 = ((bf16[64,40,128]{2,1,0:T(8,128)(2,1)}), bf16[64,40,128]{2,1,0:T(8,128)(2,1)S(1)}, u32[]{:S(2)}, u32[]{:S(2)}) async-start(bf16[64,40,128]{2,1,0:T(8,128)(2,1)} %maximum_maximum_fusion), calls=%async_computation.1 | async-start | bytes 1310720 | tf_op jit(solution)/shard_map/all_to_all | solution.py:116
  70.3 8.0 %copy-start.7 = (bf16[2048]{0:T(1024)(128)(2,1)S(1)}, bf16[2048]{0:T(1024)(128)(2,1)}, u32[]{:S(2)}) copy-start(bf16[2048]{0:T(1024)(128)(2,1)} %param.23) | copy-start | bytes 12292
  70.3 8.0 %copy-start.10 = (bf16[256]{0:T(256)(128)(2,1)S(1)}, bf16[256]{0:T(256)(128)(2,1)}, u32[]{:S(2)}) copy-start(bf16[256]{0:T(256)(128)(2,1)} %param.24) | copy-start | bytes 1540
  70.3 8.0 %copy-start.11 = (bf16[256]{0:T(256)(128)(2,1)S(1)}, bf16[256]{0:T(256)(128)(2,1)}, u32[]{:S(2)}) copy-start(bf16[256]{0:T(256)(128)(2,1)} %param.25) | copy-start | bytes 1540
  70.6 25.7 %copy-start.3 = (bf16[16,2048]{1,0:T(8,128)(2,1)S(1)}, bf16[16,2048]{1,0:T(8,128)(2,1)}, u32[]{:S(2)}) copy-start(bf16[16,2048]{1,0:T(8,128)(2,1)} %param.21) | copy-start | bytes 196612
  71.4 24.8 %all-to-all-start.2 = ((bf16[8,16,2048]{2,1,0:T(8,128)(2,1)}), bf16[8,16,2048]{2,1,0:T(8,128)(2,1)S(1)}, u32[]{:S(2)}, u32[]{:S(2)}) async-start(bf16[8,16,2048]{2,1,0:T(8,128)(2,1)} %broadcast_in_dim.116), calls=%async_computation.2 | async-start | bytes 1048576 | tf_op jit(solution)/shard_map/all_to_all | solution.py:165

commit v12 on v11

--- a/solution.py
+++ b/solution.py
@@ -155,13 +155,13 @@
         jnp.bfloat16
     )
     attention = attention.reshape(row_count, feat_width)
-    partial_value = jnp.dot(attention, out_weight, preferred_element_type=f32)
     model_width = residual.shape[1]
     own_start = lax.axis_index("tp") * feat_width
     tp_size = lax.axis_size("tp")
-    partial_copies = jnp.broadcast_to(
-        partial_value.astype(jnp.bfloat16)[None], (tp_size,) + partial_value.shape
-    )
+    attention_copies = jnp.broadcast_to(attention[None], (tp_size,) + attention.shape)
+    partial_copies = jnp.einsum(
+        "kqi,ij->kqj", attention_copies, out_weight, preferred_element_type=f32
+    ).astype(jnp.bfloat16)
     gathered = lax.all_to_all(partial_copies, "tp", 0, 0, tiled=True)
     projected = gathered.astype(f32).sum(0) + out_bias.astype(f32)[None, :]
     attention_full = projected.astype(jnp.bfloat16)

time: 98.2 us -> 98.2 us (level)
  no operation moved by 1% of the time
where the time goes in v12:
time: 98.2 us; the launch traced here: 97.8 us
  waiting for transfers between devices  40.2 us (41%)
  starting transfers between devices  27.4 us (28%)
  local copies, waits for them, and re-layouts  18.7 us (19%)
  matrix products  6.09 us (6%)
  other arithmetic  4.39 us (4%)
  between operations  1.06 us (1%)
    all_to_all x1, waiting for transfers between devices, local(): gathered = lax.all_to_all(partial_copies, 'tp', 0, 0, tiled=True)  17.9 us
    all_to_all x1, waiting for transfers between devices, local(): arrived = lax.all_to_all(packed, 'req', 0, 0, tiled=True)  17.5 us
    all_to_all x1, starting transfers between devices, local(): everyone = lax.all_to_all(copies, 'req', 0, 0, tiled=True)  14.8 us
    slice x1, local copies, waits for them, and re-layouts, local(): pool_cache[:, :, 1].reshape(page_count, PAGE, heads_here, HEAD)  11.7 us
    all_to_all x1, starting transfers between devices, local(): gathered = lax.all_to_all(partial_copies, 'tp', 0, 0, tiled=True)  6.82 us
    all_to_all x1, starting transfers between devices, local(): arrived = lax.all_to_all(packed, 'req', 0, 0, tiled=True)  5.73 us
    all_to_all x1, waiting for transfers between devices, local(): everyone = lax.all_to_all(copies, 'req', 0, 0, tiled=True)  4.8 us
    slice x1, local copies, waits for them, and re-layouts, local(): tail_cache[:, :, 1].reshape(row_count, tail_slots, heads_here, HEAD)  2.17 us
  transfers between devices with their start and end apart: 3, of which 3 were waited for; matrix products, arithmetic and copies ran while one was open for 16% of the time, Pallas kernels for 0%

profile of v12, /device:TPU:1, one launch (start us, length us, event | category | flops | bytes accessed | tf_op | source)
XLA Modules:
  0.0 97.8 jit_solution(3716391815237201868)
XLA Ops:
  0.7 1.6 %broadcast_in_dim.67 = bf16[64,16,256]{2,1,0:T(8,128)(2,1)} broadcast(bf16[16,256]{1,0:T(8,128)(2,1)} %param.13), dimensions={1,2} | broadcast | bytes 532480 | tf_op jit(solution)/shard_map/broadcast_in_dim | solution.py:51
  2.3 14.8 %all-to-all-start = ((bf16[64,16,256]{2,1,0:T(8,128)(2,1)}), bf16[64,16,256]{2,1,0:T(8,128)(2,1)S(1)}, u32[]{:S(2)}, u32[]{:S(2)}) async-start(bf16[64,16,256]{2,1,0:T(8,128)(2,1)} %broadcast_in_dim.67), calls=%async_computation | async-start | bytes 1048576 | tf_op jit(solution)/shard_map/all_to_all | solution.py:52
  17.2 0.7 gather_fusion
  18.0 0.1 fusion.46
  18.4 11.7 %slice_reduce_fusion = (bf16[32,64,256]{2,1,0:T(8,128)(2,1)S(1)}, bf16[32,64,256]{2,1,0:T(8,128)(2,1)}) fusion(bf16[32,64,2,256]{3,2,1,0:T(2,128)(2,1)} %param.17), kind=kLoop, calls=%fused_computation.3 | loop fusion | bytes 4194304 | tf_op jit(solution)/shard_map/slice | solution.py:61
  30.1 4.8 %all-to-all-done = bf16[64,16,256]{2,1,0:T(8,128)(2,1)S(1)} async-done(((bf16[64,16,256]{2,1,0:T(8,128)(2,1)}), bf16[64,16,256]{2,1,0:T(8,128)(2,1)S(1)}, u32[]{:S(2)}, u32[]{:S(2)}) %all-to-all-start) | async-done | bytes 524320 | tf_op jit(solution)/shard_map/all_to_all | solution.py:52
  34.9 0.2 copy.79
  35.1 0.3 convolution_convert_fusion
  35.3 0.2 reshape.265
  35.5 2.0 %fusion.67 = (bf16[32,16,2]{1,2,0:T(2,128)(2,1)S(1)}, f32[32,16,2,64]{3,1,2,0:T(8,128)S(1)}) fusion(f32[32,2,64]{2,1,0:T(2,128)S(1)} %broadcast_multiply_fusion, bf16[32,16,2,128]{3,2,1,0:T(2,128)(2,1)S(1)} %reshape.265, pred[32,64]{1,0:T(8,128)(4,1)S(1)} %get-tuple-element.24, bf16[32,64,256]{2,1,0:T(8,128)(2,1)} %get-tuple-element.3), kind=kOutput, calls=%fused_computation.116 | convolution fusion | flops 17038336 | bytes 1593344 | tf_op jit(solution)/shard_map/pqhd,pshd->pqhs/dot_general | solution.py:67
  37.5 0.2 select_reduce_fusion
  37.7 0.2 fusion.50
  37.9 0.1 copy.48
  38.0 0.4 fusion.14
  38.5 0.4 fusion.6
  38.9 0.5 fusion.69
  39.3 0.4 fusion.23
  39.9 0.4 fusion
  40.3 0.3 copy.54
  40.7 0.2 fusion.68
  41.0 0.1 copy.55
  41.1 1.0 %maximum_maximum_fusion = bf16[64,40,128]{2,1,0:T(8,128)(2,1)} fusion(bf16[64,1,128]{2,1,0:T(2,128)(2,1)S(1)} %copy.55, bf16[64,32,128]{2,1,0:T(8,128)(2,1)S(1)} %copy.54, bf16[40]{0:T(256)(128)(2,1)S(1)} %pad.7.clone), kind=kLoop, calls=%fused_computation.23 | loop fusion | flops 1966080 | bytes 1196112 | tf_op jit(solution)/shard_map/concatenate | solution.py:108
  42.1 5.7 %all-to-all-start.1 = ((bf16[64,40,128]{2,1,0:T(8,128)(2,1)}), bf16[64,40,128]{2,1,0:T(8,128)(2,1)S(1)}, u32[]{:S(2)}, u32[]{:S(2)}) async-start(bf16[64,40,128]{2,1,0:T(8,128)(2,1)} %maximum_maximum_fusion), calls=%async_computation.1 | async-start | bytes 1310720 | tf_op jit(solution)/shard_map/all_to_all | solution.py:116
  47.9 0.1 fusion.40
  48.2 2.2 %slice_reduce_fusion.2 = (bf16[16,32,256]{2,1,0:T(8,128)(2,1)S(1)}, bf16[16,32,256]{2,1,0:T(8,128)(2,1)S(1)}) fusion(bf16[16,32,2,256]{3,2,1,0:T(2,128)(2,1)S(1)} %copy-done.2), kind=kLoop, calls=%fused_computation.24 | loop fusion | bytes 1048576 | tf_op jit(solution)/shard_map/slice | solution.py:127
  50.4 0.2 fusion.19
  50.6 0.1 fusion.57
  50.7 17.5 %all-to-all-done.1 = bf16[64,40,128]{2,1,0:T(8,128)(2,1)S(1)} async-done(((bf16[64,40,128]{2,1,0:T(8,128)(2,1)}), bf16[64,40,128]{2,1,0:T(8,128)(2,1)S(1)}, u32[]{:S(2)}, u32[]{:S(2)}) %all-to-all-start.1) | async-done | bytes 655392 | tf_op jit(solution)/shard_map/all_to_all | solution.py:116
  68.3 0.1 reduce_max.42
  68.3 0.1 copy.56
  68.5 0.1 fusion.54
  68.6 0.1 copy.57
  68.7 0.2 fusion.53
  68.8 0.1 sub.78
  68.9 0.1 fusion.38
  69.1 0.1 copy.59
  69.3 0.1 copy.58
  69.4 0.1 copy.60
  69.5 0.2 fusion.15
  69.7 0.2 fusion.17
  69.8 0.3 multiply_reduce_fusion
  70.2 0.1 fusion.52
  70.4 1.1 %convolution_convert_fusion.1 = bf16[8,16,2048]{2,1,0:T(8,128)(2,1)} fusion(bf16[256,2048]{1,0:T(8,128)(2,1)S(1)} %copy-done, bf16[16,256]{1,0:T(8,128)(2,1)S(1)} %bitcast.110), kind=kOutput, calls=%fused_computation.2 | convolution fusion | flops 134479872 | bytes 1581056 | tf_op jit(solution)/shard_map/kqi,ij->kqj/dot_general | solution.py:162
  71.5 6.8 %all-to-all-start.2 = ((bf16[8,16,2048]{2,1,0:T(8,128)(2,1)}), bf16[8,16,2048]{2,1,0:T(8,128)(2,1)S(1)}, u32[]{:S(2)}, u32[]{:S(2)}) async-start(bf16[8,16,2048]{2,1,0:T(8,128)(2,1)} %convolution_convert_fusion.1), calls=%async_computation.2 | async-start | bytes 1048576 | tf_op jit(solution)/shard_map/all_to_all | solution.py:165
  78.4 17.9 %all-to-all-done.2 = bf16[8,16,2048]{2,1,0:T(8,128)(2,1)S(1)} async-done(((bf16[8,16,2048]{2,1,0:T(8,128)(2,1)}), bf16[8,16,2048]{2,1,0:T(8,128)(2,1)S(1)}, u32[]{:S(2)}, u32[]{:S(2)}) %all-to-all-start.2) | async-done | bytes 524320 | tf_op jit(solution)/shard_map/all_to_all | solution.py:165
  96.3 0.2 fusion.59
  96.5 0.6 constant_dynamic-slice_fusion
  97.1 0.7 add_convert_fusion.1
  (58 shorter events, 1.2 us)
Async XLA Ops:
  0.6 69.7 %copy-start = (bf16[256,2048]{1,0:T(8,128)(2,1)S(1)}, bf16[256,2048]{1,0:T(8,128)(2,1)}, u32[]{:S(2)}) copy-start(bf16[256,2048]{1,0:T(8,128)(2,1)} %param.22) | copy-start | bytes 3145732
  0.6 17.6 %copy-start.4 = (bf16[16,256]{1,0:T(8,128)(2,1)S(1)}, bf16[16,256]{1,0:T(8,128)(2,1)}, u32[]{:S(2)}) copy-start(bf16[16,256]{1,0:T(8,128)(2,1)} %param.13) | copy-start | bytes 24580
  0.7 16.5 %copy-start.6 = (s32[32]{0:T(128)S(1)}, s32[32]{0:T(128)}, u32[]{:S(2)}) copy-start(s32[32]{0:T(128)} %param.18) | copy-start | bytes 388
  0.7 16.6 %copy-start.1 = (s32[64]{0:T(128)S(1)}, s32[64]{0:T(128)}, u32[]{:S(2)}) copy-start(s32[64]{0:T(128)} %param.20) | copy-start | bytes 772
  0.7 17.3 %copy-start.8 = (s32[32]{0:T(128)S(1)}, s32[32]{0:T(128)}, u32[]{:S(2)}) copy-start(s32[32]{0:T(128)} %param.19) | copy-start | bytes 388
  0.7 17.4 %copy-start.5 = (bf16[16,2,256]{2,1,0:T(2,128)(2,1)S(1)}, bf16[16,2,256]{2,1,0:T(2,128)(2,1)}, u32[]{:S(2)}) copy-start(bf16[16,2,256]{2,1,0:T(2,128)(2,1)} %param.14) | copy-start | bytes 49156
  2.3 32.6 %all-to-all-start = ((bf16[64,16,256]{2,1,0:T(8,128)(2,1)}), bf16[64,16,256]{2,1,0:T(8,128)(2,1)S(1)}, u32[]{:S(2)}, u32[]{:S(2)}) async-start(bf16[64,16,256]{2,1,0:T(8,128)(2,1)} %broadcast_in_dim.67), calls=%async_computation | async-start | bytes 1048576 | tf_op jit(solution)/shard_map/all_to_all | solution.py:52
  41.0 7.1 %copy-start.9 = (s32[16]{0:T(128)S(1)}, s32[16]{0:T(128)}, u32[]{:S(2)}) copy-start(s32[16]{0:T(128)} %param.16) | copy-start | bytes 196
  41.0 7.2 %copy-start.2 = (bf16[16,32,2,256]{3,2,1,0:T(2,128)(2,1)S(1)}, bf16[16,32,2,256]{3,2,1,0:T(2,128)(2,1)}, u32[]{:S(2)}) copy-start(bf16[16,32,2,256]{3,2,1,0:T(2,128)(2,1)} %param.15) | copy-start | bytes 1572868
  42.1 26.1 %all-to-all-start.1 = ((bf16[64,40,128]{2,1,0:T(8,128)(2,1)}), bf16[64,40,128]{2,1,0:T(8,128)(2,1)S(1)}, u32[]{:S(2)}, u32[]{:S(2)}) async-start(bf16[64,40,128]{2,1,0:T(8,128)(2,1)} %maximum_maximum_fusion), calls=%async_computation.1 | async-start | bytes 1310720 | tf_op jit(solution)/shard_map/all_to_all | solution.py:116
  70.3 8.0 %copy-start.7 = (bf16[2048]{0:T(1024)(128)(2,1)S(1)}, bf16[2048]{0:T(1024)(128)(2,1)}, u32[]{:S(2)}) copy-start(bf16[2048]{0:T(1024)(128)(2,1)} %param.23) | copy-start | bytes 12292
  70.3 8.0 %copy-start.10 = (bf16[256]{0:T(256)(128)(2,1)S(1)}, bf16[256]{0:T(256)(128)(2,1)}, u32[]{:S(2)}) copy-start(bf16[256]{0:T(256)(128)(2,1)} %param.24) | copy-start | bytes 1540
  70.3 8.0 %copy-start.11 = (bf16[256]{0:T(256)(128)(2,1)S(1)}, bf16[256]{0:T(256)(128)(2,1)}, u32[]{:S(2)}) copy-start(bf16[256]{0:T(256)(128)(2,1)} %param.25) | copy-start | bytes 1540
  70.4 26.0 %copy-start.3 = (bf16[16,2048]{1,0:T(8,128)(2,1)S(1)}, bf16[16,2048]{1,0:T(8,128)(2,1)}, u32[]{:S(2)}) copy-start(bf16[16,2048]{1,0:T(8,128)(2,1)} %param.21) | copy-start | bytes 196612
  71.5 24.8 %all-to-all-start.2 = ((bf16[8,16,2048]{2,1,0:T(8,128)(2,1)}), bf16[8,16,2048]{2,1,0:T(8,128)(2,1)S(1)}, u32[]{:S(2)}, u32[]{:S(2)}) async-start(bf16[8,16,2048]{2,1,0:T(8,128)(2,1)} %convolution_convert_fusion.1), calls=%async_computation.2 | async-start | bytes 1048576 | tf_op jit(solution)/shard_map/all_to_all | solution.py:165

commit v13 on v12

--- a/solution.py
+++ b/solution.py
@@ -54,9 +54,9 @@
     safe_group = jnp.clip(page_group, 0, group_count - 1)
     member = (page_group[:, None] == jnp.arange(group_count)[None, :]) & (page_group[:, None] >= 0)
     pick = member.astype(jnp.bfloat16)
-    page_queries = jnp.dot(
-        pick, everyone.reshape(group_count, -1), preferred_element_type=f32
-    ).astype(jnp.bfloat16).reshape(page_count, row_count, heads_here, HEAD)
+    page_queries = jnp.einsum(
+        "pg,gqhd->pqhd", pick, by_group, preferred_element_type=f32
+    ).astype(jnp.bfloat16)
     page_keys = pool_cache[:, :, 0].reshape(page_count, PAGE, heads_here, HEAD)
     page_values = pool_cache[:, :, 1].reshape(page_count, PAGE, heads_here, HEAD)
     prompt_here = prompt_len[safe_group]

time: 98.2 us -> 98 us (level)
  no operation moved by 1% of the time
where the time goes in v13:
time: 98 us; the launch traced here: 97.6 us
  waiting for transfers between devices  40.2 us (41%)
  starting transfers between devices  27.4 us (28%)
  local copies, waits for them, and re-layouts  18.4 us (19%)
  matrix products  6.11 us (6%)
  other arithmetic  4.39 us (4%)
  between operations  1.07 us (1%)
    all_to_all x1, waiting for transfers between devices, local(): gathered = lax.all_to_all(partial_copies, 'tp', 0, 0, tiled=True)  17.9 us
    all_to_all x1, waiting for transfers between devices, local(): arrived = lax.all_to_all(packed, 'req', 0, 0, tiled=True)  17.5 us
    all_to_all x1, starting transfers between devices, local(): everyone = lax.all_to_all(copies, 'req', 0, 0, tiled=True)  14.8 us
    slice x1, local copies, waits for them, and re-layouts, local(): pool_cache[:, :, 1].reshape(page_count, PAGE, heads_here, HEAD)  11.7 us
    all_to_all x1, starting transfers between devices, local(): gathered = lax.all_to_all(partial_copies, 'tp', 0, 0, tiled=True)  6.82 us
    all_to_all x1, starting transfers between devices, local(): arrived = lax.all_to_all(packed, 'req', 0, 0, tiled=True)  5.73 us
    all_to_all x1, waiting for transfers between devices, local(): everyone = lax.all_to_all(copies, 'req', 0, 0, tiled=True)  4.8 us
    slice x1, local copies, waits for them, and re-layouts, local(): tail_cache[:, :, 1].reshape(row_count, tail_slots, heads_here, HEAD)  2.17 us
  transfers between devices with their start and end apart: 3, of which 3 were waited for; matrix products, arithmetic and copies ran while one was open for 16% of the time, Pallas kernels for 0%

profile of v13, /device:TPU:1, one launch (start us, length us, event | category | flops | bytes accessed | tf_op | source)
XLA Modules:
  0.0 97.6 jit_solution(17802394628944615079)
XLA Ops:
  0.7 1.6 %broadcast_in_dim.67 = bf16[64,16,256]{2,1,0:T(8,128)(2,1)} broadcast(bf16[16,256]{1,0:T(8,128)(2,1)} %param.13), dimensions={1,2} | broadcast | bytes 532480 | tf_op jit(solution)/shard_map/broadcast_in_dim | solution.py:51
  2.3 14.8 %all-to-all-start = ((bf16[64,16,256]{2,1,0:T(8,128)(2,1)}), bf16[64,16,256]{2,1,0:T(8,128)(2,1)S(1)}, u32[]{:S(2)}, u32[]{:S(2)}) async-start(bf16[64,16,256]{2,1,0:T(8,128)(2,1)} %broadcast_in_dim.67), calls=%async_computation | async-start | bytes 1048576 | tf_op jit(solution)/shard_map/all_to_all | solution.py:52
  17.2 0.7 gather_fusion
  18.0 0.1 fusion.47
  18.4 11.7 %slice_reduce_fusion = (bf16[32,64,256]{2,1,0:T(8,128)(2,1)S(1)}, bf16[32,64,256]{2,1,0:T(8,128)(2,1)}) fusion(bf16[32,64,2,256]{3,2,1,0:T(2,128)(2,1)} %param.17), kind=kLoop, calls=%fused_computation.2 | loop fusion | bytes 4194304 | tf_op jit(solution)/shard_map/slice | solution.py:61
  30.1 4.8 %all-to-all-done = bf16[64,16,256]{2,1,0:T(8,128)(2,1)S(1)} async-done(((bf16[64,16,256]{2,1,0:T(8,128)(2,1)}), bf16[64,16,256]{2,1,0:T(8,128)(2,1)S(1)}, u32[]{:S(2)}, u32[]{:S(2)}) %all-to-all-start) | async-done | bytes 524320 | tf_op jit(solution)/shard_map/all_to_all | solution.py:52
  34.9 0.1 reshape.261
  35.0 0.3 convolution_convert_fusion.1
  35.3 2.0 %fusion.69 = (bf16[32,16,2]{1,2,0:T(2,128)(2,1)S(1)}, f32[32,16,2,64]{3,1,2,0:T(8,128)S(1)}) fusion(f32[32,2,64]{2,1,0:T(2,128)S(1)} %broadcast_multiply_fusion, bf16[32,16,2,128]{3,0,2,1:T(8,128)(2,1)S(1)} %convolution_convert_fusion.1, pred[32,64]{1,0:T(8,128)(4,1)S(1)} %get-tuple-element.24, bf16[32,64,256]{2,1,0:T(8,128)(2,1)} %get-tuple-element.3), kind=kOutput, calls=%fused_computation.118 | convolution fusion | flops 17038336 | bytes 1593344 | tf_op jit(solution)/shard_map/pqhd,pshd->pqhs/dot_general | solution.py:67
  37.3 0.2 select_reduce_fusion
  37.5 0.2 fusion.49
  37.7 0.1 copy.60
  37.8 0.4 fusion.15
  38.3 0.4 fusion.6
  38.7 0.5 fusion.71
  39.1 0.4 fusion.24
  39.6 0.4 fusion
  40.1 0.3 copy.66
  40.5 0.2 fusion.70
  40.8 0.1 copy.67
  40.9 1.0 %maximum_maximum_fusion = bf16[64,40,128]{2,1,0:T(8,128)(2,1)} fusion(bf16[64,1,128]{2,1,0:T(2,128)(2,1)S(1)} %copy.67, bf16[64,32,128]{2,1,0:T(8,128)(2,1)S(1)} %copy.66, bf16[40]{0:T(256)(128)(2,1)S(1)} %pad.7.clone), kind=kLoop, calls=%fused_computation.23 | loop fusion | flops 1966080 | bytes 1196112 | tf_op jit(solution)/shard_map/concatenate | solution.py:108
  41.9 5.7 %all-to-all-start.1 = ((bf16[64,40,128]{2,1,0:T(8,128)(2,1)}), bf16[64,40,128]{2,1,0:T(8,128)(2,1)S(1)}, u32[]{:S(2)}, u32[]{:S(2)}) async-start(bf16[64,40,128]{2,1,0:T(8,128)(2,1)} %maximum_maximum_fusion), calls=%async_computation.1 | async-start | bytes 1310720 | tf_op jit(solution)/shard_map/all_to_all | solution.py:116
  47.6 0.1 fusion.41
  48.0 2.2 %slice_reduce_fusion.2 = (bf16[16,32,256]{2,1,0:T(8,128)(2,1)S(1)}, bf16[16,32,256]{2,1,0:T(8,128)(2,1)S(1)}) fusion(bf16[16,32,2,256]{3,2,1,0:T(2,128)(2,1)S(1)} %copy-done.2), kind=kLoop, calls=%fused_computation.25 | loop fusion | bytes 1048576 | tf_op jit(solution)/shard_map/slice | solution.py:127
  50.2 0.2 fusion.20
  50.4 0.1 fusion.59
  50.5 17.5 %all-to-all-done.1 = bf16[64,40,128]{2,1,0:T(8,128)(2,1)S(1)} async-done(((bf16[64,40,128]{2,1,0:T(8,128)(2,1)}), bf16[64,40,128]{2,1,0:T(8,128)(2,1)S(1)}, u32[]{:S(2)}, u32[]{:S(2)}) %all-to-all-start.1) | async-done | bytes 655392 | tf_op jit(solution)/shard_map/all_to_all | solution.py:116
  68.0 0.1 reduce_max.42
  68.1 0.1 copy.68
  68.3 0.1 fusion.56
  68.4 0.1 copy.69
  68.5 0.2 fusion.55
  68.6 0.1 sub.78
  68.7 0.1 fusion.39
  68.8 0.1 reduce_sum.71
  68.9 0.1 copy.71
  69.1 0.1 copy.70
  69.2 0.1 copy.72
  69.2 0.2 fusion.16
  69.4 0.2 fusion.18
  69.6 0.3 multiply_reduce_fusion
  70.0 0.1 fusion.54
  70.2 1.1 %convolution_convert_fusion = bf16[8,16,2048]{2,1,0:T(8,128)(2,1)} fusion(bf16[256,2048]{1,0:T(8,128)(2,1)S(1)} %copy-done, bf16[16,256]{1,0:T(8,128)(2,1)S(1)} %bitcast.107), kind=kOutput, calls=%fused_computation.1 | convolution fusion | flops 134479872 | bytes 1581056 | tf_op jit(solution)/shard_map/kqi,ij->kqj/dot_general | solution.py:162
  71.3 6.8 %all-to-all-start.2 = ((bf16[8,16,2048]{2,1,0:T(8,128)(2,1)}), bf16[8,16,2048]{2,1,0:T(8,128)(2,1)S(1)}, u32[]{:S(2)}, u32[]{:S(2)}) async-start(bf16[8,16,2048]{2,1,0:T(8,128)(2,1)} %convolution_convert_fusion), calls=%async_computation.2 | async-start | bytes 1048576 | tf_op jit(solution)/shard_map/all_to_all | solution.py:165
  78.1 17.9 %all-to-all-done.2 = bf16[8,16,2048]{2,1,0:T(8,128)(2,1)S(1)} async-done(((bf16[8,16,2048]{2,1,0:T(8,128)(2,1)}), bf16[8,16,2048]{2,1,0:T(8,128)(2,1)S(1)}, u32[]{:S(2)}, u32[]{:S(2)}) %all-to-all-start.2) | async-done | bytes 524320 | tf_op jit(solution)/shard_map/all_to_all | solution.py:165
  96.1 0.2 fusion.61
  96.3 0.6 constant_dynamic-slice_fusion
  96.9 0.7 add_convert_fusion.1
  (57 shorter events, 1.2 us)
Async XLA Ops:
  0.6 69.5 %copy-start = (bf16[256,2048]{1,0:T(8,128)(2,1)S(1)}, bf16[256,2048]{1,0:T(8,128)(2,1)}, u32[]{:S(2)}) copy-start(bf16[256,2048]{1,0:T(8,128)(2,1)} %param.22) | copy-start | bytes 3145732
  0.6 17.6 %copy-start.4 = (bf16[16,256]{1,0:T(8,128)(2,1)S(1)}, bf16[16,256]{1,0:T(8,128)(2,1)}, u32[]{:S(2)}) copy-start(bf16[16,256]{1,0:T(8,128)(2,1)} %param.13) | copy-start | bytes 24580
  0.7 16.5 %copy-start.6 = (s32[32]{0:T(128)S(1)}, s32[32]{0:T(128)}, u32[]{:S(2)}) copy-start(s32[32]{0:T(128)} %param.18) | copy-start | bytes 388
  0.7 16.6 %copy-start.1 = (s32[64]{0:T(128)S(1)}, s32[64]{0:T(128)}, u32[]{:S(2)}) copy-start(s32[64]{0:T(128)} %param.20) | copy-start | bytes 772
  0.7 17.3 %copy-start.8 = (s32[32]{0:T(128)S(1)}, s32[32]{0:T(128)}, u32[]{:S(2)}) copy-start(s32[32]{0:T(128)} %param.19) | copy-start | bytes 388
  0.7 17.4 %copy-start.5 = (bf16[16,2,256]{2,1,0:T(2,128)(2,1)S(1)}, bf16[16,2,256]{2,1,0:T(2,128)(2,1)}, u32[]{:S(2)}) copy-start(bf16[16,2,256]{2,1,0:T(2,128)(2,1)} %param.14) | copy-start | bytes 49156
  2.3 32.6 %all-to-all-start = ((bf16[64,16,256]{2,1,0:T(8,128)(2,1)}), bf16[64,16,256]{2,1,0:T(8,128)(2,1)S(1)}, u32[]{:S(2)}, u32[]{:S(2)}) async-start(bf16[64,16,256]{2,1,0:T(8,128)(2,1)} %broadcast_in_dim.67), calls=%async_computation | async-start | bytes 1048576 | tf_op jit(solution)/shard_map/all_to_all | solution.py:52
  40.7 7.1 %copy-start.9 = (s32[16]{0:T(128)S(1)}, s32[16]{0:T(128)}, u32[]{:S(2)}) copy-start(s32[16]{0:T(128)} %param.16) | copy-start | bytes 196
  40.7 7.2 %copy-start.2 = (bf16[16,32,2,256]{3,2,1,0:T(2,128)(2,1)S(1)}, bf16[16,32,2,256]{3,2,1,0:T(2,128)(2,1)}, u32[]{:S(2)}) copy-start(bf16[16,32,2,256]{3,2,1,0:T(2,128)(2,1)} %param.15) | copy-start | bytes 1572868
  41.9 26.1 %all-to-all-start.1 = ((bf16[64,40,128]{2,1,0:T(8,128)(2,1)}), bf16[64,40,128]{2,1,0:T(8,128)(2,1)S(1)}, u32[]{:S(2)}, u32[]{:S(2)}) async-start(bf16[64,40,128]{2,1,0:T(8,128)(2,1)} %maximum_maximum_fusion), calls=%async_computation.1 | async-start | bytes 1310720 | tf_op jit(solution)/shard_map/all_to_all | solution.py:116
  70.1 8.0 %copy-start.7 = (bf16[2048]{0:T(1024)(128)(2,1)S(1)}, bf16[2048]{0:T(1024)(128)(2,1)}, u32[]{:S(2)}) copy-start(bf16[2048]{0:T(1024)(128)(2,1)} %param.23) | copy-start | bytes 12292
  70.1 8.0 %copy-start.10 = (bf16[256]{0:T(256)(128)(2,1)S(1)}, bf16[256]{0:T(256)(128)(2,1)}, u32[]{:S(2)}) copy-start(bf16[256]{0:T(256)(128)(2,1)} %param.24) | copy-start | bytes 1540
  70.1 8.0 %copy-start.11 = (bf16[256]{0:T(256)(128)(2,1)S(1)}, bf16[256]{0:T(256)(128)(2,1)}, u32[]{:S(2)}) copy-start(bf16[256]{0:T(256)(128)(2,1)} %param.25) | copy-start | bytes 1540
  70.1 26.0 %copy-start.3 = (bf16[16,2048]{1,0:T(8,128)(2,1)S(1)}, bf16[16,2048]{1,0:T(8,128)(2,1)}, u32[]{:S(2)}) copy-start(bf16[16,2048]{1,0:T(8,128)(2,1)} %param.21) | copy-start | bytes 196612
  71.3 24.8 %all-to-all-start.2 = ((bf16[8,16,2048]{2,1,0:T(8,128)(2,1)}), bf16[8,16,2048]{2,1,0:T(8,128)(2,1)S(1)}, u32[]{:S(2)}, u32[]{:S(2)}) async-start(bf16[8,16,2048]{2,1,0:T(8,128)(2,1)} %convolution_convert_fusion), calls=%async_computation.2 | async-start | bytes 1048576 | tf_op jit(solution)/shard_map/all_to_all | solution.py:165

commit v14 on v13

--- a/solution.py
+++ b/solution.py
@@ -89,9 +89,9 @@
     group_accum = group_accum + jnp.einsum(
         "gp,pqhd->gqhd", spread, accum_lower, preferred_element_type=f32
     )
-    group_totals = jnp.dot(
-        member.T.astype(f32), page_totals.reshape(page_count, -1), precision=highest
-    )
+    page_totals_upper, page_totals_lower = split_halves(page_totals.reshape(page_count, -1))
+    group_totals = jnp.dot(spread, page_totals_upper, preferred_element_type=f32)
+    group_totals = group_totals + jnp.dot(spread, page_totals_lower, preferred_element_type=f32)
     stats_width = row_count * heads_here
     totals_upper, totals_lower = split_halves(group_totals)
     stats = jnp.concatenate(

time: 98 us -> 98.2 us (level)
  no operation moved by 1% of the time
where the time goes in v14:
time: 98.2 us; the launch traced here: 97.8 us
  waiting for transfers between devices  40.2 us (41%)
  starting transfers between devices  27.4 us (28%)
  local copies, waits for them, and re-layouts  18.4 us (19%)
  matrix products  6.31 us (6%)
  other arithmetic  4.39 us (4%)
  between operations  1.07 us (1%)
    all_to_all x1, waiting for transfers between devices, local(): gathered = lax.all_to_all(partial_copies, 'tp', 0, 0, tiled=True)  17.9 us
    all_to_all x1, waiting for transfers between devices, local(): arrived = lax.all_to_all(packed, 'req', 0, 0, tiled=True)  17.5 us
    all_to_all x1, starting transfers between devices, local(): everyone = lax.all_to_all(copies, 'req', 0, 0, tiled=True)  14.8 us
    slice x1, local copies, waits for them, and re-layouts, local(): pool_cache[:, :, 1].reshape(page_count, PAGE, heads_here, HEAD)  11.7 us
    all_to_all x1, starting transfers between devices, local(): gathered = lax.all_to_all(partial_copies, 'tp', 0, 0, tiled=True)  6.82 us
    all_to_all x1, starting transfers between devices, local(): arrived = lax.all_to_all(packed, 'req', 0, 0, tiled=True)  5.73 us
    all_to_all x1, waiting for transfers between devices, local(): everyone = lax.all_to_all(copies, 'req', 0, 0, tiled=True)  4.8 us
    slice x1, local copies, waits for them, and re-layouts, local(): tail_cache[:, :, 1].reshape(row_count, tail_slots, heads_here, HEAD)  2.17 us
  transfers between devices with their start and end apart: 3, of which 3 were waited for; matrix products, arithmetic and copies ran while one was open for 16% of the time, Pallas kernels for 0%

profile of v14, /device:TPU:1, one launch (start us, length us, event | category | flops | bytes accessed | tf_op | source)
XLA Modules:
  0.0 97.8 jit_solution(7774905891740140572)
XLA Ops:
  0.7 1.6 %broadcast_in_dim.67 = bf16[64,16,256]{2,1,0:T(8,128)(2,1)} broadcast(bf16[16,256]{1,0:T(8,128)(2,1)} %param.13), dimensions={1,2} | broadcast | bytes 532480 | tf_op jit(solution)/shard_map/broadcast_in_dim | solution.py:51
  2.3 14.8 %all-to-all-start = ((bf16[64,16,256]{2,1,0:T(8,128)(2,1)}), bf16[64,16,256]{2,1,0:T(8,128)(2,1)S(1)}, u32[]{:S(2)}, u32[]{:S(2)}) async-start(bf16[64,16,256]{2,1,0:T(8,128)(2,1)} %broadcast_in_dim.67), calls=%async_computation | async-start | bytes 1048576 | tf_op jit(solution)/shard_map/all_to_all | solution.py:52
  17.2 0.7 gather_fusion
  18.0 0.1 fusion.47
  18.4 11.7 %slice_reduce_fusion = (bf16[32,64,256]{2,1,0:T(8,128)(2,1)S(1)}, bf16[32,64,256]{2,1,0:T(8,128)(2,1)}) fusion(bf16[32,64,2,256]{3,2,1,0:T(2,128)(2,1)} %param.17), kind=kLoop, calls=%fused_computation.2 | loop fusion | bytes 4194304 | tf_op jit(solution)/shard_map/slice | solution.py:61
  30.1 4.8 %all-to-all-done = bf16[64,16,256]{2,1,0:T(8,128)(2,1)S(1)} async-done(((bf16[64,16,256]{2,1,0:T(8,128)(2,1)}), bf16[64,16,256]{2,1,0:T(8,128)(2,1)S(1)}, u32[]{:S(2)}, u32[]{:S(2)}) %all-to-all-start) | async-done | bytes 524320 | tf_op jit(solution)/shard_map/all_to_all | solution.py:52
  34.9 0.1 reshape.261
  35.0 0.3 convolution_convert_fusion.1
  35.3 2.0 %fusion.70 = (bf16[32,16,2]{1,2,0:T(2,128)(2,1)S(1)}, f32[32,16,2,64]{3,1,2,0:T(8,128)S(1)}) fusion(f32[32,2,64]{2,1,0:T(2,128)S(1)} %broadcast_multiply_fusion, bf16[32,16,2,128]{3,0,2,1:T(8,128)(2,1)S(1)} %convolution_convert_fusion.1, pred[32,64]{1,0:T(8,128)(4,1)S(1)} %get-tuple-element.24, bf16[32,64,256]{2,1,0:T(8,128)(2,1)} %get-tuple-element.3), kind=kOutput, calls=%fused_computation.120 | convolution fusion | flops 17038336 | bytes 1593344 | tf_op jit(solution)/shard_map/pqhd,pshd->pqhs/dot_general | solution.py:67
  37.3 0.2 select_reduce_fusion
  37.5 0.2 fusion.49
  37.7 0.1 copy.60
  37.8 0.4 fusion.15
  38.3 0.4 fusion.6
  38.7 0.5 fusion.72
  39.1 0.4 fusion.24
  39.6 0.4 fusion
  40.1 0.3 copy.66
  40.5 0.2 fusion.64
  40.7 0.2 fusion.71
  41.0 0.1 copy.67
  41.1 1.0 %maximum_maximum_fusion = bf16[64,40,128]{2,1,0:T(8,128)(2,1)} fusion(bf16[64,1,128]{2,1,0:T(2,128)(2,1)S(1)} %copy.67, bf16[64,32,128]{2,1,0:T(8,128)(2,1)S(1)} %copy.66, bf16[40]{0:T(256)(128)(2,1)S(1)} %pad.7.clone), kind=kLoop, calls=%fused_computation.24 | loop fusion | flops 1966080 | bytes 1196112 | tf_op jit(solution)/shard_map/concatenate | solution.py:108
  42.1 5.7 %all-to-all-start.1 = ((bf16[64,40,128]{2,1,0:T(8,128)(2,1)}), bf16[64,40,128]{2,1,0:T(8,128)(2,1)S(1)}, u32[]{:S(2)}, u32[]{:S(2)}) async-start(bf16[64,40,128]{2,1,0:T(8,128)(2,1)} %maximum_maximum_fusion), calls=%async_computation.1 | async-start | bytes 1310720 | tf_op jit(solution)/shard_map/all_to_all | solution.py:116
  47.8 0.1 fusion.41
  48.2 2.2 %slice_reduce_fusion.2 = (bf16[16,32,256]{2,1,0:T(8,128)(2,1)S(1)}, bf16[16,32,256]{2,1,0:T(8,128)(2,1)S(1)}) fusion(bf16[16,32,2,256]{3,2,1,0:T(2,128)(2,1)S(1)} %copy-done.2), kind=kLoop, calls=%fused_computation.26 | loop fusion | bytes 1048576 | tf_op jit(solution)/shard_map/slice | solution.py:127
  50.4 0.2 fusion.20
  50.6 0.1 fusion.59
  50.7 17.5 %all-to-all-done.1 = bf16[64,40,128]{2,1,0:T(8,128)(2,1)S(1)} async-done(((bf16[64,40,128]{2,1,0:T(8,128)(2,1)}), bf16[64,40,128]{2,1,0:T(8,128)(2,1)S(1)}, u32[]{:S(2)}, u32[]{:S(2)}) %all-to-all-start.1) | async-done | bytes 655392 | tf_op jit(solution)/shard_map/all_to_all | solution.py:116
  68.2 0.1 reduce_max.42
  68.3 0.1 copy.68
  68.5 0.1 fusion.56
  68.6 0.1 copy.69
  68.7 0.2 fusion.55
  68.8 0.1 sub.82
  68.9 0.1 fusion.39
  69.1 0.1 copy.71
  69.3 0.1 copy.70
  69.4 0.1 copy.72
  69.4 0.2 fusion.16
  69.6 0.2 fusion.18
  69.8 0.3 multiply_reduce_fusion
  70.2 0.1 fusion.54
  70.3 1.1 %convolution_convert_fusion = bf16[8,16,2048]{2,1,0:T(8,128)(2,1)} fusion(bf16[256,2048]{1,0:T(8,128)(2,1)S(1)} %copy-done, bf16[16,256]{1,0:T(8,128)(2,1)S(1)} %bitcast.109), kind=kOutput, calls=%fused_computation.1 | convolution fusion | flops 134479872 | bytes 1581056 | tf_op jit(solution)/shard_map/kqi,ij->kqj/dot_general | solution.py:162
  71.5 6.8 %all-to-all-start.2 = ((bf16[8,16,2048]{2,1,0:T(8,128)(2,1)}), bf16[8,16,2048]{2,1,0:T(8,128)(2,1)S(1)}, u32[]{:S(2)}, u32[]{:S(2)}) async-start(bf16[8,16,2048]{2,1,0:T(8,128)(2,1)} %convolution_convert_fusion), calls=%async_computation.2 | async-start | bytes 1048576 | tf_op jit(solution)/shard_map/all_to_all | solution.py:165
  78.3 17.9 %all-to-all-done.2 = bf16[8,16,2048]{2,1,0:T(8,128)(2,1)S(1)} async-done(((bf16[8,16,2048]{2,1,0:T(8,128)(2,1)}), bf16[8,16,2048]{2,1,0:T(8,128)(2,1)S(1)}, u32[]{:S(2)}, u32[]{:S(2)}) %all-to-all-start.2) | async-done | bytes 524320 | tf_op jit(solution)/shard_map/all_to_all | solution.py:165
  96.3 0.2 fusion.61
  96.5 0.6 constant_dynamic-slice_fusion
  97.1 0.7 add_convert_fusion.1
  (59 shorter events, 1.2 us)
Async XLA Ops:
  0.6 69.7 %copy-start = (bf16[256,2048]{1,0:T(8,128)(2,1)S(1)}, bf16[256,2048]{1,0:T(8,128)(2,1)}, u32[]{:S(2)}) copy-start(bf16[256,2048]{1,0:T(8,128)(2,1)} %param.22) | copy-start | bytes 3145732
  0.6 17.6 %copy-start.4 = (bf16[16,256]{1,0:T(8,128)(2,1)S(1)}, bf16[16,256]{1,0:T(8,128)(2,1)}, u32[]{:S(2)}) copy-start(bf16[16,256]{1,0:T(8,128)(2,1)} %param.13) | copy-start | bytes 24580
  0.7 16.5 %copy-start.6 = (s32[32]{0:T(128)S(1)}, s32[32]{0:T(128)}, u32[]{:S(2)}) copy-start(s32[32]{0:T(128)} %param.18) | copy-start | bytes 388
  0.7 16.6 %copy-start.1 = (s32[64]{0:T(128)S(1)}, s32[64]{0:T(128)}, u32[]{:S(2)}) copy-start(s32[64]{0:T(128)} %param.20) | copy-start | bytes 772
  0.7 17.3 %copy-start.8 = (s32[32]{0:T(128)S(1)}, s32[32]{0:T(128)}, u32[]{:S(2)}) copy-start(s32[32]{0:T(128)} %param.19) | copy-start | bytes 388
  0.7 17.4 %copy-start.5 = (bf16[16,2,256]{2,1,0:T(2,128)(2,1)S(1)}, bf16[16,2,256]{2,1,0:T(2,128)(2,1)}, u32[]{:S(2)}) copy-start(bf16[16,2,256]{2,1,0:T(2,128)(2,1)} %param.14) | copy-start | bytes 49156
  2.3 32.6 %all-to-all-start = ((bf16[64,16,256]{2,1,0:T(8,128)(2,1)}), bf16[64,16,256]{2,1,0:T(8,128)(2,1)S(1)}, u32[]{:S(2)}, u32[]{:S(2)}) async-start(bf16[64,16,256]{2,1,0:T(8,128)(2,1)} %broadcast_in_dim.67), calls=%async_computation | async-start | bytes 1048576 | tf_op jit(solution)/shard_map/all_to_all | solution.py:52
  40.9 7.1 %copy-start.9 = (s32[16]{0:T(128)S(1)}, s32[16]{0:T(128)}, u32[]{:S(2)}) copy-start(s32[16]{0:T(128)} %param.16) | copy-start | bytes 196
  40.9 7.2 %copy-start.2 = (bf16[16,32,2,256]{3,2,1,0:T(2,128)(2,1)S(1)}, bf16[16,32,2,256]{3,2,1,0:T(2,128)(2,1)}, u32[]{:S(2)}) copy-start(bf16[16,32,2,256]{3,2,1,0:T(2,128)(2,1)} %param.15) | copy-start | bytes 1572868
  42.1 26.1 %all-to-all-start.1 = ((bf16[64,40,128]{2,1,0:T(8,128)(2,1)}), bf16[64,40,128]{2,1,0:T(8,128)(2,1)S(1)}, u32[]{:S(2)}, u32[]{:S(2)}) async-start(bf16[64,40,128]{2,1,0:T(8,128)(2,1)} %maximum_maximum_fusion), calls=%async_computation.1 | async-start | bytes 1310720 | tf_op jit(solution)/shard_map/all_to_all | solution.py:116
  70.3 8.0 %copy-start.7 = (bf16[2048]{0:T(1024)(128)(2,1)S(1)}, bf16[2048]{0:T(1024)(128)(2,1)}, u32[]{:S(2)}) copy-start(bf16[2048]{0:T(1024)(128)(2,1)} %param.23) | copy-start | bytes 12292
  70.3 8.0 %copy-start.10 = (bf16[256]{0:T(256)(128)(2,1)S(1)}, bf16[256]{0:T(256)(128)(2,1)}, u32[]{:S(2)}) copy-start(bf16[256]{0:T(256)(128)(2,1)} %param.24) | copy-start | bytes 1540
  70.3 8.0 %copy-start.11 = (bf16[256]{0:T(256)(128)(2,1)S(1)}, bf16[256]{0:T(256)(128)(2,1)}, u32[]{:S(2)}) copy-start(bf16[256]{0:T(256)(128)(2,1)} %param.25) | copy-start | bytes 1540
  70.3 26.0 %copy-start.3 = (bf16[16,2048]{1,0:T(8,128)(2,1)S(1)}, bf16[16,2048]{1,0:T(8,128)(2,1)}, u32[]{:S(2)}) copy-start(bf16[16,2048]{1,0:T(8,128)(2,1)} %param.21) | copy-start | bytes 196612
  71.5 24.8 %all-to-all-start.2 = ((bf16[8,16,2048]{2,1,0:T(8,128)(2,1)}), bf16[8,16,2048]{2,1,0:T(8,128)(2,1)S(1)}, u32[]{:S(2)}, u32[]{:S(2)}) async-start(bf16[8,16,2048]{2,1,0:T(8,128)(2,1)} %convolution_convert_fusion), calls=%async_computation.2 | async-start | bytes 1048576 | tf_op jit(solution)/shard_map/all_to_all | solution.py:165

commit v15 on v13

--- a/solution.py
+++ b/solution.py
@@ -140,17 +140,20 @@
     )
     own_scores = own_scores + slopes[None, :] * tail_len.astype(f32)[:, None]
     home_top = jnp.maximum(tail_scores.max(-1), own_scores)
-    row_top = jnp.maximum(home_top, part_top.max(0))
-    part_scale = jnp.exp(part_top - row_top[None])
-    pool_totals = jnp.sum(part_scale * part_totals, 0)
-    pool_accum = jnp.sum(part_scale[..., None] * part_accum, 0)
-    tail_weights = jnp.exp(tail_scores - row_top[:, :, None])
-    own_weights = jnp.exp(own_scores - row_top)
+    tail_weights = jnp.exp(tail_scores - home_top[:, :, None])
+    own_weights = jnp.exp(own_scores - home_top)
     totals = tail_weights.sum(-1) + own_weights
     upper_part, lower_part = split_halves(tail_weights)
     accum = jnp.einsum("qhj,qjhd->qhd", upper_part, tail_values, preferred_element_type=f32)
     accum = accum + jnp.einsum("qhj,qjhd->qhd", lower_part, tail_values, preferred_element_type=f32)
     home_accum = accum + own_weights[:, :, None] * fresh_values.astype(f32)
+    row_top = jnp.maximum(home_top, part_top.max(0))
+    part_scale = jnp.exp(part_top - row_top[None])
+    pool_totals = jnp.sum(part_scale * part_totals, 0)
+    pool_accum = jnp.sum(part_scale[..., None] * part_accum, 0)
+    home_scale = jnp.exp(home_top - row_top)
+    totals = totals * home_scale
+    home_accum = home_accum * home_scale[:, :, None]
     attention = ((pool_accum + home_accum) / (pool_totals + totals)[:, :, None]).astype(
         jnp.bfloat16
     )

time: 98 us -> 98.1 us (level)
  no operation moved by 1% of the time
where the time goes in v15:
time: 98.1 us; the launch traced here: 97.7 us
  waiting for transfers between devices  40.2 us (41%)
  starting transfers between devices  27.4 us (28%)
  local copies, waits for them, and re-layouts  18.5 us (19%)
  matrix products  6.09 us (6%)
  other arithmetic  4.42 us (5%)
  between operations  1.07 us (1%)
    all_to_all x1, waiting for transfers between devices, local(): gathered = lax.all_to_all(partial_copies, 'tp', 0, 0, tiled=True)  17.9 us
    all_to_all x1, waiting for transfers between devices, local(): arrived = lax.all_to_all(packed, 'req', 0, 0, tiled=True)  17.5 us
    all_to_all x1, starting transfers between devices, local(): everyone = lax.all_to_all(copies, 'req', 0, 0, tiled=True)  14.8 us
    slice x1, local copies, waits for them, and re-layouts, local(): pool_cache[:, :, 1].reshape(page_count, PAGE, heads_here, HEAD)  11.7 us
    all_to_all x1, starting transfers between devices, local(): gathered = lax.all_to_all(partial_copies, 'tp', 0, 0, tiled=True)  6.82 us
    all_to_all x1, starting transfers between devices, local(): arrived = lax.all_to_all(packed, 'req', 0, 0, tiled=True)  5.73 us
    all_to_all x1, waiting for transfers between devices, local(): everyone = lax.all_to_all(copies, 'req', 0, 0, tiled=True)  4.8 us
    slice x1, local copies, waits for them, and re-layouts, local(): tail_cache[:, :, 1].reshape(row_count, tail_slots, heads_here, HEAD)  2.17 us
  transfers between devices with their start and end apart: 3, of which 3 were waited for; matrix products, arithmetic and copies ran while one was open for 16% of the time, Pallas kernels for 0%

profile of v15, /device:TPU:1, one launch (start us, length us, event | category | flops | bytes accessed | tf_op | source)
XLA Modules:
  0.0 97.7 jit_solution(12446067529027810591)
XLA Ops:
  0.7 1.6 %broadcast_in_dim.67 = bf16[64,16,256]{2,1,0:T(8,128)(2,1)} broadcast(bf16[16,256]{1,0:T(8,128)(2,1)} %param.13), dimensions={1,2} | broadcast | bytes 532480 | tf_op jit(solution)/shard_map/broadcast_in_dim | solution.py:51
  2.3 14.8 %all-to-all-start = ((bf16[64,16,256]{2,1,0:T(8,128)(2,1)}), bf16[64,16,256]{2,1,0:T(8,128)(2,1)S(1)}, u32[]{:S(2)}, u32[]{:S(2)}) async-start(bf16[64,16,256]{2,1,0:T(8,128)(2,1)} %broadcast_in_dim.67), calls=%async_computation | async-start | bytes 1048576 | tf_op jit(solution)/shard_map/all_to_all | solution.py:52
  17.2 0.7 gather_fusion
  18.0 0.1 fusion.47
  18.4 11.7 %slice_reduce_fusion = (bf16[32,64,256]{2,1,0:T(8,128)(2,1)S(1)}, bf16[32,64,256]{2,1,0:T(8,128)(2,1)}) fusion(bf16[32,64,2,256]{3,2,1,0:T(2,128)(2,1)} %param.17), kind=kLoop, calls=%fused_computation.2 | loop fusion | bytes 4194304 | tf_op jit(solution)/shard_map/slice | solution.py:61
  30.1 4.8 %all-to-all-done = bf16[64,16,256]{2,1,0:T(8,128)(2,1)S(1)} async-done(((bf16[64,16,256]{2,1,0:T(8,128)(2,1)}), bf16[64,16,256]{2,1,0:T(8,128)(2,1)S(1)}, u32[]{:S(2)}, u32[]{:S(2)}) %all-to-all-start) | async-done | bytes 524320 | tf_op jit(solution)/shard_map/all_to_all | solution.py:52
  34.9 0.1 reshape.262
  35.0 0.3 convolution_convert_fusion.1
  35.3 2.0 %fusion.72 = (bf16[32,16,2]{1,2,0:T(2,128)(2,1)S(1)}, f32[32,16,2,64]{3,1,2,0:T(8,128)S(1)}) fusion(f32[32,2,64]{2,1,0:T(2,128)S(1)} %broadcast_multiply_fusion, bf16[32,16,2,128]{3,0,2,1:T(8,128)(2,1)S(1)} %convolution_convert_fusion.1, pred[32,64]{1,0:T(8,128)(4,1)S(1)} %get-tuple-element.27, bf16[32,64,256]{2,1,0:T(8,128)(2,1)} %get-tuple-element.3), kind=kOutput, calls=%fused_computation.120 | convolution fusion | flops 17038336 | bytes 1593344 | tf_op jit(solution)/shard_map/pqhd,pshd->pqhs/dot_general | solution.py:67
  37.3 0.2 select_reduce_fusion
  37.5 0.2 fusion.49
  37.7 0.1 copy.60
  37.8 0.4 fusion.15
  38.3 0.4 fusion.6
  38.7 0.5 fusion.74
  39.1 0.4 fusion.24
  39.6 0.4 fusion
  40.1 0.3 copy.66
  40.5 0.2 fusion.73
  40.8 0.1 copy.67
  40.9 1.0 %maximum_maximum_fusion = bf16[64,40,128]{2,1,0:T(8,128)(2,1)} fusion(bf16[64,1,128]{2,1,0:T(2,128)(2,1)S(1)} %copy.67, bf16[64,32,128]{2,1,0:T(8,128)(2,1)S(1)} %copy.66, bf16[40]{0:T(256)(128)(2,1)S(1)} %pad.7.clone), kind=kLoop, calls=%fused_computation.23 | loop fusion | flops 1966080 | bytes 1196112 | tf_op jit(solution)/shard_map/concatenate | solution.py:108
  41.9 5.7 %all-to-all-start.1 = ((bf16[64,40,128]{2,1,0:T(8,128)(2,1)}), bf16[64,40,128]{2,1,0:T(8,128)(2,1)S(1)}, u32[]{:S(2)}, u32[]{:S(2)}) async-start(bf16[64,40,128]{2,1,0:T(8,128)(2,1)} %maximum_maximum_fusion), calls=%async_computation.1 | async-start | bytes 1310720 | tf_op jit(solution)/shard_map/all_to_all | solution.py:116
  47.6 0.1 fusion.41
  48.0 2.2 %slice_reduce_fusion.2 = (bf16[16,32,256]{2,1,0:T(8,128)(2,1)S(1)}, bf16[16,32,256]{2,1,0:T(8,128)(2,1)S(1)}) fusion(bf16[16,32,2,256]{3,2,1,0:T(2,128)(2,1)S(1)} %copy-done.2), kind=kLoop, calls=%fused_computation.25 | loop fusion | bytes 1048576 | tf_op jit(solution)/shard_map/slice | solution.py:127
  50.2 0.2 fusion.20
  50.4 0.1 fusion.59
  50.5 17.5 %all-to-all-done.1 = bf16[64,40,128]{2,1,0:T(8,128)(2,1)S(1)} async-done(((bf16[64,40,128]{2,1,0:T(8,128)(2,1)}), bf16[64,40,128]{2,1,0:T(8,128)(2,1)S(1)}, u32[]{:S(2)}, u32[]{:S(2)}) %all-to-all-start.1) | async-done | bytes 655392 | tf_op jit(solution)/shard_map/all_to_all | solution.py:116
  68.1 0.1 copy.68
  68.3 0.2 fusion.55
  68.5 0.1 copy.69
  68.5 0.1 sub.81
  68.6 0.1 fusion.39
  68.7 0.1 reduce_sum.71
  68.8 0.1 copy.72
  69.0 0.1 copy.70
  69.1 0.1 copy.71
  69.2 0.1 copy.73
  69.2 0.1 fusion.57
  69.3 0.2 fusion.16
  69.5 0.2 fusion.18
  69.7 0.3 multiply_reduce_fusion
  70.1 0.1 fusion.54
  70.3 1.1 %convolution_convert_fusion = bf16[8,16,2048]{2,1,0:T(8,128)(2,1)} fusion(bf16[256,2048]{1,0:T(8,128)(2,1)S(1)} %copy-done, bf16[16,256]{1,0:T(8,128)(2,1)S(1)} %bitcast.107), kind=kOutput, calls=%fused_computation.1 | convolution fusion | flops 134479872 | bytes 1581056 | tf_op jit(solution)/shard_map/kqi,ij->kqj/dot_general | solution.py:165
  71.4 6.8 %all-to-all-start.2 = ((bf16[8,16,2048]{2,1,0:T(8,128)(2,1)}), bf16[8,16,2048]{2,1,0:T(8,128)(2,1)S(1)}, u32[]{:S(2)}, u32[]{:S(2)}) async-start(bf16[8,16,2048]{2,1,0:T(8,128)(2,1)} %convolution_convert_fusion), calls=%async_computation.2 | async-start | bytes 1048576 | tf_op jit(solution)/shard_map/all_to_all | solution.py:168
  78.2 17.9 %all-to-all-done.2 = bf16[8,16,2048]{2,1,0:T(8,128)(2,1)S(1)} async-done(((bf16[8,16,2048]{2,1,0:T(8,128)(2,1)}), bf16[8,16,2048]{2,1,0:T(8,128)(2,1)S(1)}, u32[]{:S(2)}, u32[]{:S(2)}) %all-to-all-start.2) | async-done | bytes 524320 | tf_op jit(solution)/shard_map/all_to_all | solution.py:168
  96.2 0.2 fusion.62
  96.4 0.6 constant_dynamic-slice_fusion
  97.0 0.7 add_convert_fusion.1
  (58 shorter events, 1.2 us)
Async XLA Ops:
  0.6 69.6 %copy-start = (bf16[256,2048]{1,0:T(8,128)(2,1)S(1)}, bf16[256,2048]{1,0:T(8,128)(2,1)}, u32[]{:S(2)}) copy-start(bf16[256,2048]{1,0:T(8,128)(2,1)} %param.22) | copy-start | bytes 3145732
  0.6 17.6 %copy-start.4 = (bf16[16,256]{1,0:T(8,128)(2,1)S(1)}, bf16[16,256]{1,0:T(8,128)(2,1)}, u32[]{:S(2)}) copy-start(bf16[16,256]{1,0:T(8,128)(2,1)} %param.13) | copy-start | bytes 24580
  0.7 16.5 %copy-start.6 = (s32[32]{0:T(128)S(1)}, s32[32]{0:T(128)}, u32[]{:S(2)}) copy-start(s32[32]{0:T(128)} %param.18) | copy-start | bytes 388
  0.7 16.6 %copy-start.1 = (s32[64]{0:T(128)S(1)}, s32[64]{0:T(128)}, u32[]{:S(2)}) copy-start(s32[64]{0:T(128)} %param.20) | copy-start | bytes 772
  0.7 17.3 %copy-start.8 = (s32[32]{0:T(128)S(1)}, s32[32]{0:T(128)}, u32[]{:S(2)}) copy-start(s32[32]{0:T(128)} %param.19) | copy-start | bytes 388
  0.7 17.4 %copy-start.5 = (bf16[16,2,256]{2,1,0:T(2,128)(2,1)S(1)}, bf16[16,2,256]{2,1,0:T(2,128)(2,1)}, u32[]{:S(2)}) copy-start(bf16[16,2,256]{2,1,0:T(2,128)(2,1)} %param.14) | copy-start | bytes 49156
  2.3 32.6 %all-to-all-start = ((bf16[64,16,256]{2,1,0:T(8,128)(2,1)}), bf16[64,16,256]{2,1,0:T(8,128)(2,1)S(1)}, u32[]{:S(2)}, u32[]{:S(2)}) async-start(bf16[64,16,256]{2,1,0:T(8,128)(2,1)} %broadcast_in_dim.67), calls=%async_computation | async-start | bytes 1048576 | tf_op jit(solution)/shard_map/all_to_all | solution.py:52
  40.7 7.1 %copy-start.9 = (s32[16]{0:T(128)S(1)}, s32[16]{0:T(128)}, u32[]{:S(2)}) copy-start(s32[16]{0:T(128)} %param.16) | copy-start | bytes 196
  40.7 7.2 %copy-start.2 = (bf16[16,32,2,256]{3,2,1,0:T(2,128)(2,1)S(1)}, bf16[16,32,2,256]{3,2,1,0:T(2,128)(2,1)}, u32[]{:S(2)}) copy-start(bf16[16,32,2,256]{3,2,1,0:T(2,128)(2,1)} %param.15) | copy-start | bytes 1572868
  41.9 26.1 %all-to-all-start.1 = ((bf16[64,40,128]{2,1,0:T(8,128)(2,1)}), bf16[64,40,128]{2,1,0:T(8,128)(2,1)S(1)}, u32[]{:S(2)}, u32[]{:S(2)}) async-start(bf16[64,40,128]{2,1,0:T(8,128)(2,1)} %maximum_maximum_fusion), calls=%async_computation.1 | async-start | bytes 1310720 | tf_op jit(solution)/shard_map/all_to_all | solution.py:116
  70.2 8.0 %copy-start.7 = (bf16[2048]{0:T(1024)(128)(2,1)S(1)}, bf16[2048]{0:T(1024)(128)(2,1)}, u32[]{:S(2)}) copy-start(bf16[2048]{0:T(1024)(128)(2,1)} %param.23) | copy-start | bytes 12292
  70.2 8.0 %copy-start.10 = (bf16[256]{0:T(256)(128)(2,1)S(1)}, bf16[256]{0:T(256)(128)(2,1)}, u32[]{:S(2)}) copy-start(bf16[256]{0:T(256)(128)(2,1)} %param.24) | copy-start | bytes 1540
  70.2 8.0 %copy-start.11 = (bf16[256]{0:T(256)(128)(2,1)S(1)}, bf16[256]{0:T(256)(128)(2,1)}, u32[]{:S(2)}) copy-start(bf16[256]{0:T(256)(128)(2,1)} %param.25) | copy-start | bytes 1540
  70.2 26.0 %copy-start.3 = (bf16[16,2048]{1,0:T(8,128)(2,1)S(1)}, bf16[16,2048]{1,0:T(8,128)(2,1)}, u32[]{:S(2)}) copy-start(bf16[16,2048]{1,0:T(8,128)(2,1)} %param.21) | copy-start | bytes 196612
  71.4 24.8 %all-to-all-start.2 = ((bf16[8,16,2048]{2,1,0:T(8,128)(2,1)}), bf16[8,16,2048]{2,1,0:T(8,128)(2,1)S(1)}, u32[]{:S(2)}, u32[]{:S(2)}) async-start(bf16[8,16,2048]{2,1,0:T(8,128)(2,1)} %convolution_convert_fusion), calls=%async_computation.2 | async-start | bytes 1048576 | tf_op jit(solution)/shard_map/all_to_all | solution.py:168
